TPU v7x, 128 devices: a whole 4x4x4 slice. The times are simulated.
128 devices in a mesh: gx: 16 (over y_hi, z, core), gy: 8 (over x, y_lo).
Axes of the slice: x: 4, y: 4 (y_hi: 2, y_lo: 2; y = y_hi * 2 + y_lo), z: 4, core: 2. Of those that a mesh axis runs over, the one named last changes fastest.
Arguments:
- payload: float32 [4, 2097152], P(None, ('gx', 'gy'))
- cells: int32 [3, 2097152], P(None, ('gx', 'gy')), may hold values from 0 to 127, as said below
- counts: int32 [128, 9], P(('gx', 'gy')), may hold values from 128 to 12596, as said below
Outputs:
- scalar_field: float32 [8, 256, 1024], P(None, 'gx', 'gy')
- momentum: float32 [3, 8, 256, 1024], P(None, None, 'gx', 'gy')
Inputs may be any that keep to these rules, and one draw needn't show every extreme that they name: Rows of a tile are grouped by direction in the order of counts' columns. A face direction holds at most 2048 rows of a tile and a corner direction at most 512; each of these bounds is reached in some tile. A row of counts sums to 16384. cells[0] is below 8, cells[1] below 16, cells[2] below 128. A particle moving +x lands in x layers 0 to 1 of its destination tile, one moving -x in layers 14 to 15; likewise +y in y layers 0 to 15 and -y in 112 to 127; corner directions are bound in both; otherwise any cell.
All inputs are finite; a program needn't handle non-finite values.
Results may differ from a plain program's by a relative error of at most 0.000054.
Values sent between devices are 32-bit elements; how exact they have to be, the bound alone decides.
No kernel may reach another device: no remote copies, remote signals or barrier semaphores. Data moves between devices by JAX's collectives and lax.ppermute only.
A program may use at most 64 MiB of HBM per device.

v0:
```python
import jax
import jax.numpy as jnp
from jax import lax
from jax.experimental import pallas as pl
from jax.experimental.pallas import tpu as pltpu
from jax.sharding import PartitionSpec as P

CX = 16
CY = 128
NZ = 8
SWEEPS = 4
CAP_F = 2048
CAP_D = 512


SCREENING = 0.5
CUBIC_TERM = 0.3
COUPLING = 1.5
SMOOTHING = 0.1
BACKGROUND = 1.0

HALO = 2 * SWEEPS
ROWS = 64
COLS = 256
SPLITS = 2
BLOCK = 2048
LANE = 128
WIDE_X = 2 * CX
WIDE_Y = 2 * CY


def local_start(count_ref):
    total = count_ref[0, 0]
    for edge in range(1, 8):
        total = total + count_ref[0, edge]
    return total


def accumulate(first, block, step, p, c, acc_ref):
    width = p.shape[1]
    masses = p[0:1]
    vals = jnp.concatenate([masses, masses * p[1:4]], axis=0)
    cell = (c[0:1] * CX + c[1:2]) * CY + c[2:3]
    position = step * block + lax.broadcasted_iota(jnp.int32, (1, width), 1)
    cell = jnp.where(position >= first, cell, -1)
    row = lax.shift_right_arithmetic(cell, 8)
    col = lax.bitwise_and(cell, COLS - 1)
    hi = vals.astype(jnp.bfloat16)
    lo = (vals - hi.astype(jnp.float32)).astype(jnp.bfloat16)
    parts = [q.astype(jnp.float32)[e : e + 1] for q in (hi, lo) for e in range(4)]
    row_hot = (lax.broadcasted_iota(jnp.int32, (ROWS, width), 0) == row).astype(jnp.float32)
    left = jnp.concatenate([(row_hot * part).astype(jnp.bfloat16) for part in parts], axis=0)
    right = (lax.broadcasted_iota(jnp.int32, (COLS, width), 0) == col).astype(jnp.bfloat16)
    acc_ref[...] += lax.dot_general(
        left, right, (((1,), (1,)), ((), ())), preferred_element_type=jnp.float32
    )


def local_kernel(count_ref, p_ref, c_ref, o_ref):
    step = pl.program_id(0)
    first = local_start(count_ref)

    @pl.when(step == 0)
    def _():
        o_ref[...] = jnp.zeros(o_ref.shape, o_ref.dtype)

    @pl.when(step * BLOCK + BLOCK > first)
    def _():
        accumulate(first, BLOCK, step, p_ref[...], c_ref[...], o_ref)


def arrived_kernel(block, x_ref, y_ref, a_ref, o_ref):
    o_ref[...] = a_ref[...]
    for source in (x_ref, y_ref):
        x = source[...]
        accumulate(0, block, 0, x[0:4], x[4:7].astype(jnp.int32), o_ref)


ACC_SHAPE = (4 * SPLITS * ROWS, COLS)


def deposit_local(payload, cells, counts):
    pick = lambda b, f: (0, jnp.maximum(b, local_start(f) // BLOCK))
    return pl.pallas_call(
        local_kernel,
        grid_spec=pltpu.PrefetchScalarGridSpec(
            num_scalar_prefetch=1,
            grid=(payload.shape[1] // BLOCK,),
            in_specs=[pl.BlockSpec((4, BLOCK), pick), pl.BlockSpec((3, BLOCK), pick)],
            out_specs=pl.BlockSpec(ACC_SHAPE, lambda b, f: (0, 0)),
        ),
        out_shape=jax.ShapeDtypeStruct(ACC_SHAPE, jnp.float32),
        compiler_params=pltpu.CompilerParams(dimension_semantics=("arbitrary",)),
    )(counts, payload, cells)


def deposit_arrived(first, second, acc, block):
    return pl.pallas_call(
        lambda x, y, a, o: arrived_kernel(block, x, y, a, o),
        grid=(1,),
        in_specs=[
            pl.BlockSpec((7, block), lambda b: (0, 0)),
            pl.BlockSpec((7, block), lambda b: (0, 0)),
            pl.BlockSpec(ACC_SHAPE, lambda b: (0, 0)),
        ],
        out_specs=pl.BlockSpec(ACC_SHAPE, lambda b: (0, 0)),
        out_shape=jax.ShapeDtypeStruct(ACC_SHAPE, jnp.float32),
        input_output_aliases={2: 0},
    )(first, second, acc)


def pack_kernel(count_ref, p_ref, c_ref, plus_x, minus_x, plus_y, minus_y):
    face = CAP_F + LANE
    corner = CAP_D + LANE
    places = (
        (plus_x, 0), (minus_x, 0), (plus_y, 0), (minus_y, 0),
        (plus_x, face), (plus_x, face + corner), (minus_x, face), (minus_x, face + corner),
    )
    start = 0
    for which, (out_ref, column) in enumerate(places):
        tally = count_ref[0, which]
        width = face if which < 4 else corner
        base = pl.multiple_of((start // LANE) * LANE, LANE)
        offset = start - base
        p = p_ref[:, pl.ds(base, width)]
        c = c_ref[:, pl.ds(base, width)]
        lane = lax.broadcasted_iota(jnp.int32, (1, width), 1)
        living = (lane >= offset) & (lane < offset + tally)
        out_ref[0:1, column : column + width] = jnp.where(living, p[0:1], 0.0)
        out_ref[1:4, column : column + width] = p[1:4]
        out_ref[4:7, column : column + width] = c.astype(jnp.float32)
        start = start + tally


def pack(payload, cells, counts):
    face = CAP_F + LANE
    corner = CAP_D + LANE
    widths = (face + 2 * corner, face + 2 * corner, face, face)
    return pl.pallas_call(
        pack_kernel,
        in_specs=[
            pl.BlockSpec(memory_space=pltpu.SMEM),
            pl.BlockSpec(memory_space=pltpu.VMEM),
            pl.BlockSpec(memory_space=pltpu.VMEM),
        ],
        out_shape=[jax.ShapeDtypeStruct((7, w), jnp.float32) for w in widths],
    )(counts, payload, cells)


def towards(block, sx, sy):
    gx = lax.axis_size("gx")
    gy = lax.axis_size("gy")
    route = []
    for ix in range(gx):
        for iy in range(gy):
            route.append((ix * gy + iy, ((ix + sx) % gx) * gy + (iy + sy) % gy))
    return lax.ppermute(block, ("gx", "gy"), route)


def bordered_density(density):
    upper_x = towards(density[:, :HALO, :], -1, 0)
    lower_x = towards(density[:, CX - HALO :, :], 1, 0)
    wide = jnp.concatenate([density, upper_x, lower_x], axis=1)
    upper_y = towards(wide[:, :, :HALO], 0, -1)
    lower_y = towards(wide[:, :, CY - HALO :], 0, 1)
    gap = jnp.zeros((NZ, WIDE_X, WIDE_Y - CY - 2 * HALO), jnp.float32)
    return jnp.concatenate([wide, upper_y, gap, lower_y], axis=2)


def near(v):
    flat = jnp.zeros((1,) + v.shape[1:], v.dtype)
    up = jnp.concatenate([v[1:], flat], axis=0)
    down = jnp.concatenate([flat, v[:-1]], axis=0)
    return (
        up
        + down
        + pltpu.roll(v, WIDE_X - 1, 1)
        + pltpu.roll(v, 1, 1)
        + pltpu.roll(v, WIDE_Y - 1, 2)
        + pltpu.roll(v, 1, 2)
    )


def relax_kernel(d_ref, o_ref):
    density = d_ref[...]
    source = COUPLING * ((density + SMOOTHING * (near(density) - 6.0 * density)) - BACKGROUND)
    shape = density.shape
    parity = (
        lax.broadcasted_iota(jnp.int32, shape, 0)
        + lax.broadcasted_iota(jnp.int32, shape, 1)
        + lax.broadcasted_iota(jnp.int32, shape, 2)
    ) % 2
    field = jnp.zeros(shape, jnp.float32)
    for _ in range(SWEEPS):
        for colour in (0, 1):
            middle = field
            residual = (
                near(middle)
                - 6.0 * middle
                - SCREENING * middle
                - CUBIC_TERM * middle * middle * middle
                - source
            )
            slope = -6.0 - SCREENING - 3.0 * CUBIC_TERM * middle * middle
            field = jnp.where(parity == colour, middle - residual / slope, middle)
    o_ref[...] = field[:, :CX, :CY]


def relax(bordered):
    return pl.pallas_call(
        relax_kernel,
        out_shape=jax.ShapeDtypeStruct((NZ, CX, CY), jnp.float32),
    )(bordered)


def staged(payload, cells, counts):
    face = CAP_F + LANE
    corner = CAP_D + LANE
    plus_x, minus_x, plus_y, minus_y = pack(payload, cells, counts)
    from_minus_x = towards(plus_x, 1, 0)
    from_plus_x = towards(minus_x, -1, 0)
    total = deposit_local(payload, cells, counts)
    plus_y = jnp.concatenate(
        [plus_y, from_minus_x[:, face : face + corner], from_plus_x[:, face : face + corner]], axis=1
    )
    minus_y = jnp.concatenate(
        [minus_y, from_minus_x[:, face + corner :], from_plus_x[:, face + corner :]], axis=1
    )
    from_minus_y = towards(plus_y, 0, 1)
    from_plus_y = towards(minus_y, 0, -1)
    total = deposit_arrived(from_minus_x, from_plus_x, total, face)
    total = deposit_arrived(from_minus_y, from_plus_y, total, face + 2 * corner)
    total = total.reshape(SPLITS, 4, ROWS * COLS)
    interior = (total[0] + total[1]).reshape(4, NZ, CX, CY)
    density = interior[0]
    momentum = interior[1:]
    scalar_field = relax(bordered_density(density))
    return (scalar_field, momentum)


def solution(mesh):
    placed = (P(None, ("gx", "gy")), P(None, ("gx", "gy")), P(("gx", "gy"), None))
    return jax.shard_map(
        staged,
        mesh=mesh,
        in_specs=placed,
        out_specs=(P(None, "gx", "gy"), P(None, None, "gx", "gy")),
        check_vma=False,
    )
```

profile of v0, /device:TPU:0, one launch (start us, length us, event | category | flops | bytes accessed | tf_op | source)
XLA Modules:
  0.0 59.5 jit_solution(8793228088786666390)
XLA Ops:
  0.6 1.9 %shard_map.50 = (f32[7,3456]{1,0:T(8,128)}, f32[7,3456]{1,0:T(8,128)}, f32[7,2176]{1,0:T(8,128)}, f32[7,2176]{1,0:T(8,128)}) custom-call(s32[1,9]{1,0:T(1,128)} %count_ref.3, f32[4,16384]{1,0:T(4,128)} %p_ref.3, s32[3,16384]{1,0:T(4,128)} %c_ref.3), custom_call_target="tpu_custom_call" | custom-call | tf_op jit(solution)/shard_map/pallas_call | solution.py:139
  2.5 6.3 %collective-permute-start.1 = (f32[7,3456]{1,0:T(8,128)}, f32[7,3456]{1,0:T(8,128)S(1)}, u32[]{:S(2)}, u32[]{:S(2)}) collective-permute-start(f32[7,3456]{1,0:T(8,128)} %get-tuple-element.8), channel_id=1, source_target_pairs={{0,120},{1,121},{2,122},{3,123},{4,124},{5,125},{6,126},{7,127},{8... | collective-permute-start | bytes 290312 | tf_op jit(solution)/shard_map/ppermute | solution.py:157
  8.8 2.6 %collective-permute-done.x = f32[7,3456]{1,0:T(8,128)S(1)} collective-permute-done((f32[7,3456]{1,0:T(8,128)}, f32[7,3456]{1,0:T(8,128)S(1)}, u32[]{:S(2)}, u32[]{:S(2)}) %collective-permute-start) | collective-permute-done | bytes 96800 | tf_op jit(solution)/shard_map/ppermute | solution.py:157
  11.5 0.5 copy-done
  12.0 0.1 copy-done.1
  12.1 3.0 %collective-permute-start.3 = (f32[7,3456]{1,0:T(8,128)S(1)}, f32[7,3456]{1,0:T(8,128)S(1)}, u32[]{:S(2)}, u32[]{:S(2)}) collective-permute-start(f32[7,3456]{1,0:T(8,128)S(1)} %pad_maximum_fusion.2), channel_id=1, source_target_pairs={{0,7},{1,0},{2,1},{3,2},{4,3},{5,4},{6,5},{7,6},{8,15},{9,8},{10,9... | collective-permute-start | bytes 290312 | tf_op jit(solution)/shard_map/ppermute | solution.py:157
  15.1 0.1 collective-permute-start.2
  15.1 7.2 %shard_map.51.a = f32[512,256]{1,0:T(8,128)} custom-call(s32[1,9]{1,0:T(1,128)} %count_ref.3, f32[4,16384]{1,0:T(4,128)} %p_ref.3, s32[3,16384]{1,0:T(4,128)} %c_ref.3), custom_call_target="tpu_custom_call" | custom-call | tf_op jit(solution)/shard_map/pallas_call | solution.py:84
  22.3 3.3 %shard_map.52.a = f32[512,256]{1,0:T(8,128)} custom-call(f32[7,3456]{1,0:T(8,128)} %copy-done, f32[7,3456]{1,0:T(8,128)} %copy-done.1, f32[512,256]{1,0:T(8,128)} %shard_map.51.a), custom_call_target="tpu_custom_call", output_to_operand_aliasing={{}: (2, {})} | custom-call | tf_op jit(solution)/shard_map/pallas_call | solution.py:98
  25.6 0.6 %copy-done.2 = f32[7,3456]{1,0:T(8,128)} copy-done((f32[7,3456]{1,0:T(8,128)}, f32[7,3456]{1,0:T(8,128)S(1)}, u32[]{:S(2)}) %copy-start.2) | copy-done | bytes 96792
  26.3 0.6 %copy-done.3 = f32[7,3456]{1,0:T(8,128)} copy-done((f32[7,3456]{1,0:T(8,128)}, f32[7,3456]{1,0:T(8,128)S(1)}, u32[]{:S(2)}) %copy-start.3) | copy-done | bytes 96792
  26.9 4.0 %shard_map.53 = f32[512,256]{1,0:T(8,128)} custom-call(f32[7,3456]{1,0:T(8,128)} %copy-done.3, f32[7,3456]{1,0:T(8,128)} %copy-done.2, f32[512,256]{1,0:T(8,128)} %shard_map.52.a), custom_call_target="tpu_custom_call", output_to_operand_aliasing={{}: (2, {})} | custom-call | tf_op jit(solution)/shard_map/pallas_call | solution.py:98
  31.0 1.1 %slice_add_fusion = f32[256,256]{1,0:T(8,128)S(1)} fusion(f32[512,256]{1,0:T(8,128)} %shard_map.53), kind=kLoop, calls=%fused_computation | loop fusion | flops 65536 | bytes 786432 | tf_op jit(solution)/shard_map/add | solution.py:234
  32.1 5.0 %collective-permute-start.4 = (f32[8,8,128]{2,1,0:T(8,128)S(1)}, f32[8,8,128]{2,1,0:T(8,128)S(1)}, u32[]{:S(2)}, u32[]{:S(2)}) collective-permute-start(f32[8,8,128]{2,1,0:T(8,128)S(1)} %get-tuple-element.17), channel_id=1, source_target_pairs={{0,120},{1,121},{2,122},{3,123},{4,124},{5,125},{6,126},{7,127},{8... | collective-permute-start | bytes 98312 | tf_op jit(solution)/shard_map/ppermute | solution.py:157
  37.1 1.6 %collective-permute-done.4 = f32[8,8,128]{2,1,0:T(8,128)S(1)} collective-permute-done((f32[8,8,128]{2,1,0:T(8,128)S(1)}, f32[8,8,128]{2,1,0:T(8,128)S(1)}, u32[]{:S(2)}, u32[]{:S(2)}) %collective-permute-start.4) | collective-permute-done | bytes 32800 | tf_op jit(solution)/shard_map/ppermute | solution.py:157
  38.7 5.4 %collective-permute-done.5 = f32[8,8,128]{2,1,0:T(8,128)S(1)} collective-permute-done((f32[8,8,128]{2,1,0:T(8,128)S(1)}, f32[8,8,128]{2,1,0:T(8,128)S(1)}, u32[]{:S(2)}, u32[]{:S(2)}) %collective-permute-start.5) | collective-permute-done | bytes 32800 | tf_op jit(solution)/shard_map/ppermute | solution.py:157
  44.2 0.1 fusion
  44.3 3.8 %collective-permute-start.6 = (f32[8,32,8]{2,1,0:T(8,128)S(1)}, f32[8,32,8]{2,1,0:T(8,128)S(1)}, u32[]{:S(2)}, u32[]{:S(2)}) collective-permute-start(f32[8,32,8]{2,1,0:T(8,128)S(1)} %get-tuple-element.10), channel_id=1, source_target_pairs={{0,7},{1,0},{2,1},{3,2},{4,3},{5,4},{6,5},{7,6},{8,15},{9,8},{10,9... | collective-permute-start | bytes 24584 | tf_op jit(solution)/shard_map/ppermute | solution.py:157
  48.1 0.1 pad.2.clone
  48.2 0.7 %slice.56 = f32[3,8,16,128]{3,2,1,0:T(8,128)} reshape(f32[192,256]{1,0:T(8,128)S(1)} %slice.68) | data formatting | bytes 393216 | tf_op jit(solution)/shard_map/slice | solution.py:236
  48.9 1.7 %collective-permute-done.6 = f32[8,32,8]{2,1,0:T(8,128)S(1)} collective-permute-done((f32[8,32,8]{2,1,0:T(8,128)S(1)}, f32[8,32,8]{2,1,0:T(8,128)S(1)}, u32[]{:S(2)}, u32[]{:S(2)}) %collective-permute-start.6) | collective-permute-done | bytes 8224 | tf_op jit(solution)/shard_map/ppermute | solution.py:157
  50.6 4.6 %collective-permute-done.7 = f32[8,32,8]{2,1,0:T(8,128)S(1)} collective-permute-done((f32[8,32,8]{2,1,0:T(8,128)S(1)}, f32[8,32,8]{2,1,0:T(8,128)S(1)}, u32[]{:S(2)}, u32[]{:S(2)}) %collective-permute-start.7) | collective-permute-done | bytes 8224 | tf_op jit(solution)/shard_map/ppermute | solution.py:157
  55.2 0.8 %pad_maximum_fusion.d_ref = f32[8,32,256]{2,1,0:T(8,128)} fusion(f32[8,32,8]{2,1,0:T(8,128)S(1)} %collective-permute-done.7, f32[8,32,8]{2,1,0:T(8,128)S(1)} %collective-permute-done.6, f32[8,32,128]{2,1,0:T(8,128)S(1)} %constant_dynamic-update-slice_fusion, f32[256]{0:T(256)S(1)} %pad.2.clone), kind=kLoop, calls=%fused_computation.1 | loop fusion | flops 196608 | bytes 410624 | tf_op jit(solution)/shard_map/concatenate | solution.py:167
  56.0 3.6 %shard_map.54 = f32[8,16,128]{2,1,0:T(8,128)} custom-call(f32[8,32,256]{2,1,0:T(8,128)} %pad_maximum_fusion.d_ref), custom_call_target="tpu_custom_call" | custom-call | tf_op jit(solution)/shard_map/pallas_call | solution.py:210
  (26 shorter events, 0.2 us)
Async XLA Ops:
  2.5 8.9 %collective-permute-start = (f32[7,3456]{1,0:T(8,128)}, f32[7,3456]{1,0:T(8,128)S(1)}, u32[]{:S(2)}, u32[]{:S(2)}) collective-permute-start(f32[7,3456]{1,0:T(8,128)} %get-tuple-element.7), channel_id=1, source_target_pairs={{0,8},{1,9},{2,10},{3,11},{4,12},{5,13},{6,14},{7,15},{8,16},{9,17... | collective-permute-start | bytes 290312 | tf_op jit(solution)/shard_map/ppermute | solution.py:157
  2.5 8.9 %copy-start.5 = (f32[7,2176]{1,0:T(8,128)S(1)}, f32[7,2176]{1,0:T(8,128)}, u32[]{:S(2)}) copy-start(f32[7,2176]{1,0:T(8,128)} %get-tuple-element.9) | copy-start | bytes 182788
  2.5 8.9 %collective-permute-start.1 = (f32[7,3456]{1,0:T(8,128)}, f32[7,3456]{1,0:T(8,128)S(1)}, u32[]{:S(2)}, u32[]{:S(2)}) collective-permute-start(f32[7,3456]{1,0:T(8,128)} %get-tuple-element.8), channel_id=1, source_target_pairs={{0,120},{1,121},{2,122},{3,123},{4,124},{5,125},{6,126},{7,127},{8... | collective-permute-start | bytes 290312 | tf_op jit(solution)/shard_map/ppermute | solution.py:157
  11.3 0.6 %copy-start = (f32[7,3456]{1,0:T(8,128)}, f32[7,3456]{1,0:T(8,128)S(1)}, u32[]{:S(2)}) copy-start(f32[7,3456]{1,0:T(8,128)S(1)} %collective-permute-done.x) | copy-start | bytes 290308
  11.4 0.6 %copy-start.1 = (f32[7,3456]{1,0:T(8,128)}, f32[7,3456]{1,0:T(8,128)S(1)}, u32[]{:S(2)}) copy-start(f32[7,3456]{1,0:T(8,128)S(1)} %collective-permute-done.1.y) | copy-start | bytes 290308
  11.4 3.6 %copy-start.4 = (f32[7,2176]{1,0:T(8,128)S(1)}, f32[7,2176]{1,0:T(8,128)}, u32[]{:S(2)}) copy-start(f32[7,2176]{1,0:T(8,128)} %get-tuple-element.6) | copy-start | bytes 182788
  12.1 13.6 %collective-permute-start.3 = (f32[7,3456]{1,0:T(8,128)S(1)}, f32[7,3456]{1,0:T(8,128)S(1)}, u32[]{:S(2)}, u32[]{:S(2)}) collective-permute-start(f32[7,3456]{1,0:T(8,128)S(1)} %pad_maximum_fusion.2), channel_id=1, source_target_pairs={{0,7},{1,0},{2,1},{3,2},{4,3},{5,4},{6,5},{7,6},{8,15},{9,8},{10,9... | collective-permute-start | bytes 290312 | tf_op jit(solution)/shard_map/ppermute | solution.py:157
  15.1 10.6 %collective-permute-start.2 = (f32[7,3456]{1,0:T(8,128)S(1)}, f32[7,3456]{1,0:T(8,128)S(1)}, u32[]{:S(2)}, u32[]{:S(2)}) collective-permute-start(f32[7,3456]{1,0:T(8,128)S(1)} %pad_maximum_fusion.1), channel_id=1, source_target_pairs={{0,1},{1,2},{2,3},{3,4},{4,5},{5,6},{6,7},{7,0},{8,9},{9,10},{10,1... | collective-permute-start | bytes 290312 | tf_op jit(solution)/shard_map/ppermute | solution.py:157
  25.6 0.6 %copy-start.2 = (f32[7,3456]{1,0:T(8,128)}, f32[7,3456]{1,0:T(8,128)S(1)}, u32[]{:S(2)}) copy-start(f32[7,3456]{1,0:T(8,128)S(1)} %collective-permute-done.3.y) | copy-start | bytes 290308
  26.3 0.6 %copy-start.3 = (f32[7,3456]{1,0:T(8,128)}, f32[7,3456]{1,0:T(8,128)S(1)}, u32[]{:S(2)}) copy-start(f32[7,3456]{1,0:T(8,128)S(1)} %collective-permute-done.2.x) | copy-start | bytes 290308
  32.1 6.6 %collective-permute-start.4 = (f32[8,8,128]{2,1,0:T(8,128)S(1)}, f32[8,8,128]{2,1,0:T(8,128)S(1)}, u32[]{:S(2)}, u32[]{:S(2)}) collective-permute-start(f32[8,8,128]{2,1,0:T(8,128)S(1)} %get-tuple-element.17), channel_id=1, source_target_pairs={{0,120},{1,121},{2,122},{3,123},{4,124},{5,125},{6,126},{7,127},{8... | collective-permute-start | bytes 98312 | tf_op jit(solution)/shard_map/ppermute | solution.py:157
  37.1 7.0 %collective-permute-start.5 = (f32[8,8,128]{2,1,0:T(8,128)S(1)}, f32[8,8,128]{2,1,0:T(8,128)S(1)}, u32[]{:S(2)}, u32[]{:S(2)}) collective-permute-start(f32[8,8,128]{2,1,0:T(8,128)S(1)} %get-tuple-element.16), channel_id=1, source_target_pairs={{0,8},{1,9},{2,10},{3,11},{4,12},{5,13},{6,14},{7,15},{8,16},{9,17... | collective-permute-start | bytes 98312 | tf_op jit(solution)/shard_map/ppermute | solution.py:157
  44.3 6.4 %collective-permute-start.6 = (f32[8,32,8]{2,1,0:T(8,128)S(1)}, f32[8,32,8]{2,1,0:T(8,128)S(1)}, u32[]{:S(2)}, u32[]{:S(2)}) collective-permute-start(f32[8,32,8]{2,1,0:T(8,128)S(1)} %get-tuple-element.10), channel_id=1, source_target_pairs={{0,7},{1,0},{2,1},{3,2},{4,3},{5,4},{6,5},{7,6},{8,15},{9,8},{10,9... | collective-permute-start | bytes 24584 | tf_op jit(solution)/shard_map/ppermute | solution.py:157
  48.1 7.1 %collective-permute-start.7 = (f32[8,32,8]{2,1,0:T(8,128)S(1)}, f32[8,32,8]{2,1,0:T(8,128)S(1)}, u32[]{:S(2)}, u32[]{:S(2)}) collective-permute-start(f32[8,32,8]{2,1,0:T(8,128)S(1)} %get-tuple-element.11), channel_id=1, source_target_pairs={{0,1},{1,2},{2,3},{3,4},{4,5},{5,6},{6,7},{7,0},{8,9},{9,10},{10,1... | collective-permute-start | bytes 24584 | tf_op jit(solution)/shard_map/ppermute | solution.py:157
where the time goes:
time: 60.1 us; the launch traced here: 59.5 us
  Pallas kernels  19.9 us (33%)
  starting transfers between devices  18.2 us (30%)
  waiting for transfers between devices  15.9 us (26%)
  local copies, waits for them, and re-layouts  2.81 us (5%)
  other arithmetic  1.9 us (3%)
  between operations  0.73 us (1%)
    ppermute x8, starting transfers between devices, towards(): return lax.ppermute(block, ('gx', 'gy'), route)  18.2 us
    ppermute x8, waiting for transfers between devices, towards(): return lax.ppermute(block, ('gx', 'gy'), route)  15.9 us
    pallas_call x2, Pallas kernels, deposit_arrived(): pl.pallas_call(lambda x, y, a, o: arrived_kernel(block, x, y, a, o), grid...  7.38 us
    pallas_call x1, Pallas kernels, deposit_local(): pl.pallas_call(local_kernel, grid_spec=pltpu.PrefetchScalarGridSpec(num_s...  7.15 us
    pallas_call x1, Pallas kernels, relax(): pl.pallas_call(relax_kernel, out_shape=jax.ShapeDtypeStruct((NZ, CX, CY),...  3.56 us
    unnamed x14, local copies, waits for them, and re-layouts  1.91 us
    pallas_call x1, Pallas kernels, pack(): pl.pallas_call(pack_kernel, in_specs=[pl.BlockSpec(memory_space=pltpu.SME...  1.85 us
  transfers between devices with their start and end apart: 8, of which 6 were waited for; matrix products, arithmetic and copies ran while one was open for 1% of the time, Pallas kernels for 18%

commit v1 on v0

--- a/solution.py
+++ b/solution.py
@@ -163,8 +163,7 @@
     wide = jnp.concatenate([density, upper_x, lower_x], axis=1)
     upper_y = towards(wide[:, :, :HALO], 0, -1)
     lower_y = towards(wide[:, :, CY - HALO :], 0, 1)
-    gap = jnp.zeros((NZ, WIDE_X, WIDE_Y - CY - 2 * HALO), jnp.float32)
-    return jnp.concatenate([wide, upper_y, gap, lower_y], axis=2)
+    return (density, upper_x, lower_x, upper_y, lower_y)
 
 
 def near(v):
@@ -181,8 +180,14 @@
     )
 
 
-def relax_kernel(d_ref, o_ref):
-    density = d_ref[...]
+def relax_kernel(d_ref, ux_ref, lx_ref, uy_ref, ly_ref, o_ref, b_ref):
+    b_ref[...] = jnp.zeros(b_ref.shape, jnp.float32)
+    b_ref[:, 0:CX, 0:CY] = d_ref[...]
+    b_ref[:, CX : CX + HALO, 0:CY] = ux_ref[...]
+    b_ref[:, CX + HALO :, 0:CY] = lx_ref[...]
+    b_ref[:, :, CY : CY + HALO] = uy_ref[...]
+    b_ref[:, :, WIDE_Y - HALO :] = ly_ref[...]
+    density = b_ref[...]
     source = COUPLING * ((density + SMOOTHING * (near(density) - 6.0 * density)) - BACKGROUND)
     shape = density.shape
     parity = (
@@ -206,11 +211,12 @@
     o_ref[...] = field[:, :CX, :CY]
 
 
-def relax(bordered):
+def relax(pieces):
     return pl.pallas_call(
         relax_kernel,
         out_shape=jax.ShapeDtypeStruct((NZ, CX, CY), jnp.float32),
-    )(bordered)
+        scratch_shapes=[pltpu.VMEM((NZ, WIDE_X, WIDE_Y), jnp.float32)],
+    )(*pieces)
 
 
 def staged(payload, cells, counts):
@@ -231,10 +237,9 @@
     total = deposit_arrived(from_minus_x, from_plus_x, total, face)
     total = deposit_arrived(from_minus_y, from_plus_y, total, face + 2 * corner)
     total = total.reshape(SPLITS, 4, ROWS * COLS)
-    interior = (total[0] + total[1]).reshape(4, NZ, CX, CY)
-    density = interior[0]
-    momentum = interior[1:]
+    density = (total[0, 0] + total[1, 0]).reshape(NZ, CX, CY)
     scalar_field = relax(bordered_density(density))
+    momentum = (total[0, 1:] + total[1, 1:]).reshape(3, NZ, CX, CY)
     return (scalar_field, momentum)
 
 

time: 60.1 us -> 53.9 us (0.90)
  waiting for transfers between devices: 15.9 us -> 6.37 us
  local copies, waits for them, and re-layouts: 2.81 us -> 5.88 us
  starting transfers between devices: 18.2 us -> 20.1 us
  other arithmetic: 1.9 us -> 0.23 us
    ppermute x8, waiting for transfers between devices: 15.9 us -> 6.37 us  [towards(): return lax.ppermute(block, ('gx', 'gy'), route)]
    unnamed x14 -> x23, local copies, waits for them, and re-layouts: 1.91 us -> 4.48 us
    ppermute x8, starting transfers between devices: 18.2 us -> 20.1 us  [towards(): return lax.ppermute(block, ('gx', 'gy'), route)]
    reshape x0 -> x1, local copies, waits for them, and re-layouts: none -> 1.3 us  [staged(): total = total.reshape(SPLITS, 4, ROWS * COLS)]
    add x1, other arithmetic: 1.06 us -> 0.07 us  [staged(): density = (total[0, 0] + total[1, 0]).reshape(NZ, CX, CY)]
    concatenate x1, other arithmetic: 0.81 us -> 0.01 us  [bordered_density(): wide = jnp.concatenate([density, upper_x, lower_x], axis=1)]
    slice x4 -> x1, local copies, waits for them, and re-layouts: 0.8 us -> 0.09 us  [bordered_density(): lower_y = towards(wide[:, :, CY - HALO:], 0, 1)]
  transfers between devices with their start and end apart: 8 -> 8, of which waited for: 6 -> 4; matrix products, arithmetic and copies ran while one was open for 1% -> 2% of each run, Pallas kernels for 18% -> 20%
where the time goes in v1:
time: 53.9 us; the launch traced here: 53.4 us
  Pallas kernels  20.1 us (37%)
  starting transfers between devices  20.1 us (37%)
  waiting for transfers between devices  6.37 us (12%)
  local copies, waits for them, and re-layouts  5.88 us (11%)
  between operations  0.75 us (1%)
    ppermute x8, starting transfers between devices, towards(): return lax.ppermute(block, ('gx', 'gy'), route)  20.1 us
    pallas_call x2, Pallas kernels, deposit_arrived(): pl.pallas_call(lambda x, y, a, o: arrived_kernel(block, x, y, a, o), grid...  7.37 us
    pallas_call x1, Pallas kernels, deposit_local(): pl.pallas_call(local_kernel, grid_spec=pltpu.PrefetchScalarGridSpec(num_s...  7.14 us
    ppermute x8, waiting for transfers between devices, towards(): return lax.ppermute(block, ('gx', 'gy'), route)  6.37 us
    unnamed x23, local copies, waits for them, and re-layouts  4.48 us
    pallas_call x1, Pallas kernels, relax(): pl.pallas_call(relax_kernel, out_shape=jax.ShapeDtypeStruct((NZ, CX, CY),...  3.69 us
    pallas_call x1, Pallas kernels, pack(): pl.pallas_call(pack_kernel, in_specs=[pl.BlockSpec(memory_space=pltpu.SME...  1.85 us
    reshape x1, local copies, waits for them, and re-layouts, staged(): total = total.reshape(SPLITS, 4, ROWS * COLS)  1.3 us
  transfers between devices with their start and end apart: 8, of which 4 were waited for; matrix products, arithmetic and copies ran while one was open for 2% of the time, Pallas kernels for 20%

profile of v1, /device:TPU:0, one launch (start us, length us, event | category | flops | bytes accessed | tf_op | source)
XLA Modules:
  0.0 53.4 jit_solution(13833836466596758075)
XLA Ops:
  0.6 1.9 %shard_map.50 = (f32[7,3456]{1,0:T(8,128)}, f32[7,3456]{1,0:T(8,128)}, f32[7,2176]{1,0:T(8,128)}, f32[7,2176]{1,0:T(8,128)}) custom-call(s32[1,9]{1,0:T(1,128)} %count_ref.3, f32[4,16384]{1,0:T(4,128)} %p_ref.3, s32[3,16384]{1,0:T(4,128)} %c_ref.3), custom_call_target="tpu_custom_call" | custom-call | tf_op jit(solution)/shard_map/pallas_call | solution.py:139
  2.5 6.3 %collective-permute-start.1 = (f32[7,3456]{1,0:T(8,128)}, f32[7,3456]{1,0:T(8,128)S(1)}, u32[]{:S(2)}, u32[]{:S(2)}) collective-permute-start(f32[7,3456]{1,0:T(8,128)} %get-tuple-element.8), channel_id=1, source_target_pairs={{0,120},{1,121},{2,122},{3,123},{4,124},{5,125},{6,126},{7,127},{8... | collective-permute-start | bytes 290312 | tf_op jit(solution)/shard_map/ppermute | solution.py:157
  8.8 2.6 %collective-permute-done.x = f32[7,3456]{1,0:T(8,128)S(1)} collective-permute-done((f32[7,3456]{1,0:T(8,128)}, f32[7,3456]{1,0:T(8,128)S(1)}, u32[]{:S(2)}, u32[]{:S(2)}) %collective-permute-start) | collective-permute-done | bytes 96800 | tf_op jit(solution)/shard_map/ppermute | solution.py:157
  11.5 0.5 copy-done.1
  12.0 0.1 copy-done.2
  12.1 0.8 %collective-permute-start.2 = (f32[7,3456]{1,0:T(8,128)S(1)}, f32[7,3456]{1,0:T(8,128)S(1)}, u32[]{:S(2)}, u32[]{:S(2)}) collective-permute-start(f32[7,3456]{1,0:T(8,128)S(1)} %pad_maximum_fusion.1), channel_id=1, source_target_pairs={{0,1},{1,2},{2,3},{3,4},{4,5},{5,6},{6,7},{7,0},{8,9},{9,10},{10,1... | collective-permute-start | bytes 290312 | tf_op jit(solution)/shard_map/ppermute | solution.py:157
  12.9 3.4 %collective-permute-start.3 = (f32[7,3456]{1,0:T(8,128)S(1)}, f32[7,3456]{1,0:T(8,128)S(1)}, u32[]{:S(2)}, u32[]{:S(2)}) collective-permute-start(f32[7,3456]{1,0:T(8,128)S(1)} %pad_maximum_fusion.2), channel_id=1, source_target_pairs={{0,7},{1,0},{2,1},{3,2},{4,3},{5,4},{6,5},{7,6},{8,15},{9,8},{10,9... | collective-permute-start | bytes 290312 | tf_op jit(solution)/shard_map/ppermute | solution.py:157
  16.3 7.1 %shard_map.51.a = f32[512,256]{1,0:T(8,128)} custom-call(s32[1,9]{1,0:T(1,128)} %count_ref.3, f32[4,16384]{1,0:T(4,128)} %p_ref.3, s32[3,16384]{1,0:T(4,128)} %c_ref.3), custom_call_target="tpu_custom_call" | custom-call | tf_op jit(solution)/shard_map/pallas_call | solution.py:84
  23.4 3.3 %shard_map.52.a = f32[512,256]{1,0:T(8,128)} custom-call(f32[7,3456]{1,0:T(8,128)} %copy-done.1, f32[7,3456]{1,0:T(8,128)} %copy-done.2, f32[512,256]{1,0:T(8,128)} %shard_map.51.a), custom_call_target="tpu_custom_call", output_to_operand_aliasing={{}: (2, {})} | custom-call | tf_op jit(solution)/shard_map/pallas_call | solution.py:98
  26.8 0.6 %copy-done.7 = f32[7,3456]{1,0:T(8,128)} copy-done((f32[7,3456]{1,0:T(8,128)}, f32[7,3456]{1,0:T(8,128)S(1)}, u32[]{:S(2)}) %copy-start.7) | copy-done | bytes 96792
  27.4 0.6 %copy-done.8 = f32[7,3456]{1,0:T(8,128)} copy-done((f32[7,3456]{1,0:T(8,128)}, f32[7,3456]{1,0:T(8,128)S(1)}, u32[]{:S(2)}) %copy-start.8) | copy-done | bytes 96792
  28.1 4.0 %shard_map.53 = f32[512,256]{1,0:T(8,128)} custom-call(f32[7,3456]{1,0:T(8,128)} %copy-done.7, f32[7,3456]{1,0:T(8,128)} %copy-done.8, f32[512,256]{1,0:T(8,128)} %shard_map.52.a), custom_call_target="tpu_custom_call", output_to_operand_aliasing={{}: (2, {})} | custom-call | tf_op jit(solution)/shard_map/pallas_call | solution.py:98
  32.1 1.3 %reshape.15 = f32[2,4,16384]{2,1,0:T(4,128)S(1)} reshape(f32[512,256]{1,0:T(8,128)} %shard_map.53) | data formatting | bytes 1048576 | tf_op jit(solution)/shard_map/reshape | solution.py:239
  33.6 5.3 %collective-permute-start.4 = (f32[8,8,128]{2,1,0:T(8,128)S(1)}, f32[8,8,128]{2,1,0:T(8,128)S(1)}, u32[]{:S(2)}, u32[]{:S(2)}) collective-permute-start(f32[8,8,128]{2,1,0:T(8,128)S(1)} %get-tuple-element.17), channel_id=1, source_target_pairs={{0,120},{1,121},{2,122},{3,123},{4,124},{5,125},{6,126},{7,127},{8... | collective-permute-start | bytes 98312 | tf_op jit(solution)/shard_map/ppermute | solution.py:157
  38.9 1.6 %collective-permute-done.5.lx_ref = f32[8,8,128]{2,1,0:T(8,128)S(1)} collective-permute-done((f32[8,8,128]{2,1,0:T(8,128)S(1)}, f32[8,8,128]{2,1,0:T(8,128)S(1)}, u32[]{:S(2)}, u32[]{:S(2)}) %collective-permute-start.5) | collective-permute-done | bytes 32800 | tf_op jit(solution)/shard_map/ppermute | solution.py:157
  40.6 0.6 %copy-done.5 = f32[8,8,128]{2,1,0:T(8,128)} copy-done((f32[8,8,128]{2,1,0:T(8,128)}, f32[8,8,128]{2,1,0:T(8,128)S(1)}, u32[]{:S(2)}) %copy-start.5) | copy-done | bytes 32792
  41.2 0.1 fusion.1
  41.3 4.1 %collective-permute-start.6 = (f32[8,32,8]{2,1,0:T(8,128)S(1)}, f32[8,32,8]{2,1,0:T(8,128)S(1)}, u32[]{:S(2)}, u32[]{:S(2)}) collective-permute-start(f32[8,32,8]{2,1,0:T(8,128)S(1)} %get-tuple-element.11), channel_id=1, source_target_pairs={{0,7},{1,0},{2,1},{3,2},{4,3},{5,4},{6,5},{7,6},{8,15},{9,8},{10,9... | collective-permute-start | bytes 24584 | tf_op jit(solution)/shard_map/ppermute | solution.py:157
  45.5 0.1 fusion
  45.6 0.7 %copy.7 = f32[1,3,128,128]{3,2,1,0:T(8,128)} copy(f32[1,3,128,128]{3,1,2,0:T(4,128)S(1)} %fusion) | data formatting | bytes 393216
  46.3 2.1 %collective-permute-done.7.ly_ref = f32[8,32,8]{2,1,0:T(8,128)S(1)} collective-permute-done((f32[8,32,8]{2,1,0:T(8,128)S(1)}, f32[8,32,8]{2,1,0:T(8,128)S(1)}, u32[]{:S(2)}, u32[]{:S(2)}) %collective-permute-start.7) | collective-permute-done | bytes 8224 | tf_op jit(solution)/shard_map/ppermute | solution.py:157
  48.4 0.6 %copy-done.3 = f32[8,32,8]{2,1,0:T(8,128)} copy-done((f32[8,32,8]{2,1,0:T(8,128)}, f32[8,32,8]{2,1,0:T(8,128)S(1)}, u32[]{:S(2)}) %copy-start.3) | copy-done | bytes 8216
  49.1 0.6 %copy-done.4 = f32[8,32,8]{2,1,0:T(8,128)} copy-done((f32[8,32,8]{2,1,0:T(8,128)}, f32[8,32,8]{2,1,0:T(8,128)S(1)}, u32[]{:S(2)}) %copy-start.4) | copy-done | bytes 8216
  49.7 3.7 %shard_map.54 = f32[8,16,128]{2,1,0:T(8,128)} custom-call(f32[8,16,128]{2,1,0:T(8,128)} %bitcast.8, f32[8,8,128]{2,1,0:T(8,128)} %copy-done.6, f32[8,8,128]{2,1,0:T(8,128)} %copy-done.5, f32[8,32,8]{2,1,0:T(8,128)} %copy-done.4, f32[8,32,8]{2,1,0:T(8,128)} %copy-done.3), custom_call_target="tpu_custom_call" | custom-call | tf_op jit(solution)/shard_map/pallas_call | solution.py:215
  (30 shorter events, 0.4 us)
Async XLA Ops:
  2.5 8.9 %collective-permute-start = (f32[7,3456]{1,0:T(8,128)}, f32[7,3456]{1,0:T(8,128)S(1)}, u32[]{:S(2)}, u32[]{:S(2)}) collective-permute-start(f32[7,3456]{1,0:T(8,128)} %get-tuple-element.7), channel_id=1, source_target_pairs={{0,8},{1,9},{2,10},{3,11},{4,12},{5,13},{6,14},{7,15},{8,16},{9,17... | collective-permute-start | bytes 290312 | tf_op jit(solution)/shard_map/ppermute | solution.py:157
  2.5 8.9 %copy-start.10 = (f32[7,2176]{1,0:T(8,128)S(1)}, f32[7,2176]{1,0:T(8,128)}, u32[]{:S(2)}) copy-start(f32[7,2176]{1,0:T(8,128)} %get-tuple-element.6) | copy-start | bytes 182788
  2.5 8.9 %collective-permute-start.1 = (f32[7,3456]{1,0:T(8,128)}, f32[7,3456]{1,0:T(8,128)S(1)}, u32[]{:S(2)}, u32[]{:S(2)}) collective-permute-start(f32[7,3456]{1,0:T(8,128)} %get-tuple-element.8), channel_id=1, source_target_pairs={{0,120},{1,121},{2,122},{3,123},{4,124},{5,125},{6,126},{7,127},{8... | collective-permute-start | bytes 290312 | tf_op jit(solution)/shard_map/ppermute | solution.py:157
  11.3 0.6 %copy-start.1 = (f32[7,3456]{1,0:T(8,128)}, f32[7,3456]{1,0:T(8,128)S(1)}, u32[]{:S(2)}) copy-start(f32[7,3456]{1,0:T(8,128)S(1)} %collective-permute-done.x) | copy-start | bytes 290308
  11.4 0.6 %copy-start.2 = (f32[7,3456]{1,0:T(8,128)}, f32[7,3456]{1,0:T(8,128)S(1)}, u32[]{:S(2)}) copy-start(f32[7,3456]{1,0:T(8,128)S(1)} %collective-permute-done.1.y) | copy-start | bytes 290308
  11.4 1.4 %copy-start.9 = (f32[7,2176]{1,0:T(8,128)S(1)}, f32[7,2176]{1,0:T(8,128)}, u32[]{:S(2)}) copy-start(f32[7,2176]{1,0:T(8,128)} %get-tuple-element.9) | copy-start | bytes 182788
  12.1 14.7 %collective-permute-start.2 = (f32[7,3456]{1,0:T(8,128)S(1)}, f32[7,3456]{1,0:T(8,128)S(1)}, u32[]{:S(2)}, u32[]{:S(2)}) collective-permute-start(f32[7,3456]{1,0:T(8,128)S(1)} %pad_maximum_fusion.1), channel_id=1, source_target_pairs={{0,1},{1,2},{2,3},{3,4},{4,5},{5,6},{6,7},{7,0},{8,9},{9,10},{10,1... | collective-permute-start | bytes 290312 | tf_op jit(solution)/shard_map/ppermute | solution.py:157
  12.9 13.9 %collective-permute-start.3 = (f32[7,3456]{1,0:T(8,128)S(1)}, f32[7,3456]{1,0:T(8,128)S(1)}, u32[]{:S(2)}, u32[]{:S(2)}) collective-permute-start(f32[7,3456]{1,0:T(8,128)S(1)} %pad_maximum_fusion.2), channel_id=1, source_target_pairs={{0,7},{1,0},{2,1},{3,2},{4,3},{5,4},{6,5},{7,6},{8,15},{9,8},{10,9... | collective-permute-start | bytes 290312 | tf_op jit(solution)/shard_map/ppermute | solution.py:157
  26.8 0.6 %copy-start.7 = (f32[7,3456]{1,0:T(8,128)}, f32[7,3456]{1,0:T(8,128)S(1)}, u32[]{:S(2)}) copy-start(f32[7,3456]{1,0:T(8,128)S(1)} %collective-permute-done.2.x) | copy-start | bytes 290308
  27.4 0.6 %copy-start.8 = (f32[7,3456]{1,0:T(8,128)}, f32[7,3456]{1,0:T(8,128)S(1)}, u32[]{:S(2)}) copy-start(f32[7,3456]{1,0:T(8,128)S(1)} %collective-permute-done.3.y) | copy-start | bytes 290308
  33.5 7.1 %copy-start = (f32[1,1,16384]{2,1,0:T(1,128)}, f32[1,1,16384]{2,1,0:T(1,128)S(1)}, u32[]{:S(2)}) copy-start(f32[1,1,16384]{2,1,0:T(1,128)S(1)} %slice_add_fusion.1) | copy-start | bytes 196612
  33.5 7.0 %collective-permute-start.5 = (f32[8,8,128]{2,1,0:T(8,128)S(1)}, f32[8,8,128]{2,1,0:T(8,128)S(1)}, u32[]{:S(2)}, u32[]{:S(2)}) collective-permute-start(f32[8,8,128]{2,1,0:T(8,128)S(1)} %get-tuple-element.16), channel_id=1, source_target_pairs={{0,8},{1,9},{2,10},{3,11},{4,12},{5,13},{6,14},{7,15},{8,16},{9,17... | collective-permute-start | bytes 98312 | tf_op jit(solution)/shard_map/ppermute | solution.py:157
  33.6 6.9 %collective-permute-start.4 = (f32[8,8,128]{2,1,0:T(8,128)S(1)}, f32[8,8,128]{2,1,0:T(8,128)S(1)}, u32[]{:S(2)}, u32[]{:S(2)}) collective-permute-start(f32[8,8,128]{2,1,0:T(8,128)S(1)} %get-tuple-element.17), channel_id=1, source_target_pairs={{0,120},{1,121},{2,122},{3,123},{4,124},{5,125},{6,126},{7,127},{8... | collective-permute-start | bytes 98312 | tf_op jit(solution)/shard_map/ppermute | solution.py:157
  40.5 0.6 %copy-start.5 = (f32[8,8,128]{2,1,0:T(8,128)}, f32[8,8,128]{2,1,0:T(8,128)S(1)}, u32[]{:S(2)}) copy-start(f32[8,8,128]{2,1,0:T(8,128)S(1)} %collective-permute-done.5.lx_ref) | copy-start | bytes 98308
  40.6 0.6 %copy-start.6 = (f32[8,8,128]{2,1,0:T(8,128)}, f32[8,8,128]{2,1,0:T(8,128)S(1)}, u32[]{:S(2)}) copy-start(f32[8,8,128]{2,1,0:T(8,128)S(1)} %collective-permute-done.4.ux_ref) | copy-start | bytes 98308
  41.3 7.1 %collective-permute-start.7 = (f32[8,32,8]{2,1,0:T(8,128)S(1)}, f32[8,32,8]{2,1,0:T(8,128)S(1)}, u32[]{:S(2)}, u32[]{:S(2)}) collective-permute-start(f32[8,32,8]{2,1,0:T(8,128)S(1)} %get-tuple-element.10), channel_id=1, source_target_pairs={{0,1},{1,2},{2,3},{3,4},{4,5},{5,6},{6,7},{7,0},{8,9},{9,10},{10,1... | collective-permute-start | bytes 24584 | tf_op jit(solution)/shard_map/ppermute | solution.py:157
  41.3 7.1 %collective-permute-start.6 = (f32[8,32,8]{2,1,0:T(8,128)S(1)}, f32[8,32,8]{2,1,0:T(8,128)S(1)}, u32[]{:S(2)}, u32[]{:S(2)}) collective-permute-start(f32[8,32,8]{2,1,0:T(8,128)S(1)} %get-tuple-element.11), channel_id=1, source_target_pairs={{0,7},{1,0},{2,1},{3,2},{4,3},{5,4},{6,5},{7,6},{8,15},{9,8},{10,9... | collective-permute-start | bytes 24584 | tf_op jit(solution)/shard_map/ppermute | solution.py:157
  48.4 0.7 %copy-start.3 = (f32[8,32,8]{2,1,0:T(8,128)}, f32[8,32,8]{2,1,0:T(8,128)S(1)}, u32[]{:S(2)}) copy-start(f32[8,32,8]{2,1,0:T(8,128)S(1)} %collective-permute-done.7.ly_ref) | copy-start | bytes 24580
  49.1 0.7 %copy-start.4 = (f32[8,32,8]{2,1,0:T(8,128)}, f32[8,32,8]{2,1,0:T(8,128)S(1)}, u32[]{:S(2)}) copy-start(f32[8,32,8]{2,1,0:T(8,128)S(1)} %collective-permute-done.6.uy_ref) | copy-start | bytes 24580

commit v2 on v1

--- a/solution.py
+++ b/solution.py
@@ -40,11 +40,10 @@
     width = p.shape[1]
     masses = p[0:1]
     vals = jnp.concatenate([masses, masses * p[1:4]], axis=0)
-    cell = (c[0:1] * CX + c[1:2]) * CY + c[2:3]
     position = step * block + lax.broadcasted_iota(jnp.int32, (1, width), 1)
-    cell = jnp.where(position >= first, cell, -1)
-    row = lax.shift_right_arithmetic(cell, 8)
-    col = lax.bitwise_and(cell, COLS - 1)
+    row = lax.shift_right_logical(c[0:1], 1) * CX + c[1:2]
+    row = jnp.where(position >= first, row, -1)
+    col = lax.bitwise_and(c[0:1], 1) * CY + c[2:3]
     hi = vals.astype(jnp.bfloat16)
     lo = (vals - hi.astype(jnp.float32)).astype(jnp.bfloat16)
     parts = [q.astype(jnp.float32)[e : e + 1] for q in (hi, lo) for e in range(4)]
@@ -236,10 +235,12 @@
     from_plus_y = towards(minus_y, 0, -1)
     total = deposit_arrived(from_minus_x, from_plus_x, total, face)
     total = deposit_arrived(from_minus_y, from_plus_y, total, face + 2 * corner)
-    total = total.reshape(SPLITS, 4, ROWS * COLS)
-    density = (total[0, 0] + total[1, 0]).reshape(NZ, CX, CY)
+    total = total.reshape(SPLITS, 4, NZ // 2, CX, 2 * CY)
+    summed = total[0, 0] + total[1, 0]
+    density = jnp.stack([summed[..., :CY], summed[..., CY:]], axis=1).reshape(NZ, CX, CY)
     scalar_field = relax(bordered_density(density))
-    momentum = (total[0, 1:] + total[1, 1:]).reshape(3, NZ, CX, CY)
+    summed = total[0, 1:] + total[1, 1:]
+    momentum = jnp.stack([summed[..., :CY], summed[..., CY:]], axis=2).reshape(3, NZ, CX, CY)
     return (scalar_field, momentum)
 
 

time: 53.9 us -> 54.5 us (1.011)
  other arithmetic: 0.23 us -> 1.99 us
  local copies, waits for them, and re-layouts: 5.88 us -> 4.6 us
    add x1 -> x2, other arithmetic: 0.07 us -> 1.93 us  [the longest x1 1.05 us: staged(): summed = total[0, 1:] + total[1, 1:]]
    reshape x1 -> x0, local copies, waits for them, and re-layouts: 1.3 us -> none  [staged(): total = total.reshape(SPLITS, 4, ROWS * COLS)]
    another operation x0 -> x3, local copies, waits for them, and re-layouts: none -> 0.72 us  [the longest x2 0.71 us: staged(): jnp.stack([summed[..., :CY], summed[..., CY:]], axis=2)]
    unnamed x23 -> x22, local copies, waits for them, and re-layouts: 4.48 us -> 3.78 us
  transfers between devices with their start and end apart: 8 -> 8, of which waited for: 4 -> 4; matrix products, arithmetic and copies ran while one was open for 2% -> 1% of each run, Pallas kernels for 20% -> 19%
where the time goes in v2:
time: 54.5 us; the launch traced here: 54 us
  starting transfers between devices  20.1 us (37%)
  Pallas kernels  20 us (37%)
  waiting for transfers between devices  6.45 us (12%)
  local copies, waits for them, and re-layouts  4.6 us (8%)
  other arithmetic  1.99 us (4%)
  between operations  0.76 us (1%)
    ppermute x8, starting transfers between devices, towards(): return lax.ppermute(block, ('gx', 'gy'), route)  20.1 us
    pallas_call x2, Pallas kernels, deposit_arrived(): pl.pallas_call(lambda x, y, a, o: arrived_kernel(block, x, y, a, o), grid...  7.38 us
    pallas_call x1, Pallas kernels, deposit_local(): pl.pallas_call(local_kernel, grid_spec=pltpu.PrefetchScalarGridSpec(num_s...  7.12 us
    ppermute x8, waiting for transfers between devices, towards(): return lax.ppermute(block, ('gx', 'gy'), route)  6.45 us
    unnamed x22, local copies, waits for them, and re-layouts  3.78 us
    pallas_call x1, Pallas kernels, relax(): pl.pallas_call(relax_kernel, out_shape=jax.ShapeDtypeStruct((NZ, CX, CY),...  3.69 us
    pallas_call x1, Pallas kernels, pack(): pl.pallas_call(pack_kernel, in_specs=[pl.BlockSpec(memory_space=pltpu.SME...  1.85 us
  transfers between devices with their start and end apart: 8, of which 4 were waited for; matrix products, arithmetic and copies ran while one was open for 1% of the time, Pallas kernels for 19%

profile of v2, /device:TPU:0, one launch (start us, length us, event | category | flops | bytes accessed | tf_op | source)
XLA Modules:
  0.0 54.0 jit_solution(7801854566352085250)
XLA Ops:
  0.6 1.9 %shard_map.50 = (f32[7,3456]{1,0:T(8,128)}, f32[7,3456]{1,0:T(8,128)}, f32[7,2176]{1,0:T(8,128)}, f32[7,2176]{1,0:T(8,128)}) custom-call(s32[1,9]{1,0:T(1,128)} %count_ref.3, f32[4,16384]{1,0:T(4,128)} %p_ref.3, s32[3,16384]{1,0:T(4,128)} %c_ref.3), custom_call_target="tpu_custom_call" | custom-call | tf_op jit(solution)/shard_map/pallas_call | solution.py:138
  2.5 6.3 %collective-permute-start.1 = (f32[7,3456]{1,0:T(8,128)}, f32[7,3456]{1,0:T(8,128)S(1)}, u32[]{:S(2)}, u32[]{:S(2)}) collective-permute-start(f32[7,3456]{1,0:T(8,128)} %get-tuple-element.8), channel_id=1, source_target_pairs={{0,120},{1,121},{2,122},{3,123},{4,124},{5,125},{6,126},{7,127},{8... | collective-permute-start | bytes 290312 | tf_op jit(solution)/shard_map/ppermute | solution.py:156
  8.8 2.6 %collective-permute-done.x = f32[7,3456]{1,0:T(8,128)S(1)} collective-permute-done((f32[7,3456]{1,0:T(8,128)}, f32[7,3456]{1,0:T(8,128)S(1)}, u32[]{:S(2)}, u32[]{:S(2)}) %collective-permute-start) | collective-permute-done | bytes 96800 | tf_op jit(solution)/shard_map/ppermute | solution.py:156
  11.5 0.5 copy-done.1
  12.0 0.1 copy-done.2
  12.1 0.8 %collective-permute-start.2 = (f32[7,3456]{1,0:T(8,128)S(1)}, f32[7,3456]{1,0:T(8,128)S(1)}, u32[]{:S(2)}, u32[]{:S(2)}) collective-permute-start(f32[7,3456]{1,0:T(8,128)S(1)} %pad_maximum_fusion.2), channel_id=1, source_target_pairs={{0,1},{1,2},{2,3},{3,4},{4,5},{5,6},{6,7},{7,0},{8,9},{9,10},{10,1... | collective-permute-start | bytes 290312 | tf_op jit(solution)/shard_map/ppermute | solution.py:156
  12.9 3.4 %collective-permute-start.3 = (f32[7,3456]{1,0:T(8,128)S(1)}, f32[7,3456]{1,0:T(8,128)S(1)}, u32[]{:S(2)}, u32[]{:S(2)}) collective-permute-start(f32[7,3456]{1,0:T(8,128)S(1)} %pad_maximum_fusion.3), channel_id=1, source_target_pairs={{0,7},{1,0},{2,1},{3,2},{4,3},{5,4},{6,5},{7,6},{8,15},{9,8},{10,9... | collective-permute-start | bytes 290312 | tf_op jit(solution)/shard_map/ppermute | solution.py:156
  16.3 7.1 %shard_map.51.a = f32[512,256]{1,0:T(8,128)} custom-call(s32[1,9]{1,0:T(1,128)} %count_ref.3, f32[4,16384]{1,0:T(4,128)} %p_ref.3, s32[3,16384]{1,0:T(4,128)} %c_ref.3), custom_call_target="tpu_custom_call" | custom-call | tf_op jit(solution)/shard_map/pallas_call | solution.py:83
  23.4 3.3 %shard_map.52.a = f32[512,256]{1,0:T(8,128)} custom-call(f32[7,3456]{1,0:T(8,128)} %copy-done.1, f32[7,3456]{1,0:T(8,128)} %copy-done.2, f32[512,256]{1,0:T(8,128)} %shard_map.51.a), custom_call_target="tpu_custom_call", output_to_operand_aliasing={{}: (2, {})} | custom-call | tf_op jit(solution)/shard_map/pallas_call | solution.py:97
  26.8 0.6 %copy-done.7 = f32[7,3456]{1,0:T(8,128)} copy-done((f32[7,3456]{1,0:T(8,128)}, f32[7,3456]{1,0:T(8,128)S(1)}, u32[]{:S(2)}) %copy-start.7) | copy-done | bytes 96792
  27.4 0.6 %copy-done.8 = f32[7,3456]{1,0:T(8,128)} copy-done((f32[7,3456]{1,0:T(8,128)}, f32[7,3456]{1,0:T(8,128)S(1)}, u32[]{:S(2)}) %copy-start.8) | copy-done | bytes 96792
  28.1 4.0 %shard_map.53 = f32[512,256]{1,0:T(8,128)} custom-call(f32[7,3456]{1,0:T(8,128)} %copy-done.7, f32[7,3456]{1,0:T(8,128)} %copy-done.8, f32[512,256]{1,0:T(8,128)} %shard_map.52.a), custom_call_target="tpu_custom_call", output_to_operand_aliasing={{}: (2, {})} | custom-call | tf_op jit(solution)/shard_map/pallas_call | solution.py:97
  32.1 0.9 %fusion.1 = f32[4,16,256]{2,1,0:T(8,128)S(1)} fusion(f32[2,4,4,16,256]{4,3,2,1,0:T(8,128)} %bitcast.17), kind=kLoop, calls=%fused_computation.9 | loop fusion | flops 16384 | bytes 196608 | tf_op jit(solution)/shard_map/add | solution.py:239
  33.0 1.1 %fusion = f32[3,4,16,256]{3,2,1,0:T(8,128)S(1)} fusion(f32[2,4,4,16,256]{4,3,2,1,0:T(8,128)} %bitcast.18), kind=kLoop, calls=%fused_computation.1 | loop fusion | flops 49152 | bytes 589824 | tf_op jit(solution)/shard_map/add | solution.py:242
  34.2 5.3 %collective-permute-start.4 = (f32[8,8,128]{2,1,0:T(8,128)S(1)}, f32[8,8,128]{2,1,0:T(8,128)S(1)}, u32[]{:S(2)}, u32[]{:S(2)}) collective-permute-start(f32[8,8,128]{2,1,0:T(8,128)S(1)} %get-tuple-element.19), channel_id=1, source_target_pairs={{0,120},{1,121},{2,122},{3,123},{4,124},{5,125},{6,126},{7,127},{8... | collective-permute-start | bytes 98312 | tf_op jit(solution)/shard_map/ppermute | solution.py:156
  39.5 1.6 %collective-permute-done.5.lx_ref = f32[8,8,128]{2,1,0:T(8,128)S(1)} collective-permute-done((f32[8,8,128]{2,1,0:T(8,128)S(1)}, f32[8,8,128]{2,1,0:T(8,128)S(1)}, u32[]{:S(2)}, u32[]{:S(2)}) %collective-permute-start.5) | collective-permute-done | bytes 32800 | tf_op jit(solution)/shard_map/ppermute | solution.py:156
  41.2 0.6 %copy-done.5 = f32[8,8,128]{2,1,0:T(8,128)} copy-done((f32[8,8,128]{2,1,0:T(8,128)}, f32[8,8,128]{2,1,0:T(8,128)S(1)}, u32[]{:S(2)}) %copy-start.5) | copy-done | bytes 32792
  41.7 0.1 fusion.2
  41.9 4.1 %collective-permute-start.6 = (f32[8,32,8]{2,1,0:T(8,128)S(1)}, f32[8,32,8]{2,1,0:T(8,128)S(1)}, u32[]{:S(2)}, u32[]{:S(2)}) collective-permute-start(f32[8,32,8]{2,1,0:T(8,128)S(1)} %get-tuple-element.13), channel_id=1, source_target_pairs={{0,7},{1,0},{2,1},{3,2},{4,3},{5,4},{6,5},{7,6},{8,15},{9,8},{10,9... | collective-permute-start | bytes 24584 | tf_op jit(solution)/shard_map/ppermute | solution.py:156
  46.0 0.7 %copy.8 = f32[3,4,2,16,128]{4,3,2,1,0:T(8,128)} copy(f32[3,4,2,16,128]{4,3,1,0,2:T(8,128)S(1)} %pad_maximum_fusion) | data formatting | bytes 393216 | tf_op jit(solution)/shard_map/stack | solution.py:243
  46.7 2.2 %collective-permute-done.7.ly_ref = f32[8,32,8]{2,1,0:T(8,128)S(1)} collective-permute-done((f32[8,32,8]{2,1,0:T(8,128)S(1)}, f32[8,32,8]{2,1,0:T(8,128)S(1)}, u32[]{:S(2)}, u32[]{:S(2)}) %collective-permute-start.7) | collective-permute-done | bytes 8224 | tf_op jit(solution)/shard_map/ppermute | solution.py:156
  49.0 0.6 %copy-done.3 = f32[8,32,8]{2,1,0:T(8,128)} copy-done((f32[8,32,8]{2,1,0:T(8,128)}, f32[8,32,8]{2,1,0:T(8,128)S(1)}, u32[]{:S(2)}) %copy-start.3) | copy-done | bytes 8216
  49.6 0.6 %copy-done.4 = f32[8,32,8]{2,1,0:T(8,128)} copy-done((f32[8,32,8]{2,1,0:T(8,128)}, f32[8,32,8]{2,1,0:T(8,128)S(1)}, u32[]{:S(2)}) %copy-start.4) | copy-done | bytes 8216
  50.3 3.7 %shard_map.54 = f32[8,16,128]{2,1,0:T(8,128)} custom-call(f32[8,16,128]{2,1,0:T(8,128)} %bitcast.21, f32[8,8,128]{2,1,0:T(8,128)} %copy-done.6, f32[8,8,128]{2,1,0:T(8,128)} %copy-done.5, f32[8,32,8]{2,1,0:T(8,128)} %copy-done.4, f32[8,32,8]{2,1,0:T(8,128)} %copy-done.3), custom_call_target="tpu_custom_call" | custom-call | tf_op jit(solution)/shard_map/pallas_call | solution.py:214
  (33 shorter events, 0.4 us)
Async XLA Ops:
  2.5 8.9 %collective-permute-start = (f32[7,3456]{1,0:T(8,128)}, f32[7,3456]{1,0:T(8,128)S(1)}, u32[]{:S(2)}, u32[]{:S(2)}) collective-permute-start(f32[7,3456]{1,0:T(8,128)} %get-tuple-element.7), channel_id=1, source_target_pairs={{0,8},{1,9},{2,10},{3,11},{4,12},{5,13},{6,14},{7,15},{8,16},{9,17... | collective-permute-start | bytes 290312 | tf_op jit(solution)/shard_map/ppermute | solution.py:156
  2.5 8.9 %copy-start.10 = (f32[7,2176]{1,0:T(8,128)S(1)}, f32[7,2176]{1,0:T(8,128)}, u32[]{:S(2)}) copy-start(f32[7,2176]{1,0:T(8,128)} %get-tuple-element.6) | copy-start | bytes 182788
  2.5 8.9 %collective-permute-start.1 = (f32[7,3456]{1,0:T(8,128)}, f32[7,3456]{1,0:T(8,128)S(1)}, u32[]{:S(2)}, u32[]{:S(2)}) collective-permute-start(f32[7,3456]{1,0:T(8,128)} %get-tuple-element.8), channel_id=1, source_target_pairs={{0,120},{1,121},{2,122},{3,123},{4,124},{5,125},{6,126},{7,127},{8... | collective-permute-start | bytes 290312 | tf_op jit(solution)/shard_map/ppermute | solution.py:156
  11.3 0.6 %copy-start.1 = (f32[7,3456]{1,0:T(8,128)}, f32[7,3456]{1,0:T(8,128)S(1)}, u32[]{:S(2)}) copy-start(f32[7,3456]{1,0:T(8,128)S(1)} %collective-permute-done.x) | copy-start | bytes 290308
  11.4 0.7 %copy-start.2 = (f32[7,3456]{1,0:T(8,128)}, f32[7,3456]{1,0:T(8,128)S(1)}, u32[]{:S(2)}) copy-start(f32[7,3456]{1,0:T(8,128)S(1)} %collective-permute-done.1.y) | copy-start | bytes 290308
  11.4 1.4 %copy-start.9 = (f32[7,2176]{1,0:T(8,128)S(1)}, f32[7,2176]{1,0:T(8,128)}, u32[]{:S(2)}) copy-start(f32[7,2176]{1,0:T(8,128)} %get-tuple-element.9) | copy-start | bytes 182788
  12.1 14.7 %collective-permute-start.2 = (f32[7,3456]{1,0:T(8,128)S(1)}, f32[7,3456]{1,0:T(8,128)S(1)}, u32[]{:S(2)}, u32[]{:S(2)}) collective-permute-start(f32[7,3456]{1,0:T(8,128)S(1)} %pad_maximum_fusion.2), channel_id=1, source_target_pairs={{0,1},{1,2},{2,3},{3,4},{4,5},{5,6},{6,7},{7,0},{8,9},{9,10},{10,1... | collective-permute-start | bytes 290312 | tf_op jit(solution)/shard_map/ppermute | solution.py:156
  12.9 13.9 %collective-permute-start.3 = (f32[7,3456]{1,0:T(8,128)S(1)}, f32[7,3456]{1,0:T(8,128)S(1)}, u32[]{:S(2)}, u32[]{:S(2)}) collective-permute-start(f32[7,3456]{1,0:T(8,128)S(1)} %pad_maximum_fusion.3), channel_id=1, source_target_pairs={{0,7},{1,0},{2,1},{3,2},{4,3},{5,4},{6,5},{7,6},{8,15},{9,8},{10,9... | collective-permute-start | bytes 290312 | tf_op jit(solution)/shard_map/ppermute | solution.py:156
  26.8 0.6 %copy-start.7 = (f32[7,3456]{1,0:T(8,128)}, f32[7,3456]{1,0:T(8,128)S(1)}, u32[]{:S(2)}) copy-start(f32[7,3456]{1,0:T(8,128)S(1)} %collective-permute-done.2.x) | copy-start | bytes 290308
  27.4 0.7 %copy-start.8 = (f32[7,3456]{1,0:T(8,128)}, f32[7,3456]{1,0:T(8,128)S(1)}, u32[]{:S(2)}) copy-start(f32[7,3456]{1,0:T(8,128)S(1)} %collective-permute-done.3.y) | copy-start | bytes 290308
  34.1 7.1 %copy-start = (f32[4,2,16,128]{3,2,1,0:T(8,128)}, f32[4,2,16,128]{3,2,1,0:T(8,128)S(1)}, u32[]{:S(2)}) copy-start(f32[4,2,16,128]{3,2,1,0:T(8,128)S(1)} %pad_maximum_fusion.4) | copy-start | bytes 196612
  34.1 7.0 %collective-permute-start.5 = (f32[8,8,128]{2,1,0:T(8,128)S(1)}, f32[8,8,128]{2,1,0:T(8,128)S(1)}, u32[]{:S(2)}, u32[]{:S(2)}) collective-permute-start(f32[8,8,128]{2,1,0:T(8,128)S(1)} %get-tuple-element.18), channel_id=1, source_target_pairs={{0,8},{1,9},{2,10},{3,11},{4,12},{5,13},{6,14},{7,15},{8,16},{9,17... | collective-permute-start | bytes 98312 | tf_op jit(solution)/shard_map/ppermute | solution.py:156
  34.2 6.9 %collective-permute-start.4 = (f32[8,8,128]{2,1,0:T(8,128)S(1)}, f32[8,8,128]{2,1,0:T(8,128)S(1)}, u32[]{:S(2)}, u32[]{:S(2)}) collective-permute-start(f32[8,8,128]{2,1,0:T(8,128)S(1)} %get-tuple-element.19), channel_id=1, source_target_pairs={{0,120},{1,121},{2,122},{3,123},{4,124},{5,125},{6,126},{7,127},{8... | collective-permute-start | bytes 98312 | tf_op jit(solution)/shard_map/ppermute | solution.py:156
  41.1 0.6 %copy-start.5 = (f32[8,8,128]{2,1,0:T(8,128)}, f32[8,8,128]{2,1,0:T(8,128)S(1)}, u32[]{:S(2)}) copy-start(f32[8,8,128]{2,1,0:T(8,128)S(1)} %collective-permute-done.5.lx_ref) | copy-start | bytes 98308
  41.1 0.6 %copy-start.6 = (f32[8,8,128]{2,1,0:T(8,128)}, f32[8,8,128]{2,1,0:T(8,128)S(1)}, u32[]{:S(2)}) copy-start(f32[8,8,128]{2,1,0:T(8,128)S(1)} %collective-permute-done.4.ux_ref) | copy-start | bytes 98308
  41.8 7.1 %collective-permute-start.7 = (f32[8,32,8]{2,1,0:T(8,128)S(1)}, f32[8,32,8]{2,1,0:T(8,128)S(1)}, u32[]{:S(2)}, u32[]{:S(2)}) collective-permute-start(f32[8,32,8]{2,1,0:T(8,128)S(1)} %get-tuple-element.12), channel_id=1, source_target_pairs={{0,1},{1,2},{2,3},{3,4},{4,5},{5,6},{6,7},{7,0},{8,9},{9,10},{10,1... | collective-permute-start | bytes 24584 | tf_op jit(solution)/shard_map/ppermute | solution.py:156
  41.9 7.1 %collective-permute-start.6 = (f32[8,32,8]{2,1,0:T(8,128)S(1)}, f32[8,32,8]{2,1,0:T(8,128)S(1)}, u32[]{:S(2)}, u32[]{:S(2)}) collective-permute-start(f32[8,32,8]{2,1,0:T(8,128)S(1)} %get-tuple-element.13), channel_id=1, source_target_pairs={{0,7},{1,0},{2,1},{3,2},{4,3},{5,4},{6,5},{7,6},{8,15},{9,8},{10,9... | collective-permute-start | bytes 24584 | tf_op jit(solution)/shard_map/ppermute | solution.py:156
  49.0 0.7 %copy-start.3 = (f32[8,32,8]{2,1,0:T(8,128)}, f32[8,32,8]{2,1,0:T(8,128)S(1)}, u32[]{:S(2)}) copy-start(f32[8,32,8]{2,1,0:T(8,128)S(1)} %collective-permute-done.7.ly_ref) | copy-start | bytes 24580
  49.6 0.6 %copy-start.4 = (f32[8,32,8]{2,1,0:T(8,128)}, f32[8,32,8]{2,1,0:T(8,128)S(1)}, u32[]{:S(2)}) copy-start(f32[8,32,8]{2,1,0:T(8,128)S(1)} %collective-permute-done.6.uy_ref) | copy-start | bytes 24580

commit v3 on v2

--- a/solution.py
+++ b/solution.py
@@ -68,9 +68,10 @@
         accumulate(first, BLOCK, step, p_ref[...], c_ref[...], o_ref)
 
 
-def arrived_kernel(block, x_ref, y_ref, a_ref, o_ref):
+def arrived_kernel(block, *refs):
+    a_ref, o_ref = refs[-2], refs[-1]
     o_ref[...] = a_ref[...]
-    for source in (x_ref, y_ref):
+    for source in refs[:-2]:
         x = source[...]
         accumulate(0, block, 0, x[0:4], x[4:7].astype(jnp.int32), o_ref)
 
@@ -93,19 +94,17 @@
     )(counts, payload, cells)
 
 
-def deposit_arrived(first, second, acc, block):
-    return pl.pallas_call(
-        lambda x, y, a, o: arrived_kernel(block, x, y, a, o),
+def deposit_arrived(sources, acc, block):
+    count = len(sources)
+    return pl.pallas_call(
+        lambda *refs: arrived_kernel(block, *refs),
         grid=(1,),
-        in_specs=[
-            pl.BlockSpec((7, block), lambda b: (0, 0)),
-            pl.BlockSpec((7, block), lambda b: (0, 0)),
-            pl.BlockSpec(ACC_SHAPE, lambda b: (0, 0)),
-        ],
+        in_specs=[pl.BlockSpec((7, block), lambda b: (0, 0)) for source in sources]
+        + [pl.BlockSpec(ACC_SHAPE, lambda b: (0, 0))],
         out_specs=pl.BlockSpec(ACC_SHAPE, lambda b: (0, 0)),
         out_shape=jax.ShapeDtypeStruct(ACC_SHAPE, jnp.float32),
-        input_output_aliases={2: 0},
-    )(first, second, acc)
+        input_output_aliases={count: 0},
+    )(*sources, acc)
 
 
 def pack_kernel(count_ref, p_ref, c_ref, plus_x, minus_x, plus_y, minus_y):
@@ -224,17 +223,17 @@
     plus_x, minus_x, plus_y, minus_y = pack(payload, cells, counts)
     from_minus_x = towards(plus_x, 1, 0)
     from_plus_x = towards(minus_x, -1, 0)
-    total = deposit_local(payload, cells, counts)
-    plus_y = jnp.concatenate(
-        [plus_y, from_minus_x[:, face : face + corner], from_plus_x[:, face : face + corner]], axis=1
-    )
-    minus_y = jnp.concatenate(
-        [minus_y, from_minus_x[:, face + corner :], from_plus_x[:, face + corner :]], axis=1
-    )
     from_minus_y = towards(plus_y, 0, 1)
     from_plus_y = towards(minus_y, 0, -1)
-    total = deposit_arrived(from_minus_x, from_plus_x, total, face)
-    total = deposit_arrived(from_minus_y, from_plus_y, total, face + 2 * corner)
+    total = deposit_local(payload, cells, counts)
+    upward = jnp.concatenate(
+        [from_minus_x[:, face : face + corner], from_plus_x[:, face : face + corner]], axis=1
+    )
+    downward = jnp.concatenate([from_minus_x[:, face + corner :], from_plus_x[:, face + corner :]], axis=1)
+    corners_below = towards(upward, 0, 1)
+    corners_above = towards(downward, 0, -1)
+    total = deposit_arrived((from_minus_x, from_plus_x, from_minus_y, from_plus_y), total, face)
+    total = deposit_arrived((corners_below, corners_above), total, 2 * corner)
     total = total.reshape(SPLITS, 4, NZ // 2, CX, 2 * CY)
     summed = total[0, 0] + total[1, 0]
     density = jnp.stack([summed[..., :CY], summed[..., CY:]], axis=1).reshape(NZ, CX, CY)

time: 54.5 us -> 63.2 us (1.16)
  waiting for transfers between devices: 6.45 us -> 13.4 us
  starting transfers between devices: 20.1 us -> 21.2 us
    ppermute x8 -> x10, waiting for transfers between devices: 6.45 us -> 13.4 us  [towards(): return lax.ppermute(block, ('gx', 'gy'), route)]
    ppermute x8 -> x10, starting transfers between devices: 20.1 us -> 21.2 us  [towards(): return lax.ppermute(block, ('gx', 'gy'), route)]
  transfers between devices with their start and end apart: 8 -> 10, of which waited for: 4 -> 4; matrix products, arithmetic and copies ran while one was open for 1% -> 1% of each run, Pallas kernels for 19% -> 19%
where the time goes in v3:
time: 63.2 us; the launch traced here: 62.6 us
  starting transfers between devices  21.2 us (34%)
  Pallas kernels  20.1 us (32%)
  waiting for transfers between devices  13.4 us (21%)
  local copies, waits for them, and re-layouts  5.11 us (8%)
  other arithmetic  1.97 us (3%)
  between operations  0.76 us (1%)
    ppermute x10, starting transfers between devices, towards(): return lax.ppermute(block, ('gx', 'gy'), route)  21.2 us
    ppermute x10, waiting for transfers between devices, towards(): return lax.ppermute(block, ('gx', 'gy'), route)  13.4 us
    pallas_call x2, Pallas kernels, deposit_arrived(): pl.pallas_call(lambda *refs: arrived_kernel(block, *refs), grid=(1,), in_...  7.41 us
    pallas_call x1, Pallas kernels, deposit_local(): pl.pallas_call(local_kernel, grid_spec=pltpu.PrefetchScalarGridSpec(num_s...  7.13 us
    unnamed x22, local copies, waits for them, and re-layouts  4.29 us
    pallas_call x1, Pallas kernels, relax(): pl.pallas_call(relax_kernel, out_shape=jax.ShapeDtypeStruct((NZ, CX, CY),...  3.69 us
    pallas_call x1, Pallas kernels, pack(): pl.pallas_call(pack_kernel, in_specs=[pl.BlockSpec(memory_space=pltpu.SME...  1.85 us
  transfers between devices with their start and end apart: 10, of which 4 were waited for; matrix products, arithmetic and copies ran while one was open for 1% of the time, Pallas kernels for 19%

profile of v3, /device:TPU:0, one launch (start us, length us, event | category | flops | bytes accessed | tf_op | source)
XLA Modules:
  0.0 62.6 jit_solution(17674797643935655402)
XLA Ops:
  0.6 1.9 %shard_map.50 = (f32[7,3456]{1,0:T(8,128)}, f32[7,3456]{1,0:T(8,128)}, f32[7,2176]{1,0:T(8,128)}, f32[7,2176]{1,0:T(8,128)}) custom-call(s32[1,9]{1,0:T(1,128)} %count_ref.3, f32[4,16384]{1,0:T(4,128)} %p_ref.3, s32[3,16384]{1,0:T(4,128)} %c_ref.3), custom_call_target="tpu_custom_call" | custom-call | tf_op jit(solution)/shard_map/pallas_call | solution.py:137
  2.5 6.3 %collective-permute-start.1 = (f32[7,3456]{1,0:T(8,128)}, f32[7,3456]{1,0:T(8,128)S(1)}, u32[]{:S(2)}, u32[]{:S(2)}) collective-permute-start(f32[7,3456]{1,0:T(8,128)} %get-tuple-element.7), channel_id=1, source_target_pairs={{0,120},{1,121},{2,122},{3,123},{4,124},{5,125},{6,126},{7,127},{8... | collective-permute-start | bytes 290312 | tf_op jit(solution)/shard_map/ppermute | solution.py:155
  8.8 0.8 %collective-permute-start.4 = (f32[7,2176]{1,0:T(8,128)}, f32[7,2176]{1,0:T(8,128)S(1)}, u32[]{:S(2)}, u32[]{:S(2)}) collective-permute-start(f32[7,2176]{1,0:T(8,128)} %get-tuple-element.8), channel_id=1, source_target_pairs={{0,1},{1,2},{2,3},{3,4},{4,5},{5,6},{6,7},{7,0},{8,9},{9,10},{10,1... | collective-permute-start | bytes 182792 | tf_op jit(solution)/shard_map/ppermute | solution.py:155
  9.5 3.4 %collective-permute-start.5 = (f32[7,2176]{1,0:T(8,128)}, f32[7,2176]{1,0:T(8,128)S(1)}, u32[]{:S(2)}, u32[]{:S(2)}) collective-permute-start(f32[7,2176]{1,0:T(8,128)} %get-tuple-element.9), channel_id=1, source_target_pairs={{0,7},{1,0},{2,1},{3,2},{4,3},{5,4},{6,5},{7,6},{8,15},{9,8},{10,9... | collective-permute-start | bytes 182792 | tf_op jit(solution)/shard_map/ppermute | solution.py:155
  13.6 1.5 %collective-permute-start.3 = (f32[7,1280]{1,0:T(8,128)S(1)}, f32[7,1280]{1,0:T(8,128)S(1)}, u32[]{:S(2)}, u32[]{:S(2)}) collective-permute-start(f32[7,1280]{1,0:T(8,128)S(1)} %pad_maximum_fusion.4), channel_id=1, source_target_pairs={{0,7},{1,0},{2,1},{3,2},{4,3},{5,4},{6,5},{7,6},{8,15},{9,8},{10,9... | collective-permute-start | bytes 107528 | tf_op jit(solution)/shard_map/ppermute | solution.py:155
  15.0 0.6 %collective-permute-start.2 = (f32[7,1280]{1,0:T(8,128)S(1)}, f32[7,1280]{1,0:T(8,128)S(1)}, u32[]{:S(2)}, u32[]{:S(2)}) collective-permute-start(f32[7,1280]{1,0:T(8,128)S(1)} %pad_maximum_fusion.3), channel_id=1, source_target_pairs={{0,1},{1,2},{2,3},{3,4},{4,5},{5,6},{6,7},{7,0},{8,9},{9,10},{10,1... | collective-permute-start | bytes 107528 | tf_op jit(solution)/shard_map/ppermute | solution.py:155
  15.7 7.1 %shard_map.51.refs_4_ = f32[512,256]{1,0:T(8,128)} custom-call(s32[1,9]{1,0:T(1,128)} %count_ref.3, f32[4,16384]{1,0:T(4,128)} %p_ref.3, s32[3,16384]{1,0:T(4,128)} %c_ref.3), custom_call_target="tpu_custom_call" | custom-call | tf_op jit(solution)/shard_map/pallas_call | solution.py:84
  22.8 0.6 copy-done.7
  23.4 0.6 copy-done.8
  24.0 4.6 %shard_map.52.refs_2_ = f32[512,256]{1,0:T(8,128)} custom-call(f32[7,3456]{1,0:T(8,128)} %copy-done.1, f32[7,3456]{1,0:T(8,128)} %copy-done.2, f32[7,2176]{1,0:T(8,128)} %copy-done.7, f32[7,2176]{1,0:T(8,128)} %copy-done.8, f32[512,256]{1,0:T(8,128)} %shard_map.51.refs_4_), custom_call_target="tpu_custom_call", output_to_operand_aliasing={{}: (4, {})} | custom-call | tf_op jit(solution)/shard_map/pallas_call | solution.py:99
  28.7 0.6 copy-done.9
  29.3 0.6 copy-done.10
  29.9 2.8 %shard_map.53 = f32[512,256]{1,0:T(8,128)} custom-call(f32[7,1280]{1,0:T(8,128)} %copy-done.10, f32[7,1280]{1,0:T(8,128)} %copy-done.9, f32[512,256]{1,0:T(8,128)} %shard_map.52.refs_2_), custom_call_target="tpu_custom_call", output_to_operand_aliasing={{}: (2, {})} | custom-call | tf_op jit(solution)/shard_map/pallas_call | solution.py:99
  32.7 1.0 %fusion = f32[3,4,16,256]{3,2,1,0:T(8,128)S(1)} fusion(f32[2,4,4,16,256]{4,3,2,1,0:T(8,128)} %bitcast.17), kind=kLoop, calls=%fused_computation.1 | loop fusion | flops 49152 | bytes 589824 | tf_op jit(solution)/shard_map/add | solution.py:241
  33.7 0.9 %fusion.1 = f32[4,16,256]{2,1,0:T(8,128)S(1)} fusion(f32[2,4,4,16,256]{4,3,2,1,0:T(8,128)} %bitcast.18), kind=kLoop, calls=%fused_computation.7 | loop fusion | flops 16384 | bytes 196608 | tf_op jit(solution)/shard_map/add | solution.py:238
  34.7 4.4 %collective-permute-start.6 = (f32[8,8,128]{2,1,0:T(8,128)S(1)}, f32[8,8,128]{2,1,0:T(8,128)S(1)}, u32[]{:S(2)}, u32[]{:S(2)}) collective-permute-start(f32[8,8,128]{2,1,0:T(8,128)S(1)} %get-tuple-element.19), channel_id=1, source_target_pairs={{0,120},{1,121},{2,122},{3,123},{4,124},{5,125},{6,126},{7,127},{8... | collective-permute-start | bytes 98312 | tf_op jit(solution)/shard_map/ppermute | solution.py:155
  39.1 1.6 %collective-permute-done.6.ux_ref = f32[8,8,128]{2,1,0:T(8,128)S(1)} collective-permute-done((f32[8,8,128]{2,1,0:T(8,128)S(1)}, f32[8,8,128]{2,1,0:T(8,128)S(1)}, u32[]{:S(2)}, u32[]{:S(2)}) %collective-permute-start.6) | collective-permute-done | bytes 32800 | tf_op jit(solution)/shard_map/ppermute | solution.py:155
  40.6 5.5 %collective-permute-done.7.lx_ref = f32[8,8,128]{2,1,0:T(8,128)S(1)} collective-permute-done((f32[8,8,128]{2,1,0:T(8,128)S(1)}, f32[8,8,128]{2,1,0:T(8,128)S(1)}, u32[]{:S(2)}, u32[]{:S(2)}) %collective-permute-start.7) | collective-permute-done | bytes 32800 | tf_op jit(solution)/shard_map/ppermute | solution.py:155
  46.8 4.3 %collective-permute-start.8 = (f32[8,32,8]{2,1,0:T(8,128)S(1)}, f32[8,32,8]{2,1,0:T(8,128)S(1)}, u32[]{:S(2)}, u32[]{:S(2)}) collective-permute-start(f32[8,32,8]{2,1,0:T(8,128)S(1)} %get-tuple-element.13), channel_id=1, source_target_pairs={{0,7},{1,0},{2,1},{3,2},{4,3},{5,4},{6,5},{7,6},{8,15},{9,8},{10,9... | collective-permute-start | bytes 24584 | tf_op jit(solution)/shard_map/ppermute | solution.py:155
  51.2 0.7 %copy.8 = f32[3,4,2,16,128]{4,3,2,1,0:T(8,128)} copy(f32[3,4,2,16,128]{4,3,1,0,2:T(8,128)S(1)} %pad_maximum_fusion) | data formatting | bytes 393216 | tf_op jit(solution)/shard_map/stack | solution.py:242
  51.9 1.8 %collective-permute-done.8.uy_ref = f32[8,32,8]{2,1,0:T(8,128)S(1)} collective-permute-done((f32[8,32,8]{2,1,0:T(8,128)S(1)}, f32[8,32,8]{2,1,0:T(8,128)S(1)}, u32[]{:S(2)}, u32[]{:S(2)}) %collective-permute-start.8) | collective-permute-done | bytes 8224 | tf_op jit(solution)/shard_map/ppermute | solution.py:155
  53.7 4.6 %collective-permute-done.9.ly_ref = f32[8,32,8]{2,1,0:T(8,128)S(1)} collective-permute-done((f32[8,32,8]{2,1,0:T(8,128)S(1)}, f32[8,32,8]{2,1,0:T(8,128)S(1)}, u32[]{:S(2)}, u32[]{:S(2)}) %collective-permute-start.9) | collective-permute-done | bytes 8224 | tf_op jit(solution)/shard_map/ppermute | solution.py:155
  58.2 0.6 %copy-done.4 = f32[8,32,8]{2,1,0:T(8,128)} copy-done((f32[8,32,8]{2,1,0:T(8,128)}, f32[8,32,8]{2,1,0:T(8,128)S(1)}, u32[]{:S(2)}) %copy-start.4) | copy-done | bytes 8216
  58.9 3.7 %shard_map.54 = f32[8,16,128]{2,1,0:T(8,128)} custom-call(f32[8,16,128]{2,1,0:T(8,128)} %bitcast.21, f32[8,8,128]{2,1,0:T(8,128)} %copy-done.5, f32[8,8,128]{2,1,0:T(8,128)} %copy-done.6, f32[8,32,8]{2,1,0:T(8,128)} %copy-done.3, f32[8,32,8]{2,1,0:T(8,128)} %copy-done.4), custom_call_target="tpu_custom_call" | custom-call | tf_op jit(solution)/shard_map/pallas_call | solution.py:213
  (37 shorter events, 1.4 us)
Async XLA Ops:
  2.5 10.4 %collective-permute-start = (f32[7,3456]{1,0:T(8,128)}, f32[7,3456]{1,0:T(8,128)S(1)}, u32[]{:S(2)}, u32[]{:S(2)}) collective-permute-start(f32[7,3456]{1,0:T(8,128)} %get-tuple-element.6), channel_id=1, source_target_pairs={{0,8},{1,9},{2,10},{3,11},{4,12},{5,13},{6,14},{7,15},{8,16},{9,17... | collective-permute-start | bytes 290312 | tf_op jit(solution)/shard_map/ppermute | solution.py:155
  2.5 10.4 %collective-permute-start.1 = (f32[7,3456]{1,0:T(8,128)}, f32[7,3456]{1,0:T(8,128)S(1)}, u32[]{:S(2)}, u32[]{:S(2)}) collective-permute-start(f32[7,3456]{1,0:T(8,128)} %get-tuple-element.7), channel_id=1, source_target_pairs={{0,120},{1,121},{2,122},{3,123},{4,124},{5,125},{6,126},{7,127},{8... | collective-permute-start | bytes 290312 | tf_op jit(solution)/shard_map/ppermute | solution.py:155
  8.8 14.0 %collective-permute-start.4 = (f32[7,2176]{1,0:T(8,128)}, f32[7,2176]{1,0:T(8,128)S(1)}, u32[]{:S(2)}, u32[]{:S(2)}) collective-permute-start(f32[7,2176]{1,0:T(8,128)} %get-tuple-element.8), channel_id=1, source_target_pairs={{0,1},{1,2},{2,3},{3,4},{4,5},{5,6},{6,7},{7,0},{8,9},{9,10},{10,1... | collective-permute-start | bytes 182792 | tf_op jit(solution)/shard_map/ppermute | solution.py:155
  9.5 13.3 %collective-permute-start.5 = (f32[7,2176]{1,0:T(8,128)}, f32[7,2176]{1,0:T(8,128)S(1)}, u32[]{:S(2)}, u32[]{:S(2)}) collective-permute-start(f32[7,2176]{1,0:T(8,128)} %get-tuple-element.9), channel_id=1, source_target_pairs={{0,7},{1,0},{2,1},{3,2},{4,3},{5,4},{6,5},{7,6},{8,15},{9,8},{10,9... | collective-permute-start | bytes 182792 | tf_op jit(solution)/shard_map/ppermute | solution.py:155
  12.9 0.6 %copy-start.1 = (f32[7,3456]{1,0:T(8,128)}, f32[7,3456]{1,0:T(8,128)S(1)}, u32[]{:S(2)}) copy-start(f32[7,3456]{1,0:T(8,128)S(1)} %collective-permute-done.refs_0_) | copy-start | bytes 290308
  12.9 2.1 %copy-start.2 = (f32[7,3456]{1,0:T(8,128)}, f32[7,3456]{1,0:T(8,128)S(1)}, u32[]{:S(2)}) copy-start(f32[7,3456]{1,0:T(8,128)S(1)} %collective-permute-done.1.refs_1_) | copy-start | bytes 290308
  13.6 15.1 %collective-permute-start.3 = (f32[7,1280]{1,0:T(8,128)S(1)}, f32[7,1280]{1,0:T(8,128)S(1)}, u32[]{:S(2)}, u32[]{:S(2)}) collective-permute-start(f32[7,1280]{1,0:T(8,128)S(1)} %pad_maximum_fusion.4), channel_id=1, source_target_pairs={{0,7},{1,0},{2,1},{3,2},{4,3},{5,4},{6,5},{7,6},{8,15},{9,8},{10,9... | collective-permute-start | bytes 107528 | tf_op jit(solution)/shard_map/ppermute | solution.py:155
  15.0 13.7 %collective-permute-start.2 = (f32[7,1280]{1,0:T(8,128)S(1)}, f32[7,1280]{1,0:T(8,128)S(1)}, u32[]{:S(2)}, u32[]{:S(2)}) collective-permute-start(f32[7,1280]{1,0:T(8,128)S(1)} %pad_maximum_fusion.3), channel_id=1, source_target_pairs={{0,1},{1,2},{2,3},{3,4},{4,5},{5,6},{6,7},{7,0},{8,9},{9,10},{10,1... | collective-permute-start | bytes 107528 | tf_op jit(solution)/shard_map/ppermute | solution.py:155
  22.8 0.6 %copy-start.7 = (f32[7,2176]{1,0:T(8,128)}, f32[7,2176]{1,0:T(8,128)S(1)}, u32[]{:S(2)}) copy-start(f32[7,2176]{1,0:T(8,128)S(1)} %collective-permute-done.4.refs_2_) | copy-start | bytes 182788
  23.4 0.6 copy-start.8
  28.7 0.6 copy-start.9
  29.3 0.6 copy-start.10
  34.7 11.5 %copy-start = (f32[4,2,16,128]{3,2,1,0:T(8,128)}, f32[4,2,16,128]{3,2,1,0:T(8,128)S(1)}, u32[]{:S(2)}) copy-start(f32[4,2,16,128]{3,2,1,0:T(8,128)S(1)} %pad_maximum_fusion.2) | copy-start | bytes 196612
  34.7 6.0 %collective-permute-start.6 = (f32[8,8,128]{2,1,0:T(8,128)S(1)}, f32[8,8,128]{2,1,0:T(8,128)S(1)}, u32[]{:S(2)}, u32[]{:S(2)}) collective-permute-start(f32[8,8,128]{2,1,0:T(8,128)S(1)} %get-tuple-element.19), channel_id=1, source_target_pairs={{0,120},{1,121},{2,122},{3,123},{4,124},{5,125},{6,126},{7,127},{8... | collective-permute-start | bytes 98312 | tf_op jit(solution)/shard_map/ppermute | solution.py:155
  39.0 7.1 %collective-permute-start.7 = (f32[8,8,128]{2,1,0:T(8,128)S(1)}, f32[8,8,128]{2,1,0:T(8,128)S(1)}, u32[]{:S(2)}, u32[]{:S(2)}) collective-permute-start(f32[8,8,128]{2,1,0:T(8,128)S(1)} %get-tuple-element.18), channel_id=1, source_target_pairs={{0,8},{1,9},{2,10},{3,11},{4,12},{5,13},{6,14},{7,15},{8,16},{9,17... | collective-permute-start | bytes 98312 | tf_op jit(solution)/shard_map/ppermute | solution.py:155
  40.6 5.5 %copy-start.5 = (f32[8,8,128]{2,1,0:T(8,128)}, f32[8,8,128]{2,1,0:T(8,128)S(1)}, u32[]{:S(2)}) copy-start(f32[8,8,128]{2,1,0:T(8,128)S(1)} %collective-permute-done.6.ux_ref) | copy-start | bytes 98308
  46.1 0.6 copy-start.6
  46.8 6.9 %collective-permute-start.8 = (f32[8,32,8]{2,1,0:T(8,128)S(1)}, f32[8,32,8]{2,1,0:T(8,128)S(1)}, u32[]{:S(2)}, u32[]{:S(2)}) collective-permute-start(f32[8,32,8]{2,1,0:T(8,128)S(1)} %get-tuple-element.13), channel_id=1, source_target_pairs={{0,7},{1,0},{2,1},{3,2},{4,3},{5,4},{6,5},{7,6},{8,15},{9,8},{10,9... | collective-permute-start | bytes 24584 | tf_op jit(solution)/shard_map/ppermute | solution.py:155
  51.2 7.1 %collective-permute-start.9 = (f32[8,32,8]{2,1,0:T(8,128)S(1)}, f32[8,32,8]{2,1,0:T(8,128)S(1)}, u32[]{:S(2)}, u32[]{:S(2)}) collective-permute-start(f32[8,32,8]{2,1,0:T(8,128)S(1)} %get-tuple-element.12), channel_id=1, source_target_pairs={{0,1},{1,2},{2,3},{3,4},{4,5},{5,6},{6,7},{7,0},{8,9},{9,10},{10,1... | collective-permute-start | bytes 24584 | tf_op jit(solution)/shard_map/ppermute | solution.py:155
  53.7 4.6 %copy-start.3 = (f32[8,32,8]{2,1,0:T(8,128)}, f32[8,32,8]{2,1,0:T(8,128)S(1)}, u32[]{:S(2)}) copy-start(f32[8,32,8]{2,1,0:T(8,128)S(1)} %collective-permute-done.8.uy_ref) | copy-start | bytes 24580
  58.2 0.6 %copy-start.4 = (f32[8,32,8]{2,1,0:T(8,128)}, f32[8,32,8]{2,1,0:T(8,128)S(1)}, u32[]{:S(2)}) copy-start(f32[8,32,8]{2,1,0:T(8,128)S(1)} %collective-permute-done.9.ly_ref) | copy-start | bytes 24580

commit v4 on v2

--- a/solution.py
+++ b/solution.py
@@ -11,6 +11,7 @@
 SWEEPS = 4
 CAP_F = 2048
 CAP_D = 512
+MY = 16
 
 
 SCREENING = 0.5
@@ -53,6 +54,48 @@
     acc_ref[...] += lax.dot_general(
         left, right, (((1,), (1,)), ((), ())), preferred_element_type=jnp.float32
     )
+
+
+def crossing_kernel(x_ref, y_ref, a_ref, o_ref):
+    o_ref[...] = a_ref[...]
+    for source, low in ((x_ref, 0), (y_ref, CY - MY)):
+        x = source[...]
+        p = x[0:4]
+        c = x[4:7].astype(jnp.int32)
+        width = p.shape[1]
+        masses = p[0:1]
+        vals = jnp.concatenate([masses, masses * p[1:4]], axis=0)
+        row = lax.shift_right_logical(c[0:1], 1) * CX + c[1:2]
+        near_j = c[2:3] - low
+        row = jnp.where((near_j >= 0) & (near_j < MY), row, -1)
+        col = lax.bitwise_and(c[0:1], 1) * MY + near_j
+        hi = vals.astype(jnp.bfloat16)
+        lo = (vals - hi.astype(jnp.float32)).astype(jnp.bfloat16)
+        parts = [q.astype(jnp.float32)[e : e + 1] for q in (hi, lo) for e in range(4)]
+        row_hot = (lax.broadcasted_iota(jnp.int32, (ROWS, width), 0) == row).astype(jnp.float32)
+        left = jnp.concatenate([(row_hot * part).astype(jnp.bfloat16) for part in parts], axis=0)
+        right = (lax.broadcasted_iota(jnp.int32, (2 * MY, width), 0) == col).astype(jnp.bfloat16)
+        part = lax.dot_general(
+            left, right, (((1,), (1,)), ((), ())), preferred_element_type=jnp.float32
+        )
+        o_ref[:, low : low + MY] += part[:, 0:MY]
+        o_ref[:, CY + low : CY + low + MY] += part[:, MY:]
+
+
+def deposit_crossing(first, second, acc):
+    block = first.shape[1]
+    return pl.pallas_call(
+        crossing_kernel,
+        grid=(1,),
+        in_specs=[
+            pl.BlockSpec((7, block), lambda b: (0, 0)),
+            pl.BlockSpec((7, block), lambda b: (0, 0)),
+            pl.BlockSpec(ACC_SHAPE, lambda b: (0, 0)),
+        ],
+        out_specs=pl.BlockSpec(ACC_SHAPE, lambda b: (0, 0)),
+        out_shape=jax.ShapeDtypeStruct(ACC_SHAPE, jnp.float32),
+        input_output_aliases={2: 0},
+    )(first, second, acc)
 
 
 def local_kernel(count_ref, p_ref, c_ref, o_ref):
@@ -234,7 +277,7 @@
     from_minus_y = towards(plus_y, 0, 1)
     from_plus_y = towards(minus_y, 0, -1)
     total = deposit_arrived(from_minus_x, from_plus_x, total, face)
-    total = deposit_arrived(from_minus_y, from_plus_y, total, face + 2 * corner)
+    total = deposit_crossing(from_minus_y, from_plus_y, total)
     total = total.reshape(SPLITS, 4, NZ // 2, CX, 2 * CY)
     summed = total[0, 0] + total[1, 0]
     density = jnp.stack([summed[..., :CY], summed[..., CY:]], axis=1).reshape(NZ, CX, CY)

time: 54.5 us -> 54.6 us (level)
    pallas_call x0 -> x1, Pallas kernels: none -> 4.08 us  [deposit_crossing(): pl.pallas_call(crossing_kernel, grid=(1,), in_specs=[pl.BlockSpec((7, blo...]
    pallas_call x2 -> x1, Pallas kernels: 7.38 us -> 3.33 us  [deposit_arrived(): pl.pallas_call(lambda x, y, a, o: arrived_kernel(block, x, y, a, o), grid...]
where the time goes in v4:
time: 54.6 us; the launch traced here: 54 us
  Pallas kernels  20.1 us (37%)
  starting transfers between devices  20.1 us (37%)
  waiting for transfers between devices  6.45 us (12%)
  local copies, waits for them, and re-layouts  4.6 us (8%)
  other arithmetic  1.99 us (4%)
  between operations  0.76 us (1%)
    ppermute x8, starting transfers between devices, towards(): return lax.ppermute(block, ('gx', 'gy'), route)  20.1 us
    pallas_call x1, Pallas kernels, deposit_local(): pl.pallas_call(local_kernel, grid_spec=pltpu.PrefetchScalarGridSpec(num_s...  7.12 us
    ppermute x8, waiting for transfers between devices, towards(): return lax.ppermute(block, ('gx', 'gy'), route)  6.45 us
    pallas_call x1, Pallas kernels, deposit_crossing(): pl.pallas_call(crossing_kernel, grid=(1,), in_specs=[pl.BlockSpec((7, blo...  4.08 us
    unnamed x22, local copies, waits for them, and re-layouts  3.78 us
    pallas_call x1, Pallas kernels, relax(): pl.pallas_call(relax_kernel, out_shape=jax.ShapeDtypeStruct((NZ, CX, CY),...  3.69 us
    pallas_call x1, Pallas kernels, deposit_arrived(): pl.pallas_call(lambda x, y, a, o: arrived_kernel(block, x, y, a, o), grid...  3.33 us
    pallas_call x1, Pallas kernels, pack(): pl.pallas_call(pack_kernel, in_specs=[pl.BlockSpec(memory_space=pltpu.SME...  1.85 us
  transfers between devices with their start and end apart: 8, of which 4 were waited for; matrix products, arithmetic and copies ran while one was open for 1% of the time, Pallas kernels for 19%

profile of v4, /device:TPU:0, one launch (start us, length us, event | category | flops | bytes accessed | tf_op | source)
XLA Modules:
  0.0 54.0 jit_solution(111260367077983450)
XLA Ops:
  0.6 1.9 %shard_map.50 = (f32[7,3456]{1,0:T(8,128)}, f32[7,3456]{1,0:T(8,128)}, f32[7,2176]{1,0:T(8,128)}, f32[7,2176]{1,0:T(8,128)}) custom-call(s32[1,9]{1,0:T(1,128)} %count_ref.3, f32[4,16384]{1,0:T(4,128)} %p_ref.3, s32[3,16384]{1,0:T(4,128)} %c_ref.3), custom_call_target="tpu_custom_call" | custom-call | tf_op jit(solution)/shard_map/pallas_call | solution.py:181
  2.5 6.3 %collective-permute-start.1 = (f32[7,3456]{1,0:T(8,128)}, f32[7,3456]{1,0:T(8,128)S(1)}, u32[]{:S(2)}, u32[]{:S(2)}) collective-permute-start(f32[7,3456]{1,0:T(8,128)} %get-tuple-element.8), channel_id=1, source_target_pairs={{0,120},{1,121},{2,122},{3,123},{4,124},{5,125},{6,126},{7,127},{8... | collective-permute-start | bytes 290312 | tf_op jit(solution)/shard_map/ppermute | solution.py:199
  8.8 2.6 %collective-permute-done.x = f32[7,3456]{1,0:T(8,128)S(1)} collective-permute-done((f32[7,3456]{1,0:T(8,128)}, f32[7,3456]{1,0:T(8,128)S(1)}, u32[]{:S(2)}, u32[]{:S(2)}) %collective-permute-start) | collective-permute-done | bytes 96800 | tf_op jit(solution)/shard_map/ppermute | solution.py:199
  11.5 0.5 copy-done.1
  12.0 0.1 copy-done.2
  12.1 0.8 %collective-permute-start.2 = (f32[7,3456]{1,0:T(8,128)S(1)}, f32[7,3456]{1,0:T(8,128)S(1)}, u32[]{:S(2)}, u32[]{:S(2)}) collective-permute-start(f32[7,3456]{1,0:T(8,128)S(1)} %pad_maximum_fusion.2), channel_id=1, source_target_pairs={{0,1},{1,2},{2,3},{3,4},{4,5},{5,6},{6,7},{7,0},{8,9},{9,10},{10,1... | collective-permute-start | bytes 290312 | tf_op jit(solution)/shard_map/ppermute | solution.py:199
  12.9 3.4 %collective-permute-start.3 = (f32[7,3456]{1,0:T(8,128)S(1)}, f32[7,3456]{1,0:T(8,128)S(1)}, u32[]{:S(2)}, u32[]{:S(2)}) collective-permute-start(f32[7,3456]{1,0:T(8,128)S(1)} %pad_maximum_fusion.3), channel_id=1, source_target_pairs={{0,7},{1,0},{2,1},{3,2},{4,3},{5,4},{6,5},{7,6},{8,15},{9,8},{10,9... | collective-permute-start | bytes 290312 | tf_op jit(solution)/shard_map/ppermute | solution.py:199
  16.3 7.1 %shard_map.51.a = f32[512,256]{1,0:T(8,128)} custom-call(s32[1,9]{1,0:T(1,128)} %count_ref.3, f32[4,16384]{1,0:T(4,128)} %p_ref.3, s32[3,16384]{1,0:T(4,128)} %c_ref.3), custom_call_target="tpu_custom_call" | custom-call | tf_op jit(solution)/shard_map/pallas_call | solution.py:126
  23.4 3.3 %shard_map.52.a_ref = f32[512,256]{1,0:T(8,128)} custom-call(f32[7,3456]{1,0:T(8,128)} %copy-done.1, f32[7,3456]{1,0:T(8,128)} %copy-done.2, f32[512,256]{1,0:T(8,128)} %shard_map.51.a), custom_call_target="tpu_custom_call", output_to_operand_aliasing={{}: (2, {})} | custom-call | tf_op jit(solution)/shard_map/pallas_call | solution.py:140
  26.8 0.6 %copy-done.7 = f32[7,3456]{1,0:T(8,128)} copy-done((f32[7,3456]{1,0:T(8,128)}, f32[7,3456]{1,0:T(8,128)S(1)}, u32[]{:S(2)}) %copy-start.7) | copy-done | bytes 96792
  27.4 0.6 %copy-done.8 = f32[7,3456]{1,0:T(8,128)} copy-done((f32[7,3456]{1,0:T(8,128)}, f32[7,3456]{1,0:T(8,128)S(1)}, u32[]{:S(2)}) %copy-start.8) | copy-done | bytes 96792
  28.1 4.1 %shard_map.53 = f32[512,256]{1,0:T(8,128)} custom-call(f32[7,3456]{1,0:T(8,128)} %copy-done.7, f32[7,3456]{1,0:T(8,128)} %copy-done.8, f32[512,256]{1,0:T(8,128)} %shard_map.52.a_ref), custom_call_target="tpu_custom_call", output_to_operand_aliasing={{}: (2, {})} | custom-call | tf_op jit(solution)/shard_map/pallas_call | solution.py:87
  32.1 0.9 %fusion.1 = f32[4,16,256]{2,1,0:T(8,128)S(1)} fusion(f32[2,4,4,16,256]{4,3,2,1,0:T(8,128)} %bitcast.17), kind=kLoop, calls=%fused_computation.9 | loop fusion | flops 16384 | bytes 196608 | tf_op jit(solution)/shard_map/add | solution.py:282
  33.0 1.1 %fusion = f32[3,4,16,256]{3,2,1,0:T(8,128)S(1)} fusion(f32[2,4,4,16,256]{4,3,2,1,0:T(8,128)} %bitcast.18), kind=kLoop, calls=%fused_computation.1 | loop fusion | flops 49152 | bytes 589824 | tf_op jit(solution)/shard_map/add | solution.py:285
  34.2 5.3 %collective-permute-start.4 = (f32[8,8,128]{2,1,0:T(8,128)S(1)}, f32[8,8,128]{2,1,0:T(8,128)S(1)}, u32[]{:S(2)}, u32[]{:S(2)}) collective-permute-start(f32[8,8,128]{2,1,0:T(8,128)S(1)} %get-tuple-element.19), channel_id=1, source_target_pairs={{0,120},{1,121},{2,122},{3,123},{4,124},{5,125},{6,126},{7,127},{8... | collective-permute-start | bytes 98312 | tf_op jit(solution)/shard_map/ppermute | solution.py:199
  39.6 1.6 %collective-permute-done.5.lx_ref = f32[8,8,128]{2,1,0:T(8,128)S(1)} collective-permute-done((f32[8,8,128]{2,1,0:T(8,128)S(1)}, f32[8,8,128]{2,1,0:T(8,128)S(1)}, u32[]{:S(2)}, u32[]{:S(2)}) %collective-permute-start.5) | collective-permute-done | bytes 32800 | tf_op jit(solution)/shard_map/ppermute | solution.py:199
  41.2 0.6 %copy-done.5 = f32[8,8,128]{2,1,0:T(8,128)} copy-done((f32[8,8,128]{2,1,0:T(8,128)}, f32[8,8,128]{2,1,0:T(8,128)S(1)}, u32[]{:S(2)}) %copy-start.5) | copy-done | bytes 32792
  41.8 0.1 fusion.2
  41.9 4.1 %collective-permute-start.6 = (f32[8,32,8]{2,1,0:T(8,128)S(1)}, f32[8,32,8]{2,1,0:T(8,128)S(1)}, u32[]{:S(2)}, u32[]{:S(2)}) collective-permute-start(f32[8,32,8]{2,1,0:T(8,128)S(1)} %get-tuple-element.13), channel_id=1, source_target_pairs={{0,7},{1,0},{2,1},{3,2},{4,3},{5,4},{6,5},{7,6},{8,15},{9,8},{10,9... | collective-permute-start | bytes 24584 | tf_op jit(solution)/shard_map/ppermute | solution.py:199
  46.1 0.7 %copy.8 = f32[3,4,2,16,128]{4,3,2,1,0:T(8,128)} copy(f32[3,4,2,16,128]{4,3,1,0,2:T(8,128)S(1)} %pad_maximum_fusion) | data formatting | bytes 393216 | tf_op jit(solution)/shard_map/stack | solution.py:286
  46.8 2.2 %collective-permute-done.7.ly_ref = f32[8,32,8]{2,1,0:T(8,128)S(1)} collective-permute-done((f32[8,32,8]{2,1,0:T(8,128)S(1)}, f32[8,32,8]{2,1,0:T(8,128)S(1)}, u32[]{:S(2)}, u32[]{:S(2)}) %collective-permute-start.7) | collective-permute-done | bytes 8224 | tf_op jit(solution)/shard_map/ppermute | solution.py:199
  49.0 0.6 %copy-done.3 = f32[8,32,8]{2,1,0:T(8,128)} copy-done((f32[8,32,8]{2,1,0:T(8,128)}, f32[8,32,8]{2,1,0:T(8,128)S(1)}, u32[]{:S(2)}) %copy-start.3) | copy-done | bytes 8216
  49.7 0.6 %copy-done.4 = f32[8,32,8]{2,1,0:T(8,128)} copy-done((f32[8,32,8]{2,1,0:T(8,128)}, f32[8,32,8]{2,1,0:T(8,128)S(1)}, u32[]{:S(2)}) %copy-start.4) | copy-done | bytes 8216
  50.3 3.7 %shard_map.54 = f32[8,16,128]{2,1,0:T(8,128)} custom-call(f32[8,16,128]{2,1,0:T(8,128)} %bitcast.21, f32[8,8,128]{2,1,0:T(8,128)} %copy-done.6, f32[8,8,128]{2,1,0:T(8,128)} %copy-done.5, f32[8,32,8]{2,1,0:T(8,128)} %copy-done.4, f32[8,32,8]{2,1,0:T(8,128)} %copy-done.3), custom_call_target="tpu_custom_call" | custom-call | tf_op jit(solution)/shard_map/pallas_call | solution.py:257
  (33 shorter events, 0.4 us)
Async XLA Ops:
  2.5 8.9 %collective-permute-start = (f32[7,3456]{1,0:T(8,128)}, f32[7,3456]{1,0:T(8,128)S(1)}, u32[]{:S(2)}, u32[]{:S(2)}) collective-permute-start(f32[7,3456]{1,0:T(8,128)} %get-tuple-element.7), channel_id=1, source_target_pairs={{0,8},{1,9},{2,10},{3,11},{4,12},{5,13},{6,14},{7,15},{8,16},{9,17... | collective-permute-start | bytes 290312 | tf_op jit(solution)/shard_map/ppermute | solution.py:199
  2.5 8.9 %copy-start.10 = (f32[7,2176]{1,0:T(8,128)S(1)}, f32[7,2176]{1,0:T(8,128)}, u32[]{:S(2)}) copy-start(f32[7,2176]{1,0:T(8,128)} %get-tuple-element.6) | copy-start | bytes 182788
  2.5 8.9 %collective-permute-start.1 = (f32[7,3456]{1,0:T(8,128)}, f32[7,3456]{1,0:T(8,128)S(1)}, u32[]{:S(2)}, u32[]{:S(2)}) collective-permute-start(f32[7,3456]{1,0:T(8,128)} %get-tuple-element.8), channel_id=1, source_target_pairs={{0,120},{1,121},{2,122},{3,123},{4,124},{5,125},{6,126},{7,127},{8... | collective-permute-start | bytes 290312 | tf_op jit(solution)/shard_map/ppermute | solution.py:199
  11.3 0.6 %copy-start.1 = (f32[7,3456]{1,0:T(8,128)}, f32[7,3456]{1,0:T(8,128)S(1)}, u32[]{:S(2)}) copy-start(f32[7,3456]{1,0:T(8,128)S(1)} %collective-permute-done.x) | copy-start | bytes 290308
  11.4 0.7 %copy-start.2 = (f32[7,3456]{1,0:T(8,128)}, f32[7,3456]{1,0:T(8,128)S(1)}, u32[]{:S(2)}) copy-start(f32[7,3456]{1,0:T(8,128)S(1)} %collective-permute-done.1.y) | copy-start | bytes 290308
  11.4 1.4 %copy-start.9 = (f32[7,2176]{1,0:T(8,128)S(1)}, f32[7,2176]{1,0:T(8,128)}, u32[]{:S(2)}) copy-start(f32[7,2176]{1,0:T(8,128)} %get-tuple-element.9) | copy-start | bytes 182788
  12.1 14.7 %collective-permute-start.2 = (f32[7,3456]{1,0:T(8,128)S(1)}, f32[7,3456]{1,0:T(8,128)S(1)}, u32[]{:S(2)}, u32[]{:S(2)}) collective-permute-start(f32[7,3456]{1,0:T(8,128)S(1)} %pad_maximum_fusion.2), channel_id=1, source_target_pairs={{0,1},{1,2},{2,3},{3,4},{4,5},{5,6},{6,7},{7,0},{8,9},{9,10},{10,1... | collective-permute-start | bytes 290312 | tf_op jit(solution)/shard_map/ppermute | solution.py:199
  12.9 13.9 %collective-permute-start.3 = (f32[7,3456]{1,0:T(8,128)S(1)}, f32[7,3456]{1,0:T(8,128)S(1)}, u32[]{:S(2)}, u32[]{:S(2)}) collective-permute-start(f32[7,3456]{1,0:T(8,128)S(1)} %pad_maximum_fusion.3), channel_id=1, source_target_pairs={{0,7},{1,0},{2,1},{3,2},{4,3},{5,4},{6,5},{7,6},{8,15},{9,8},{10,9... | collective-permute-start | bytes 290312 | tf_op jit(solution)/shard_map/ppermute | solution.py:199
  26.8 0.6 %copy-start.7 = (f32[7,3456]{1,0:T(8,128)}, f32[7,3456]{1,0:T(8,128)S(1)}, u32[]{:S(2)}) copy-start(f32[7,3456]{1,0:T(8,128)S(1)} %collective-permute-done.2.x_ref) | copy-start | bytes 290308
  27.4 0.7 %copy-start.8 = (f32[7,3456]{1,0:T(8,128)}, f32[7,3456]{1,0:T(8,128)S(1)}, u32[]{:S(2)}) copy-start(f32[7,3456]{1,0:T(8,128)S(1)} %collective-permute-done.3.y_ref) | copy-start | bytes 290308
  34.1 7.1 %copy-start = (f32[4,2,16,128]{3,2,1,0:T(8,128)}, f32[4,2,16,128]{3,2,1,0:T(8,128)S(1)}, u32[]{:S(2)}) copy-start(f32[4,2,16,128]{3,2,1,0:T(8,128)S(1)} %pad_maximum_fusion.4) | copy-start | bytes 196612
  34.1 7.0 %collective-permute-start.5 = (f32[8,8,128]{2,1,0:T(8,128)S(1)}, f32[8,8,128]{2,1,0:T(8,128)S(1)}, u32[]{:S(2)}, u32[]{:S(2)}) collective-permute-start(f32[8,8,128]{2,1,0:T(8,128)S(1)} %get-tuple-element.18), channel_id=1, source_target_pairs={{0,8},{1,9},{2,10},{3,11},{4,12},{5,13},{6,14},{7,15},{8,16},{9,17... | collective-permute-start | bytes 98312 | tf_op jit(solution)/shard_map/ppermute | solution.py:199
  34.2 6.9 %collective-permute-start.4 = (f32[8,8,128]{2,1,0:T(8,128)S(1)}, f32[8,8,128]{2,1,0:T(8,128)S(1)}, u32[]{:S(2)}, u32[]{:S(2)}) collective-permute-start(f32[8,8,128]{2,1,0:T(8,128)S(1)} %get-tuple-element.19), channel_id=1, source_target_pairs={{0,120},{1,121},{2,122},{3,123},{4,124},{5,125},{6,126},{7,127},{8... | collective-permute-start | bytes 98312 | tf_op jit(solution)/shard_map/ppermute | solution.py:199
  41.1 0.6 %copy-start.5 = (f32[8,8,128]{2,1,0:T(8,128)}, f32[8,8,128]{2,1,0:T(8,128)S(1)}, u32[]{:S(2)}) copy-start(f32[8,8,128]{2,1,0:T(8,128)S(1)} %collective-permute-done.5.lx_ref) | copy-start | bytes 98308
  41.2 0.6 %copy-start.6 = (f32[8,8,128]{2,1,0:T(8,128)}, f32[8,8,128]{2,1,0:T(8,128)S(1)}, u32[]{:S(2)}) copy-start(f32[8,8,128]{2,1,0:T(8,128)S(1)} %collective-permute-done.4.ux_ref) | copy-start | bytes 98308
  41.9 7.1 %collective-permute-start.7 = (f32[8,32,8]{2,1,0:T(8,128)S(1)}, f32[8,32,8]{2,1,0:T(8,128)S(1)}, u32[]{:S(2)}, u32[]{:S(2)}) collective-permute-start(f32[8,32,8]{2,1,0:T(8,128)S(1)} %get-tuple-element.12), channel_id=1, source_target_pairs={{0,1},{1,2},{2,3},{3,4},{4,5},{5,6},{6,7},{7,0},{8,9},{9,10},{10,1... | collective-permute-start | bytes 24584 | tf_op jit(solution)/shard_map/ppermute | solution.py:199
  41.9 7.1 %collective-permute-start.6 = (f32[8,32,8]{2,1,0:T(8,128)S(1)}, f32[8,32,8]{2,1,0:T(8,128)S(1)}, u32[]{:S(2)}, u32[]{:S(2)}) collective-permute-start(f32[8,32,8]{2,1,0:T(8,128)S(1)} %get-tuple-element.13), channel_id=1, source_target_pairs={{0,7},{1,0},{2,1},{3,2},{4,3},{5,4},{6,5},{7,6},{8,15},{9,8},{10,9... | collective-permute-start | bytes 24584 | tf_op jit(solution)/shard_map/ppermute | solution.py:199
  49.0 0.7 %copy-start.3 = (f32[8,32,8]{2,1,0:T(8,128)}, f32[8,32,8]{2,1,0:T(8,128)S(1)}, u32[]{:S(2)}) copy-start(f32[8,32,8]{2,1,0:T(8,128)S(1)} %collective-permute-done.7.ly_ref) | copy-start | bytes 24580
  49.7 0.6 %copy-start.4 = (f32[8,32,8]{2,1,0:T(8,128)}, f32[8,32,8]{2,1,0:T(8,128)S(1)}, u32[]{:S(2)}) copy-start(f32[8,32,8]{2,1,0:T(8,128)S(1)} %collective-permute-done.6.uy_ref) | copy-start | bytes 24580

commit v5 on v2

--- a/solution.py
+++ b/solution.py
@@ -194,9 +194,13 @@
         + lax.broadcasted_iota(jnp.int32, shape, 1)
         + lax.broadcasted_iota(jnp.int32, shape, 2)
     ) % 2
-    field = jnp.zeros(shape, jnp.float32)
-    for _ in range(SWEEPS):
+    residual = 0.0 - source
+    slope = -6.0 - SCREENING
+    field = jnp.where(parity == 0, 0.0 - residual / slope, 0.0)
+    for sweep_no in range(SWEEPS):
         for colour in (0, 1):
+            if sweep_no == 0 and colour == 0:
+                continue
             middle = field
             residual = (
                 near(middle)

time: 54.5 us -> 54.5 us (level)
  no operation moved by 1% of the time
where the time goes in v5:
time: 54.5 us; the launch traced here: 53.9 us
  starting transfers between devices  20.1 us (37%)
  Pallas kernels  20 us (37%)
  waiting for transfers between devices  6.45 us (12%)
  local copies, waits for them, and re-layouts  4.6 us (8%)
  other arithmetic  1.99 us (4%)
  between operations  0.76 us (1%)
    ppermute x8, starting transfers between devices, towards(): return lax.ppermute(block, ('gx', 'gy'), route)  20.1 us
    pallas_call x2, Pallas kernels, deposit_arrived(): pl.pallas_call(lambda x, y, a, o: arrived_kernel(block, x, y, a, o), grid...  7.38 us
    pallas_call x1, Pallas kernels, deposit_local(): pl.pallas_call(local_kernel, grid_spec=pltpu.PrefetchScalarGridSpec(num_s...  7.12 us
    ppermute x8, waiting for transfers between devices, towards(): return lax.ppermute(block, ('gx', 'gy'), route)  6.45 us
    unnamed x22, local copies, waits for them, and re-layouts  3.78 us
    pallas_call x1, Pallas kernels, relax(): pl.pallas_call(relax_kernel, out_shape=jax.ShapeDtypeStruct((NZ, CX, CY),...  3.65 us
    pallas_call x1, Pallas kernels, pack(): pl.pallas_call(pack_kernel, in_specs=[pl.BlockSpec(memory_space=pltpu.SME...  1.85 us
  transfers between devices with their start and end apart: 8, of which 4 were waited for; matrix products, arithmetic and copies ran while one was open for 1% of the time, Pallas kernels for 19%

profile of v5, /device:TPU:0, one launch (start us, length us, event | category | flops | bytes accessed | tf_op | source)
XLA Modules:
  0.0 53.9 jit_solution(11102677666902384384)
XLA Ops:
  0.6 1.9 %shard_map.50 = (f32[7,3456]{1,0:T(8,128)}, f32[7,3456]{1,0:T(8,128)}, f32[7,2176]{1,0:T(8,128)}, f32[7,2176]{1,0:T(8,128)}) custom-call(s32[1,9]{1,0:T(1,128)} %count_ref.3, f32[4,16384]{1,0:T(4,128)} %p_ref.3, s32[3,16384]{1,0:T(4,128)} %c_ref.3), custom_call_target="tpu_custom_call" | custom-call | tf_op jit(solution)/shard_map/pallas_call | solution.py:138
  2.5 6.3 %collective-permute-start.1 = (f32[7,3456]{1,0:T(8,128)}, f32[7,3456]{1,0:T(8,128)S(1)}, u32[]{:S(2)}, u32[]{:S(2)}) collective-permute-start(f32[7,3456]{1,0:T(8,128)} %get-tuple-element.8), channel_id=1, source_target_pairs={{0,120},{1,121},{2,122},{3,123},{4,124},{5,125},{6,126},{7,127},{8... | collective-permute-start | bytes 290312 | tf_op jit(solution)/shard_map/ppermute | solution.py:156
  8.8 2.6 %collective-permute-done.x = f32[7,3456]{1,0:T(8,128)S(1)} collective-permute-done((f32[7,3456]{1,0:T(8,128)}, f32[7,3456]{1,0:T(8,128)S(1)}, u32[]{:S(2)}, u32[]{:S(2)}) %collective-permute-start) | collective-permute-done | bytes 96800 | tf_op jit(solution)/shard_map/ppermute | solution.py:156
  11.5 0.5 copy-done.1
  12.0 0.1 copy-done.2
  12.1 0.8 %collective-permute-start.2 = (f32[7,3456]{1,0:T(8,128)S(1)}, f32[7,3456]{1,0:T(8,128)S(1)}, u32[]{:S(2)}, u32[]{:S(2)}) collective-permute-start(f32[7,3456]{1,0:T(8,128)S(1)} %pad_maximum_fusion.2), channel_id=1, source_target_pairs={{0,1},{1,2},{2,3},{3,4},{4,5},{5,6},{6,7},{7,0},{8,9},{9,10},{10,1... | collective-permute-start | bytes 290312 | tf_op jit(solution)/shard_map/ppermute | solution.py:156
  12.9 3.4 %collective-permute-start.3 = (f32[7,3456]{1,0:T(8,128)S(1)}, f32[7,3456]{1,0:T(8,128)S(1)}, u32[]{:S(2)}, u32[]{:S(2)}) collective-permute-start(f32[7,3456]{1,0:T(8,128)S(1)} %pad_maximum_fusion.3), channel_id=1, source_target_pairs={{0,7},{1,0},{2,1},{3,2},{4,3},{5,4},{6,5},{7,6},{8,15},{9,8},{10,9... | collective-permute-start | bytes 290312 | tf_op jit(solution)/shard_map/ppermute | solution.py:156
  16.3 7.1 %shard_map.51.a = f32[512,256]{1,0:T(8,128)} custom-call(s32[1,9]{1,0:T(1,128)} %count_ref.3, f32[4,16384]{1,0:T(4,128)} %p_ref.3, s32[3,16384]{1,0:T(4,128)} %c_ref.3), custom_call_target="tpu_custom_call" | custom-call | tf_op jit(solution)/shard_map/pallas_call | solution.py:83
  23.4 3.3 %shard_map.52.a = f32[512,256]{1,0:T(8,128)} custom-call(f32[7,3456]{1,0:T(8,128)} %copy-done.1, f32[7,3456]{1,0:T(8,128)} %copy-done.2, f32[512,256]{1,0:T(8,128)} %shard_map.51.a), custom_call_target="tpu_custom_call", output_to_operand_aliasing={{}: (2, {})} | custom-call | tf_op jit(solution)/shard_map/pallas_call | solution.py:97
  26.8 0.6 %copy-done.7 = f32[7,3456]{1,0:T(8,128)} copy-done((f32[7,3456]{1,0:T(8,128)}, f32[7,3456]{1,0:T(8,128)S(1)}, u32[]{:S(2)}) %copy-start.7) | copy-done | bytes 96792
  27.4 0.6 %copy-done.8 = f32[7,3456]{1,0:T(8,128)} copy-done((f32[7,3456]{1,0:T(8,128)}, f32[7,3456]{1,0:T(8,128)S(1)}, u32[]{:S(2)}) %copy-start.8) | copy-done | bytes 96792
  28.1 4.0 %shard_map.53 = f32[512,256]{1,0:T(8,128)} custom-call(f32[7,3456]{1,0:T(8,128)} %copy-done.7, f32[7,3456]{1,0:T(8,128)} %copy-done.8, f32[512,256]{1,0:T(8,128)} %shard_map.52.a), custom_call_target="tpu_custom_call", output_to_operand_aliasing={{}: (2, {})} | custom-call | tf_op jit(solution)/shard_map/pallas_call | solution.py:97
  32.1 0.9 %fusion.1 = f32[4,16,256]{2,1,0:T(8,128)S(1)} fusion(f32[2,4,4,16,256]{4,3,2,1,0:T(8,128)} %bitcast.17), kind=kLoop, calls=%fused_computation.9 | loop fusion | flops 16384 | bytes 196608 | tf_op jit(solution)/shard_map/add | solution.py:243
  33.0 1.1 %fusion = f32[3,4,16,256]{3,2,1,0:T(8,128)S(1)} fusion(f32[2,4,4,16,256]{4,3,2,1,0:T(8,128)} %bitcast.18), kind=kLoop, calls=%fused_computation.1 | loop fusion | flops 49152 | bytes 589824 | tf_op jit(solution)/shard_map/add | solution.py:246
  34.2 5.3 %collective-permute-start.4 = (f32[8,8,128]{2,1,0:T(8,128)S(1)}, f32[8,8,128]{2,1,0:T(8,128)S(1)}, u32[]{:S(2)}, u32[]{:S(2)}) collective-permute-start(f32[8,8,128]{2,1,0:T(8,128)S(1)} %get-tuple-element.19), channel_id=1, source_target_pairs={{0,120},{1,121},{2,122},{3,123},{4,124},{5,125},{6,126},{7,127},{8... | collective-permute-start | bytes 98312 | tf_op jit(solution)/shard_map/ppermute | solution.py:156
  39.5 1.6 %collective-permute-done.5.lx_ref = f32[8,8,128]{2,1,0:T(8,128)S(1)} collective-permute-done((f32[8,8,128]{2,1,0:T(8,128)S(1)}, f32[8,8,128]{2,1,0:T(8,128)S(1)}, u32[]{:S(2)}, u32[]{:S(2)}) %collective-permute-start.5) | collective-permute-done | bytes 32800 | tf_op jit(solution)/shard_map/ppermute | solution.py:156
  41.2 0.6 %copy-done.5 = f32[8,8,128]{2,1,0:T(8,128)} copy-done((f32[8,8,128]{2,1,0:T(8,128)}, f32[8,8,128]{2,1,0:T(8,128)S(1)}, u32[]{:S(2)}) %copy-start.5) | copy-done | bytes 32792
  41.7 0.1 fusion.2
  41.9 4.1 %collective-permute-start.6 = (f32[8,32,8]{2,1,0:T(8,128)S(1)}, f32[8,32,8]{2,1,0:T(8,128)S(1)}, u32[]{:S(2)}, u32[]{:S(2)}) collective-permute-start(f32[8,32,8]{2,1,0:T(8,128)S(1)} %get-tuple-element.13), channel_id=1, source_target_pairs={{0,7},{1,0},{2,1},{3,2},{4,3},{5,4},{6,5},{7,6},{8,15},{9,8},{10,9... | collective-permute-start | bytes 24584 | tf_op jit(solution)/shard_map/ppermute | solution.py:156
  46.0 0.7 %copy.8 = f32[3,4,2,16,128]{4,3,2,1,0:T(8,128)} copy(f32[3,4,2,16,128]{4,3,1,0,2:T(8,128)S(1)} %pad_maximum_fusion) | data formatting | bytes 393216 | tf_op jit(solution)/shard_map/stack | solution.py:247
  46.7 2.2 %collective-permute-done.7.ly_ref = f32[8,32,8]{2,1,0:T(8,128)S(1)} collective-permute-done((f32[8,32,8]{2,1,0:T(8,128)S(1)}, f32[8,32,8]{2,1,0:T(8,128)S(1)}, u32[]{:S(2)}, u32[]{:S(2)}) %collective-permute-start.7) | collective-permute-done | bytes 8224 | tf_op jit(solution)/shard_map/ppermute | solution.py:156
  49.0 0.6 %copy-done.3 = f32[8,32,8]{2,1,0:T(8,128)} copy-done((f32[8,32,8]{2,1,0:T(8,128)}, f32[8,32,8]{2,1,0:T(8,128)S(1)}, u32[]{:S(2)}) %copy-start.3) | copy-done | bytes 8216
  49.6 0.6 %copy-done.4 = f32[8,32,8]{2,1,0:T(8,128)} copy-done((f32[8,32,8]{2,1,0:T(8,128)}, f32[8,32,8]{2,1,0:T(8,128)S(1)}, u32[]{:S(2)}) %copy-start.4) | copy-done | bytes 8216
  50.3 3.6 %shard_map.54 = f32[8,16,128]{2,1,0:T(8,128)} custom-call(f32[8,16,128]{2,1,0:T(8,128)} %bitcast.21, f32[8,8,128]{2,1,0:T(8,128)} %copy-done.6, f32[8,8,128]{2,1,0:T(8,128)} %copy-done.5, f32[8,32,8]{2,1,0:T(8,128)} %copy-done.4, f32[8,32,8]{2,1,0:T(8,128)} %copy-done.3), custom_call_target="tpu_custom_call" | custom-call | tf_op jit(solution)/shard_map/pallas_call | solution.py:218
  (33 shorter events, 0.4 us)
Async XLA Ops:
  2.5 8.9 %collective-permute-start = (f32[7,3456]{1,0:T(8,128)}, f32[7,3456]{1,0:T(8,128)S(1)}, u32[]{:S(2)}, u32[]{:S(2)}) collective-permute-start(f32[7,3456]{1,0:T(8,128)} %get-tuple-element.7), channel_id=1, source_target_pairs={{0,8},{1,9},{2,10},{3,11},{4,12},{5,13},{6,14},{7,15},{8,16},{9,17... | collective-permute-start | bytes 290312 | tf_op jit(solution)/shard_map/ppermute | solution.py:156
  2.5 8.9 %copy-start.10 = (f32[7,2176]{1,0:T(8,128)S(1)}, f32[7,2176]{1,0:T(8,128)}, u32[]{:S(2)}) copy-start(f32[7,2176]{1,0:T(8,128)} %get-tuple-element.6) | copy-start | bytes 182788
  2.5 8.9 %collective-permute-start.1 = (f32[7,3456]{1,0:T(8,128)}, f32[7,3456]{1,0:T(8,128)S(1)}, u32[]{:S(2)}, u32[]{:S(2)}) collective-permute-start(f32[7,3456]{1,0:T(8,128)} %get-tuple-element.8), channel_id=1, source_target_pairs={{0,120},{1,121},{2,122},{3,123},{4,124},{5,125},{6,126},{7,127},{8... | collective-permute-start | bytes 290312 | tf_op jit(solution)/shard_map/ppermute | solution.py:156
  11.3 0.6 %copy-start.1 = (f32[7,3456]{1,0:T(8,128)}, f32[7,3456]{1,0:T(8,128)S(1)}, u32[]{:S(2)}) copy-start(f32[7,3456]{1,0:T(8,128)S(1)} %collective-permute-done.x) | copy-start | bytes 290308
  11.4 0.7 %copy-start.2 = (f32[7,3456]{1,0:T(8,128)}, f32[7,3456]{1,0:T(8,128)S(1)}, u32[]{:S(2)}) copy-start(f32[7,3456]{1,0:T(8,128)S(1)} %collective-permute-done.1.y) | copy-start | bytes 290308
  11.4 1.4 %copy-start.9 = (f32[7,2176]{1,0:T(8,128)S(1)}, f32[7,2176]{1,0:T(8,128)}, u32[]{:S(2)}) copy-start(f32[7,2176]{1,0:T(8,128)} %get-tuple-element.9) | copy-start | bytes 182788
  12.1 14.7 %collective-permute-start.2 = (f32[7,3456]{1,0:T(8,128)S(1)}, f32[7,3456]{1,0:T(8,128)S(1)}, u32[]{:S(2)}, u32[]{:S(2)}) collective-permute-start(f32[7,3456]{1,0:T(8,128)S(1)} %pad_maximum_fusion.2), channel_id=1, source_target_pairs={{0,1},{1,2},{2,3},{3,4},{4,5},{5,6},{6,7},{7,0},{8,9},{9,10},{10,1... | collective-permute-start | bytes 290312 | tf_op jit(solution)/shard_map/ppermute | solution.py:156
  12.9 13.9 %collective-permute-start.3 = (f32[7,3456]{1,0:T(8,128)S(1)}, f32[7,3456]{1,0:T(8,128)S(1)}, u32[]{:S(2)}, u32[]{:S(2)}) collective-permute-start(f32[7,3456]{1,0:T(8,128)S(1)} %pad_maximum_fusion.3), channel_id=1, source_target_pairs={{0,7},{1,0},{2,1},{3,2},{4,3},{5,4},{6,5},{7,6},{8,15},{9,8},{10,9... | collective-permute-start | bytes 290312 | tf_op jit(solution)/shard_map/ppermute | solution.py:156
  26.8 0.6 %copy-start.7 = (f32[7,3456]{1,0:T(8,128)}, f32[7,3456]{1,0:T(8,128)S(1)}, u32[]{:S(2)}) copy-start(f32[7,3456]{1,0:T(8,128)S(1)} %collective-permute-done.2.x) | copy-start | bytes 290308
  27.4 0.7 %copy-start.8 = (f32[7,3456]{1,0:T(8,128)}, f32[7,3456]{1,0:T(8,128)S(1)}, u32[]{:S(2)}) copy-start(f32[7,3456]{1,0:T(8,128)S(1)} %collective-permute-done.3.y) | copy-start | bytes 290308
  34.1 7.1 %copy-start = (f32[4,2,16,128]{3,2,1,0:T(8,128)}, f32[4,2,16,128]{3,2,1,0:T(8,128)S(1)}, u32[]{:S(2)}) copy-start(f32[4,2,16,128]{3,2,1,0:T(8,128)S(1)} %pad_maximum_fusion.4) | copy-start | bytes 196612
  34.1 7.0 %collective-permute-start.5 = (f32[8,8,128]{2,1,0:T(8,128)S(1)}, f32[8,8,128]{2,1,0:T(8,128)S(1)}, u32[]{:S(2)}, u32[]{:S(2)}) collective-permute-start(f32[8,8,128]{2,1,0:T(8,128)S(1)} %get-tuple-element.18), channel_id=1, source_target_pairs={{0,8},{1,9},{2,10},{3,11},{4,12},{5,13},{6,14},{7,15},{8,16},{9,17... | collective-permute-start | bytes 98312 | tf_op jit(solution)/shard_map/ppermute | solution.py:156
  34.2 6.9 %collective-permute-start.4 = (f32[8,8,128]{2,1,0:T(8,128)S(1)}, f32[8,8,128]{2,1,0:T(8,128)S(1)}, u32[]{:S(2)}, u32[]{:S(2)}) collective-permute-start(f32[8,8,128]{2,1,0:T(8,128)S(1)} %get-tuple-element.19), channel_id=1, source_target_pairs={{0,120},{1,121},{2,122},{3,123},{4,124},{5,125},{6,126},{7,127},{8... | collective-permute-start | bytes 98312 | tf_op jit(solution)/shard_map/ppermute | solution.py:156
  41.1 0.6 %copy-start.5 = (f32[8,8,128]{2,1,0:T(8,128)}, f32[8,8,128]{2,1,0:T(8,128)S(1)}, u32[]{:S(2)}) copy-start(f32[8,8,128]{2,1,0:T(8,128)S(1)} %collective-permute-done.5.lx_ref) | copy-start | bytes 98308
  41.1 0.6 %copy-start.6 = (f32[8,8,128]{2,1,0:T(8,128)}, f32[8,8,128]{2,1,0:T(8,128)S(1)}, u32[]{:S(2)}) copy-start(f32[8,8,128]{2,1,0:T(8,128)S(1)} %collective-permute-done.4.ux_ref) | copy-start | bytes 98308
  41.8 7.1 %collective-permute-start.7 = (f32[8,32,8]{2,1,0:T(8,128)S(1)}, f32[8,32,8]{2,1,0:T(8,128)S(1)}, u32[]{:S(2)}, u32[]{:S(2)}) collective-permute-start(f32[8,32,8]{2,1,0:T(8,128)S(1)} %get-tuple-element.12), channel_id=1, source_target_pairs={{0,1},{1,2},{2,3},{3,4},{4,5},{5,6},{6,7},{7,0},{8,9},{9,10},{10,1... | collective-permute-start | bytes 24584 | tf_op jit(solution)/shard_map/ppermute | solution.py:156
  41.9 7.1 %collective-permute-start.6 = (f32[8,32,8]{2,1,0:T(8,128)S(1)}, f32[8,32,8]{2,1,0:T(8,128)S(1)}, u32[]{:S(2)}, u32[]{:S(2)}) collective-permute-start(f32[8,32,8]{2,1,0:T(8,128)S(1)} %get-tuple-element.13), channel_id=1, source_target_pairs={{0,7},{1,0},{2,1},{3,2},{4,3},{5,4},{6,5},{7,6},{8,15},{9,8},{10,9... | collective-permute-start | bytes 24584 | tf_op jit(solution)/shard_map/ppermute | solution.py:156
  49.0 0.7 %copy-start.3 = (f32[8,32,8]{2,1,0:T(8,128)}, f32[8,32,8]{2,1,0:T(8,128)S(1)}, u32[]{:S(2)}) copy-start(f32[8,32,8]{2,1,0:T(8,128)S(1)} %collective-permute-done.7.ly_ref) | copy-start | bytes 24580
  49.6 0.6 %copy-start.4 = (f32[8,32,8]{2,1,0:T(8,128)}, f32[8,32,8]{2,1,0:T(8,128)S(1)}, u32[]{:S(2)}) copy-start(f32[8,32,8]{2,1,0:T(8,128)S(1)} %collective-permute-done.6.uy_ref) | copy-start | bytes 24580

commit v6 on v5

--- a/solution.py
+++ b/solution.py
@@ -9,6 +9,7 @@
 CY = 128
 NZ = 8
 SWEEPS = 4
+PART = 16384
 CAP_F = 2048
 CAP_D = 512
 
@@ -55,13 +56,17 @@
     )
 
 
-def local_kernel(count_ref, p_ref, c_ref, o_ref):
-    step = pl.program_id(0)
+def local_kernel(offset, count_ref, p_ref, c_ref, *rest):
+    o_ref = rest[-1]
+    step = pl.program_id(0) + offset
     first = local_start(count_ref)
 
-    @pl.when(step == 0)
+    @pl.when(pl.program_id(0) == 0)
     def _():
-        o_ref[...] = jnp.zeros(o_ref.shape, o_ref.dtype)
+        if len(rest) == 1:
+            o_ref[...] = jnp.zeros(o_ref.shape, o_ref.dtype)
+        else:
+            o_ref[...] = rest[0][...]
 
     @pl.when(step * BLOCK + BLOCK > first)
     def _():
@@ -78,19 +83,27 @@
 ACC_SHAPE = (4 * SPLITS * ROWS, COLS)
 
 
-def deposit_local(payload, cells, counts):
-    pick = lambda b, f: (0, jnp.maximum(b, local_start(f) // BLOCK))
-    return pl.pallas_call(
-        local_kernel,
+def deposit_local(payload, cells, counts, offset, count, acc=None):
+    pick = lambda b, f: (0, jnp.maximum(b + offset, local_start(f) // BLOCK))
+    in_specs = [pl.BlockSpec((4, BLOCK), pick), pl.BlockSpec((3, BLOCK), pick)]
+    operands = [counts, payload, cells]
+    aliases = {}
+    if acc is not None:
+        in_specs.append(pl.BlockSpec(ACC_SHAPE, lambda b, f: (0, 0)))
+        operands.append(acc)
+        aliases = {3: 0}
+    return pl.pallas_call(
+        lambda *refs: local_kernel(offset, *refs),
         grid_spec=pltpu.PrefetchScalarGridSpec(
             num_scalar_prefetch=1,
-            grid=(payload.shape[1] // BLOCK,),
-            in_specs=[pl.BlockSpec((4, BLOCK), pick), pl.BlockSpec((3, BLOCK), pick)],
+            grid=(count,),
+            in_specs=in_specs,
             out_specs=pl.BlockSpec(ACC_SHAPE, lambda b, f: (0, 0)),
         ),
         out_shape=jax.ShapeDtypeStruct(ACC_SHAPE, jnp.float32),
+        input_output_aliases=aliases,
         compiler_params=pltpu.CompilerParams(dimension_semantics=("arbitrary",)),
-    )(counts, payload, cells)
+    )(*operands)
 
 
 def deposit_arrived(first, second, acc, block):
@@ -228,7 +241,8 @@
     plus_x, minus_x, plus_y, minus_y = pack(payload, cells, counts)
     from_minus_x = towards(plus_x, 1, 0)
     from_plus_x = towards(minus_x, -1, 0)
-    total = deposit_local(payload, cells, counts)
+    half = PART // BLOCK // 2
+    total = deposit_local(payload, cells, counts, 0, half)
     plus_y = jnp.concatenate(
         [plus_y, from_minus_x[:, face : face + corner], from_plus_x[:, face : face + corner]], axis=1
     )
@@ -237,6 +251,7 @@
     )
     from_minus_y = towards(plus_y, 0, 1)
     from_plus_y = towards(minus_y, 0, -1)
+    total = deposit_local(payload, cells, counts, half, half, total)
     total = deposit_arrived(from_minus_x, from_plus_x, total, face)
     total = deposit_arrived(from_minus_y, from_plus_y, total, face + 2 * corner)
     total = total.reshape(SPLITS, 4, NZ // 2, CX, 2 * CY)

time: 54.5 us -> 57 us (1.046)
  Pallas kernels: 20 us -> 22.6 us
    pallas_call x1 -> x2, Pallas kernels: 7.12 us -> 9.7 us  [deposit_local(): pl.pallas_call(lambda *refs: local_kernel(offset, *refs), grid_spec=pltpu...]
  transfers between devices with their start and end apart: 8 -> 8, of which waited for: 4 -> 4; matrix products, arithmetic and copies ran while one was open for 1% -> 1% of each run, Pallas kernels for 19% -> 23%
where the time goes in v6:
time: 57 us; the launch traced here: 56.5 us
  Pallas kernels  22.6 us (40%)
  starting transfers between devices  20.1 us (35%)
  waiting for transfers between devices  6.45 us (11%)
  local copies, waits for them, and re-layouts  4.6 us (8%)
  other arithmetic  1.99 us (3%)
  between operations  0.76 us (1%)
    ppermute x8, starting transfers between devices, towards(): return lax.ppermute(block, ('gx', 'gy'), route)  20.1 us
    pallas_call x2, Pallas kernels, deposit_local(): pl.pallas_call(lambda *refs: local_kernel(offset, *refs), grid_spec=pltpu...  9.7 us
    pallas_call x2, Pallas kernels, deposit_arrived(): pl.pallas_call(lambda x, y, a, o: arrived_kernel(block, x, y, a, o), grid...  7.38 us
    ppermute x8, waiting for transfers between devices, towards(): return lax.ppermute(block, ('gx', 'gy'), route)  6.45 us
    unnamed x22, local copies, waits for them, and re-layouts  3.78 us
    pallas_call x1, Pallas kernels, relax(): pl.pallas_call(relax_kernel, out_shape=jax.ShapeDtypeStruct((NZ, CX, CY),...  3.65 us
    pallas_call x1, Pallas kernels, pack(): pl.pallas_call(pack_kernel, in_specs=[pl.BlockSpec(memory_space=pltpu.SME...  1.85 us
  transfers between devices with their start and end apart: 8, of which 4 were waited for; matrix products, arithmetic and copies ran while one was open for 1% of the time, Pallas kernels for 23%

profile of v6, /device:TPU:0, one launch (start us, length us, event | category | flops | bytes accessed | tf_op | source)
XLA Modules:
  0.0 56.5 jit_solution(13654255922241589102)
XLA Ops:
  0.6 1.9 %shard_map.50 = (f32[7,3456]{1,0:T(8,128)}, f32[7,3456]{1,0:T(8,128)}, f32[7,2176]{1,0:T(8,128)}, f32[7,2176]{1,0:T(8,128)}) custom-call(s32[1,9]{1,0:T(1,128)} %refs_0_.3, f32[4,16384]{1,0:T(4,128)} %refs_1_.3, s32[3,16384]{1,0:T(4,128)} %refs_2_.3), custom_call_target="tpu_custom_call" | custom-call | tf_op jit(solution)/shard_map/pallas_call | solution.py:151
  2.5 6.3 %collective-permute-start.1 = (f32[7,3456]{1,0:T(8,128)}, f32[7,3456]{1,0:T(8,128)S(1)}, u32[]{:S(2)}, u32[]{:S(2)}) collective-permute-start(f32[7,3456]{1,0:T(8,128)} %get-tuple-element.8), channel_id=1, source_target_pairs={{0,120},{1,121},{2,122},{3,123},{4,124},{5,125},{6,126},{7,127},{8... | collective-permute-start | bytes 290312 | tf_op jit(solution)/shard_map/ppermute | solution.py:169
  8.8 2.6 %collective-permute-done.x = f32[7,3456]{1,0:T(8,128)S(1)} collective-permute-done((f32[7,3456]{1,0:T(8,128)}, f32[7,3456]{1,0:T(8,128)S(1)}, u32[]{:S(2)}, u32[]{:S(2)}) %collective-permute-start) | collective-permute-done | bytes 96800 | tf_op jit(solution)/shard_map/ppermute | solution.py:169
  11.5 0.5 copy-done.1
  12.1 0.8 %collective-permute-start.2 = (f32[7,3456]{1,0:T(8,128)S(1)}, f32[7,3456]{1,0:T(8,128)S(1)}, u32[]{:S(2)}, u32[]{:S(2)}) collective-permute-start(f32[7,3456]{1,0:T(8,128)S(1)} %pad_maximum_fusion.2), channel_id=1, source_target_pairs={{0,1},{1,2},{2,3},{3,4},{4,5},{5,6},{6,7},{7,0},{8,9},{9,10},{10,1... | collective-permute-start | bytes 290312 | tf_op jit(solution)/shard_map/ppermute | solution.py:169
  12.9 3.4 %collective-permute-start.3 = (f32[7,3456]{1,0:T(8,128)S(1)}, f32[7,3456]{1,0:T(8,128)S(1)}, u32[]{:S(2)}, u32[]{:S(2)}) collective-permute-start(f32[7,3456]{1,0:T(8,128)S(1)} %pad_maximum_fusion.3), channel_id=1, source_target_pairs={{0,7},{1,0},{2,1},{3,2},{4,3},{5,4},{6,5},{7,6},{8,15},{9,8},{10,9... | collective-permute-start | bytes 290312 | tf_op jit(solution)/shard_map/ppermute | solution.py:169
  16.3 3.9 %shard_map.51.refs_3_ = f32[512,256]{1,0:T(8,128)} custom-call(s32[1,9]{1,0:T(1,128)} %refs_0_.3, f32[4,16384]{1,0:T(4,128)} %refs_1_.3, s32[3,16384]{1,0:T(4,128)} %refs_2_.3), custom_call_target="tpu_custom_call" | custom-call | tf_op jit(solution)/shard_map/pallas_call | solution.py:95
  20.2 5.8 %shard_map.52.a = f32[512,256]{1,0:T(8,128)} custom-call(s32[1,9]{1,0:T(1,128)} %refs_0_.3, f32[4,16384]{1,0:T(4,128)} %refs_1_.3, s32[3,16384]{1,0:T(4,128)} %refs_2_.3, f32[512,256]{1,0:T(8,128)} %shard_map.51.refs_3_), custom_call_target="tpu_custom_call", output_to_operand_aliasing={{}: (3, {})} | custom-call | tf_op jit(solution)/shard_map/pallas_call | solution.py:95
  26.0 3.3 %shard_map.53.a = f32[512,256]{1,0:T(8,128)} custom-call(f32[7,3456]{1,0:T(8,128)} %copy-done.1, f32[7,3456]{1,0:T(8,128)} %copy-done.2, f32[512,256]{1,0:T(8,128)} %shard_map.52.a), custom_call_target="tpu_custom_call", output_to_operand_aliasing={{}: (2, {})} | custom-call | tf_op jit(solution)/shard_map/pallas_call | solution.py:110
  29.3 0.6 %copy-done.7 = f32[7,3456]{1,0:T(8,128)} copy-done((f32[7,3456]{1,0:T(8,128)}, f32[7,3456]{1,0:T(8,128)S(1)}, u32[]{:S(2)}) %copy-start.7) | copy-done | bytes 96792
  30.0 0.6 %copy-done.8 = f32[7,3456]{1,0:T(8,128)} copy-done((f32[7,3456]{1,0:T(8,128)}, f32[7,3456]{1,0:T(8,128)S(1)}, u32[]{:S(2)}) %copy-start.8) | copy-done | bytes 96792
  30.6 4.0 %shard_map.54 = f32[512,256]{1,0:T(8,128)} custom-call(f32[7,3456]{1,0:T(8,128)} %copy-done.7, f32[7,3456]{1,0:T(8,128)} %copy-done.8, f32[512,256]{1,0:T(8,128)} %shard_map.53.a), custom_call_target="tpu_custom_call", output_to_operand_aliasing={{}: (2, {})} | custom-call | tf_op jit(solution)/shard_map/pallas_call | solution.py:110
  34.7 0.9 %fusion.1 = f32[4,16,256]{2,1,0:T(8,128)S(1)} fusion(f32[2,4,4,16,256]{4,3,2,1,0:T(8,128)} %bitcast.17), kind=kLoop, calls=%fused_computation.9 | loop fusion | flops 16384 | bytes 196608 | tf_op jit(solution)/shard_map/add | solution.py:258
  35.6 1.1 %fusion = f32[3,4,16,256]{3,2,1,0:T(8,128)S(1)} fusion(f32[2,4,4,16,256]{4,3,2,1,0:T(8,128)} %bitcast.18), kind=kLoop, calls=%fused_computation.1 | loop fusion | flops 49152 | bytes 589824 | tf_op jit(solution)/shard_map/add | solution.py:261
  36.7 5.3 %collective-permute-start.4 = (f32[8,8,128]{2,1,0:T(8,128)S(1)}, f32[8,8,128]{2,1,0:T(8,128)S(1)}, u32[]{:S(2)}, u32[]{:S(2)}) collective-permute-start(f32[8,8,128]{2,1,0:T(8,128)S(1)} %get-tuple-element.19), channel_id=1, source_target_pairs={{0,120},{1,121},{2,122},{3,123},{4,124},{5,125},{6,126},{7,127},{8... | collective-permute-start | bytes 98312 | tf_op jit(solution)/shard_map/ppermute | solution.py:169
  42.1 1.6 %collective-permute-done.5.lx_ref = f32[8,8,128]{2,1,0:T(8,128)S(1)} collective-permute-done((f32[8,8,128]{2,1,0:T(8,128)S(1)}, f32[8,8,128]{2,1,0:T(8,128)S(1)}, u32[]{:S(2)}, u32[]{:S(2)}) %collective-permute-start.5) | collective-permute-done | bytes 32800 | tf_op jit(solution)/shard_map/ppermute | solution.py:169
  43.7 0.6 copy-done.5
  44.3 0.1 fusion.2
  44.5 4.1 %collective-permute-start.6 = (f32[8,32,8]{2,1,0:T(8,128)S(1)}, f32[8,32,8]{2,1,0:T(8,128)S(1)}, u32[]{:S(2)}, u32[]{:S(2)}) collective-permute-start(f32[8,32,8]{2,1,0:T(8,128)S(1)} %get-tuple-element.13), channel_id=1, source_target_pairs={{0,7},{1,0},{2,1},{3,2},{4,3},{5,4},{6,5},{7,6},{8,15},{9,8},{10,9... | collective-permute-start | bytes 24584 | tf_op jit(solution)/shard_map/ppermute | solution.py:169
  48.6 0.7 %copy.9 = f32[3,4,2,16,128]{4,3,2,1,0:T(8,128)} copy(f32[3,4,2,16,128]{4,3,1,0,2:T(8,128)S(1)} %pad_maximum_fusion) | data formatting | bytes 393216 | tf_op jit(solution)/shard_map/stack | solution.py:262
  49.3 2.2 %collective-permute-done.7.ly_ref = f32[8,32,8]{2,1,0:T(8,128)S(1)} collective-permute-done((f32[8,32,8]{2,1,0:T(8,128)S(1)}, f32[8,32,8]{2,1,0:T(8,128)S(1)}, u32[]{:S(2)}, u32[]{:S(2)}) %collective-permute-start.7) | collective-permute-done | bytes 8224 | tf_op jit(solution)/shard_map/ppermute | solution.py:169
  51.6 0.6 %copy-done.3 = f32[8,32,8]{2,1,0:T(8,128)} copy-done((f32[8,32,8]{2,1,0:T(8,128)}, f32[8,32,8]{2,1,0:T(8,128)S(1)}, u32[]{:S(2)}) %copy-start.3) | copy-done | bytes 8216
  52.2 0.6 %copy-done.4 = f32[8,32,8]{2,1,0:T(8,128)} copy-done((f32[8,32,8]{2,1,0:T(8,128)}, f32[8,32,8]{2,1,0:T(8,128)S(1)}, u32[]{:S(2)}) %copy-start.4) | copy-done | bytes 8216
  52.8 3.6 %shard_map.55 = f32[8,16,128]{2,1,0:T(8,128)} custom-call(f32[8,16,128]{2,1,0:T(8,128)} %bitcast.21, f32[8,8,128]{2,1,0:T(8,128)} %copy-done.6, f32[8,8,128]{2,1,0:T(8,128)} %copy-done.5, f32[8,32,8]{2,1,0:T(8,128)} %copy-done.4, f32[8,32,8]{2,1,0:T(8,128)} %copy-done.3), custom_call_target="tpu_custom_call" | custom-call | tf_op jit(solution)/shard_map/pallas_call | solution.py:231
  (34 shorter events, 0.5 us)
Async XLA Ops:
  2.5 8.9 %collective-permute-start = (f32[7,3456]{1,0:T(8,128)}, f32[7,3456]{1,0:T(8,128)S(1)}, u32[]{:S(2)}, u32[]{:S(2)}) collective-permute-start(f32[7,3456]{1,0:T(8,128)} %get-tuple-element.7), channel_id=1, source_target_pairs={{0,8},{1,9},{2,10},{3,11},{4,12},{5,13},{6,14},{7,15},{8,16},{9,17... | collective-permute-start | bytes 290312 | tf_op jit(solution)/shard_map/ppermute | solution.py:169
  2.5 8.9 %copy-start.10 = (f32[7,2176]{1,0:T(8,128)S(1)}, f32[7,2176]{1,0:T(8,128)}, u32[]{:S(2)}) copy-start(f32[7,2176]{1,0:T(8,128)} %get-tuple-element.6) | copy-start | bytes 182788
  2.5 8.9 %collective-permute-start.1 = (f32[7,3456]{1,0:T(8,128)}, f32[7,3456]{1,0:T(8,128)S(1)}, u32[]{:S(2)}, u32[]{:S(2)}) collective-permute-start(f32[7,3456]{1,0:T(8,128)} %get-tuple-element.8), channel_id=1, source_target_pairs={{0,120},{1,121},{2,122},{3,123},{4,124},{5,125},{6,126},{7,127},{8... | collective-permute-start | bytes 290312 | tf_op jit(solution)/shard_map/ppermute | solution.py:169
  11.3 0.6 %copy-start.1 = (f32[7,3456]{1,0:T(8,128)}, f32[7,3456]{1,0:T(8,128)S(1)}, u32[]{:S(2)}) copy-start(f32[7,3456]{1,0:T(8,128)S(1)} %collective-permute-done.x) | copy-start | bytes 290308
  11.4 0.7 %copy-start.2 = (f32[7,3456]{1,0:T(8,128)}, f32[7,3456]{1,0:T(8,128)S(1)}, u32[]{:S(2)}) copy-start(f32[7,3456]{1,0:T(8,128)S(1)} %collective-permute-done.1.y) | copy-start | bytes 290308
  11.4 1.4 %copy-start.9 = (f32[7,2176]{1,0:T(8,128)S(1)}, f32[7,2176]{1,0:T(8,128)}, u32[]{:S(2)}) copy-start(f32[7,2176]{1,0:T(8,128)} %get-tuple-element.9) | copy-start | bytes 182788
  12.1 17.3 %collective-permute-start.2 = (f32[7,3456]{1,0:T(8,128)S(1)}, f32[7,3456]{1,0:T(8,128)S(1)}, u32[]{:S(2)}, u32[]{:S(2)}) collective-permute-start(f32[7,3456]{1,0:T(8,128)S(1)} %pad_maximum_fusion.2), channel_id=1, source_target_pairs={{0,1},{1,2},{2,3},{3,4},{4,5},{5,6},{6,7},{7,0},{8,9},{9,10},{10,1... | collective-permute-start | bytes 290312 | tf_op jit(solution)/shard_map/ppermute | solution.py:169
  12.9 16.5 %collective-permute-start.3 = (f32[7,3456]{1,0:T(8,128)S(1)}, f32[7,3456]{1,0:T(8,128)S(1)}, u32[]{:S(2)}, u32[]{:S(2)}) collective-permute-start(f32[7,3456]{1,0:T(8,128)S(1)} %pad_maximum_fusion.3), channel_id=1, source_target_pairs={{0,7},{1,0},{2,1},{3,2},{4,3},{5,4},{6,5},{7,6},{8,15},{9,8},{10,9... | collective-permute-start | bytes 290312 | tf_op jit(solution)/shard_map/ppermute | solution.py:169
  29.3 0.6 %copy-start.7 = (f32[7,3456]{1,0:T(8,128)}, f32[7,3456]{1,0:T(8,128)S(1)}, u32[]{:S(2)}) copy-start(f32[7,3456]{1,0:T(8,128)S(1)} %collective-permute-done.2.x) | copy-start | bytes 290308
  30.0 0.7 %copy-start.8 = (f32[7,3456]{1,0:T(8,128)}, f32[7,3456]{1,0:T(8,128)S(1)}, u32[]{:S(2)}) copy-start(f32[7,3456]{1,0:T(8,128)S(1)} %collective-permute-done.3.y) | copy-start | bytes 290308
  36.6 7.1 %copy-start = (f32[4,2,16,128]{3,2,1,0:T(8,128)}, f32[4,2,16,128]{3,2,1,0:T(8,128)S(1)}, u32[]{:S(2)}) copy-start(f32[4,2,16,128]{3,2,1,0:T(8,128)S(1)} %pad_maximum_fusion.4) | copy-start | bytes 196612
  36.7 7.0 %collective-permute-start.5 = (f32[8,8,128]{2,1,0:T(8,128)S(1)}, f32[8,8,128]{2,1,0:T(8,128)S(1)}, u32[]{:S(2)}, u32[]{:S(2)}) collective-permute-start(f32[8,8,128]{2,1,0:T(8,128)S(1)} %get-tuple-element.18), channel_id=1, source_target_pairs={{0,8},{1,9},{2,10},{3,11},{4,12},{5,13},{6,14},{7,15},{8,16},{9,17... | collective-permute-start | bytes 98312 | tf_op jit(solution)/shard_map/ppermute | solution.py:169
  36.7 6.9 %collective-permute-start.4 = (f32[8,8,128]{2,1,0:T(8,128)S(1)}, f32[8,8,128]{2,1,0:T(8,128)S(1)}, u32[]{:S(2)}, u32[]{:S(2)}) collective-permute-start(f32[8,8,128]{2,1,0:T(8,128)S(1)} %get-tuple-element.19), channel_id=1, source_target_pairs={{0,120},{1,121},{2,122},{3,123},{4,124},{5,125},{6,126},{7,127},{8... | collective-permute-start | bytes 98312 | tf_op jit(solution)/shard_map/ppermute | solution.py:169
  43.7 0.6 %copy-start.5 = (f32[8,8,128]{2,1,0:T(8,128)}, f32[8,8,128]{2,1,0:T(8,128)S(1)}, u32[]{:S(2)}) copy-start(f32[8,8,128]{2,1,0:T(8,128)S(1)} %collective-permute-done.5.lx_ref) | copy-start | bytes 98308
  43.7 0.6 %copy-start.6 = (f32[8,8,128]{2,1,0:T(8,128)}, f32[8,8,128]{2,1,0:T(8,128)S(1)}, u32[]{:S(2)}) copy-start(f32[8,8,128]{2,1,0:T(8,128)S(1)} %collective-permute-done.4.ux_ref) | copy-start | bytes 98308
  44.4 7.1 %collective-permute-start.7 = (f32[8,32,8]{2,1,0:T(8,128)S(1)}, f32[8,32,8]{2,1,0:T(8,128)S(1)}, u32[]{:S(2)}, u32[]{:S(2)}) collective-permute-start(f32[8,32,8]{2,1,0:T(8,128)S(1)} %get-tuple-element.12), channel_id=1, source_target_pairs={{0,1},{1,2},{2,3},{3,4},{4,5},{5,6},{6,7},{7,0},{8,9},{9,10},{10,1... | collective-permute-start | bytes 24584 | tf_op jit(solution)/shard_map/ppermute | solution.py:169
  44.5 7.1 %collective-permute-start.6 = (f32[8,32,8]{2,1,0:T(8,128)S(1)}, f32[8,32,8]{2,1,0:T(8,128)S(1)}, u32[]{:S(2)}, u32[]{:S(2)}) collective-permute-start(f32[8,32,8]{2,1,0:T(8,128)S(1)} %get-tuple-element.13), channel_id=1, source_target_pairs={{0,7},{1,0},{2,1},{3,2},{4,3},{5,4},{6,5},{7,6},{8,15},{9,8},{10,9... | collective-permute-start | bytes 24584 | tf_op jit(solution)/shard_map/ppermute | solution.py:169
  51.5 0.7 %copy-start.3 = (f32[8,32,8]{2,1,0:T(8,128)}, f32[8,32,8]{2,1,0:T(8,128)S(1)}, u32[]{:S(2)}) copy-start(f32[8,32,8]{2,1,0:T(8,128)S(1)} %collective-permute-done.7.ly_ref) | copy-start | bytes 24580
  52.2 0.6 %copy-start.4 = (f32[8,32,8]{2,1,0:T(8,128)}, f32[8,32,8]{2,1,0:T(8,128)S(1)}, u32[]{:S(2)}) copy-start(f32[8,32,8]{2,1,0:T(8,128)S(1)} %collective-permute-done.6.uy_ref) | copy-start | bytes 24580

commit v7 on v5

--- a/solution.py
+++ b/solution.py
@@ -11,6 +11,7 @@
 SWEEPS = 4
 CAP_F = 2048
 CAP_D = 512
+MX = 2
 
 
 SCREENING = 0.5
@@ -53,6 +54,50 @@
     acc_ref[...] += lax.dot_general(
         left, right, (((1,), (1,)), ((), ())), preferred_element_type=jnp.float32
     )
+
+
+def faces_kernel(x_ref, y_ref, a_ref, o_ref):
+    o_ref[...] = a_ref[...]
+    near_rows = NZ // 2 * MX
+    for source, low in ((x_ref, 0), (y_ref, CX - MX)):
+        x = source[...]
+        p = x[0:4]
+        c = x[4:7].astype(jnp.int32)
+        width = p.shape[1]
+        masses = p[0:1]
+        vals = jnp.concatenate([masses, masses * p[1:4]], axis=0)
+        near_i = c[1:2] - low
+        row = lax.shift_right_logical(c[0:1], 1) * MX + near_i
+        row = jnp.where((near_i >= 0) & (near_i < MX), row, -1)
+        col = lax.bitwise_and(c[0:1], 1) * CY + c[2:3]
+        hi = vals.astype(jnp.bfloat16)
+        lo = (vals - hi.astype(jnp.float32)).astype(jnp.bfloat16)
+        parts = [q.astype(jnp.float32)[e : e + 1] for q in (hi, lo) for e in range(4)]
+        row_hot = (lax.broadcasted_iota(jnp.int32, (near_rows, width), 0) == row).astype(jnp.float32)
+        left = jnp.concatenate([row_hot * part for part in parts], axis=0)
+        right = (lax.broadcasted_iota(jnp.int32, (COLS, width), 0) == col).astype(jnp.float32)
+        part = lax.dot_general(left, right, (((1,), (1,)), ((), ())), preferred_element_type=jnp.float32)
+        for piece in range(4 * SPLITS):
+            for half in range(NZ // 2):
+                target = piece * ROWS + half * CX + low
+                origin = piece * near_rows + half * MX
+                o_ref[target : target + MX, :] += part[origin : origin + MX, :]
+
+
+def deposit_faces(first, second, acc):
+    block = CAP_F + LANE
+    return pl.pallas_call(
+        faces_kernel,
+        grid=(1,),
+        in_specs=[
+            pl.BlockSpec((7, block), lambda b: (0, 0)),
+            pl.BlockSpec((7, block), lambda b: (0, 0)),
+            pl.BlockSpec(ACC_SHAPE, lambda b: (0, 0)),
+        ],
+        out_specs=pl.BlockSpec(ACC_SHAPE, lambda b: (0, 0)),
+        out_shape=jax.ShapeDtypeStruct(ACC_SHAPE, jnp.float32),
+        input_output_aliases={2: 0},
+    )(first, second, acc)
 
 
 def local_kernel(count_ref, p_ref, c_ref, o_ref):
@@ -237,7 +282,7 @@
     )
     from_minus_y = towards(plus_y, 0, 1)
     from_plus_y = towards(minus_y, 0, -1)
-    total = deposit_arrived(from_minus_x, from_plus_x, total, face)
+    total = deposit_faces(from_minus_x, from_plus_x, total)
     total = deposit_arrived(from_minus_y, from_plus_y, total, face + 2 * corner)
     total = total.reshape(SPLITS, 4, NZ // 2, CX, 2 * CY)
     summed = total[0, 0] + total[1, 0]

time: 54.5 us -> 53.9 us (0.989)
  Pallas kernels: 20 us -> 19.4 us
    pallas_call x2 -> x1, Pallas kernels: 7.38 us -> 4.05 us  [deposit_arrived(): pl.pallas_call(lambda x, y, a, o: arrived_kernel(block, x, y, a, o), grid...]
    pallas_call x0 -> x1, Pallas kernels: none -> 2.76 us  [deposit_faces(): pl.pallas_call(faces_kernel, grid=(1,), in_specs=[pl.BlockSpec((7, block)...]
where the time goes in v7:
time: 53.9 us; the launch traced here: 53.3 us
  starting transfers between devices  20.1 us (37%)
  Pallas kernels  19.4 us (36%)
  waiting for transfers between devices  6.45 us (12%)
  local copies, waits for them, and re-layouts  4.6 us (9%)
  other arithmetic  1.99 us (4%)
  between operations  0.76 us (1%)
    ppermute x8, starting transfers between devices, towards(): return lax.ppermute(block, ('gx', 'gy'), route)  20.1 us
    pallas_call x1, Pallas kernels, deposit_local(): pl.pallas_call(local_kernel, grid_spec=pltpu.PrefetchScalarGridSpec(num_s...  7.12 us
    ppermute x8, waiting for transfers between devices, towards(): return lax.ppermute(block, ('gx', 'gy'), route)  6.45 us
    pallas_call x1, Pallas kernels, deposit_arrived(): pl.pallas_call(lambda x, y, a, o: arrived_kernel(block, x, y, a, o), grid...  4.05 us
    unnamed x22, local copies, waits for them, and re-layouts  3.78 us
    pallas_call x1, Pallas kernels, relax(): pl.pallas_call(relax_kernel, out_shape=jax.ShapeDtypeStruct((NZ, CX, CY),...  3.65 us
    pallas_call x1, Pallas kernels, deposit_faces(): pl.pallas_call(faces_kernel, grid=(1,), in_specs=[pl.BlockSpec((7, block)...  2.76 us
    pallas_call x1, Pallas kernels, pack(): pl.pallas_call(pack_kernel, in_specs=[pl.BlockSpec(memory_space=pltpu.SME...  1.85 us
  transfers between devices with their start and end apart: 8, of which 4 were waited for; matrix products, arithmetic and copies ran while one was open for 1% of the time, Pallas kernels for 19%

profile of v7, /device:TPU:0, one launch (start us, length us, event | category | flops | bytes accessed | tf_op | source)
XLA Modules:
  0.0 53.3 jit_solution(504821512334554783)
XLA Ops:
  0.6 1.9 %shard_map.50 = (f32[7,3456]{1,0:T(8,128)}, f32[7,3456]{1,0:T(8,128)}, f32[7,2176]{1,0:T(8,128)}, f32[7,2176]{1,0:T(8,128)}) custom-call(s32[1,9]{1,0:T(1,128)} %count_ref.3, f32[4,16384]{1,0:T(4,128)} %p_ref.3, s32[3,16384]{1,0:T(4,128)} %c_ref.3), custom_call_target="tpu_custom_call" | custom-call | tf_op jit(solution)/shard_map/pallas_call | solution.py:183
  2.5 6.3 %collective-permute-start.1 = (f32[7,3456]{1,0:T(8,128)}, f32[7,3456]{1,0:T(8,128)S(1)}, u32[]{:S(2)}, u32[]{:S(2)}) collective-permute-start(f32[7,3456]{1,0:T(8,128)} %get-tuple-element.8), channel_id=1, source_target_pairs={{0,120},{1,121},{2,122},{3,123},{4,124},{5,125},{6,126},{7,127},{8... | collective-permute-start | bytes 290312 | tf_op jit(solution)/shard_map/ppermute | solution.py:201
  8.8 2.6 %collective-permute-done.x_ref = f32[7,3456]{1,0:T(8,128)S(1)} collective-permute-done((f32[7,3456]{1,0:T(8,128)}, f32[7,3456]{1,0:T(8,128)S(1)}, u32[]{:S(2)}, u32[]{:S(2)}) %collective-permute-start) | collective-permute-done | bytes 96800 | tf_op jit(solution)/shard_map/ppermute | solution.py:201
  11.5 0.5 copy-done.1
  12.0 0.1 copy-done.2
  12.1 0.8 %collective-permute-start.2 = (f32[7,3456]{1,0:T(8,128)S(1)}, f32[7,3456]{1,0:T(8,128)S(1)}, u32[]{:S(2)}, u32[]{:S(2)}) collective-permute-start(f32[7,3456]{1,0:T(8,128)S(1)} %pad_maximum_fusion.2), channel_id=1, source_target_pairs={{0,1},{1,2},{2,3},{3,4},{4,5},{5,6},{6,7},{7,0},{8,9},{9,10},{10,1... | collective-permute-start | bytes 290312 | tf_op jit(solution)/shard_map/ppermute | solution.py:201
  12.9 3.4 %collective-permute-start.3 = (f32[7,3456]{1,0:T(8,128)S(1)}, f32[7,3456]{1,0:T(8,128)S(1)}, u32[]{:S(2)}, u32[]{:S(2)}) collective-permute-start(f32[7,3456]{1,0:T(8,128)S(1)} %pad_maximum_fusion.3), channel_id=1, source_target_pairs={{0,7},{1,0},{2,1},{3,2},{4,3},{5,4},{6,5},{7,6},{8,15},{9,8},{10,9... | collective-permute-start | bytes 290312 | tf_op jit(solution)/shard_map/ppermute | solution.py:201
  16.3 7.1 %shard_map.51.a_ref = f32[512,256]{1,0:T(8,128)} custom-call(s32[1,9]{1,0:T(1,128)} %count_ref.3, f32[4,16384]{1,0:T(4,128)} %p_ref.3, s32[3,16384]{1,0:T(4,128)} %c_ref.3), custom_call_target="tpu_custom_call" | custom-call | tf_op jit(solution)/shard_map/pallas_call | solution.py:128
  23.4 2.8 %shard_map.52.a = f32[512,256]{1,0:T(8,128)} custom-call(f32[7,3456]{1,0:T(8,128)} %copy-done.1, f32[7,3456]{1,0:T(8,128)} %copy-done.2, f32[512,256]{1,0:T(8,128)} %shard_map.51.a_ref), custom_call_target="tpu_custom_call", output_to_operand_aliasing={{}: (2, {})} | custom-call | tf_op jit(solution)/shard_map/pallas_call | solution.py:89
  26.2 0.6 %copy-done.7 = f32[7,3456]{1,0:T(8,128)} copy-done((f32[7,3456]{1,0:T(8,128)}, f32[7,3456]{1,0:T(8,128)S(1)}, u32[]{:S(2)}) %copy-start.7) | copy-done | bytes 96792
  26.8 0.6 %copy-done.8 = f32[7,3456]{1,0:T(8,128)} copy-done((f32[7,3456]{1,0:T(8,128)}, f32[7,3456]{1,0:T(8,128)S(1)}, u32[]{:S(2)}) %copy-start.8) | copy-done | bytes 96792
  27.5 4.0 %shard_map.53 = f32[512,256]{1,0:T(8,128)} custom-call(f32[7,3456]{1,0:T(8,128)} %copy-done.7, f32[7,3456]{1,0:T(8,128)} %copy-done.8, f32[512,256]{1,0:T(8,128)} %shard_map.52.a), custom_call_target="tpu_custom_call", output_to_operand_aliasing={{}: (2, {})} | custom-call | tf_op jit(solution)/shard_map/pallas_call | solution.py:142
  31.5 0.9 %fusion.1 = f32[4,16,256]{2,1,0:T(8,128)S(1)} fusion(f32[2,4,4,16,256]{4,3,2,1,0:T(8,128)} %bitcast.17), kind=kLoop, calls=%fused_computation.9 | loop fusion | flops 16384 | bytes 196608 | tf_op jit(solution)/shard_map/add | solution.py:288
  32.4 1.1 %fusion = f32[3,4,16,256]{3,2,1,0:T(8,128)S(1)} fusion(f32[2,4,4,16,256]{4,3,2,1,0:T(8,128)} %bitcast.18), kind=kLoop, calls=%fused_computation.1 | loop fusion | flops 49152 | bytes 589824 | tf_op jit(solution)/shard_map/add | solution.py:291
  33.6 5.3 %collective-permute-start.4 = (f32[8,8,128]{2,1,0:T(8,128)S(1)}, f32[8,8,128]{2,1,0:T(8,128)S(1)}, u32[]{:S(2)}, u32[]{:S(2)}) collective-permute-start(f32[8,8,128]{2,1,0:T(8,128)S(1)} %get-tuple-element.19), channel_id=1, source_target_pairs={{0,120},{1,121},{2,122},{3,123},{4,124},{5,125},{6,126},{7,127},{8... | collective-permute-start | bytes 98312 | tf_op jit(solution)/shard_map/ppermute | solution.py:201
  39.0 1.6 %collective-permute-done.5.lx_ref = f32[8,8,128]{2,1,0:T(8,128)S(1)} collective-permute-done((f32[8,8,128]{2,1,0:T(8,128)S(1)}, f32[8,8,128]{2,1,0:T(8,128)S(1)}, u32[]{:S(2)}, u32[]{:S(2)}) %collective-permute-start.5) | collective-permute-done | bytes 32800 | tf_op jit(solution)/shard_map/ppermute | solution.py:201
  40.6 0.6 %copy-done.5 = f32[8,8,128]{2,1,0:T(8,128)} copy-done((f32[8,8,128]{2,1,0:T(8,128)}, f32[8,8,128]{2,1,0:T(8,128)S(1)}, u32[]{:S(2)}) %copy-start.5) | copy-done | bytes 32792
  41.2 0.1 fusion.2
  41.3 4.1 %collective-permute-start.6 = (f32[8,32,8]{2,1,0:T(8,128)S(1)}, f32[8,32,8]{2,1,0:T(8,128)S(1)}, u32[]{:S(2)}, u32[]{:S(2)}) collective-permute-start(f32[8,32,8]{2,1,0:T(8,128)S(1)} %get-tuple-element.13), channel_id=1, source_target_pairs={{0,7},{1,0},{2,1},{3,2},{4,3},{5,4},{6,5},{7,6},{8,15},{9,8},{10,9... | collective-permute-start | bytes 24584 | tf_op jit(solution)/shard_map/ppermute | solution.py:201
  45.5 0.7 %copy.8 = f32[3,4,2,16,128]{4,3,2,1,0:T(8,128)} copy(f32[3,4,2,16,128]{4,3,1,0,2:T(8,128)S(1)} %pad_maximum_fusion) | data formatting | bytes 393216 | tf_op jit(solution)/shard_map/stack | solution.py:292
  46.2 2.2 %collective-permute-done.7.ly_ref = f32[8,32,8]{2,1,0:T(8,128)S(1)} collective-permute-done((f32[8,32,8]{2,1,0:T(8,128)S(1)}, f32[8,32,8]{2,1,0:T(8,128)S(1)}, u32[]{:S(2)}, u32[]{:S(2)}) %collective-permute-start.7) | collective-permute-done | bytes 8224 | tf_op jit(solution)/shard_map/ppermute | solution.py:201
  48.4 0.6 %copy-done.3 = f32[8,32,8]{2,1,0:T(8,128)} copy-done((f32[8,32,8]{2,1,0:T(8,128)}, f32[8,32,8]{2,1,0:T(8,128)S(1)}, u32[]{:S(2)}) %copy-start.3) | copy-done | bytes 8216
  49.1 0.6 %copy-done.4 = f32[8,32,8]{2,1,0:T(8,128)} copy-done((f32[8,32,8]{2,1,0:T(8,128)}, f32[8,32,8]{2,1,0:T(8,128)S(1)}, u32[]{:S(2)}) %copy-start.4) | copy-done | bytes 8216
  49.7 3.6 %shard_map.54 = f32[8,16,128]{2,1,0:T(8,128)} custom-call(f32[8,16,128]{2,1,0:T(8,128)} %bitcast.21, f32[8,8,128]{2,1,0:T(8,128)} %copy-done.6, f32[8,8,128]{2,1,0:T(8,128)} %copy-done.5, f32[8,32,8]{2,1,0:T(8,128)} %copy-done.4, f32[8,32,8]{2,1,0:T(8,128)} %copy-done.3), custom_call_target="tpu_custom_call" | custom-call | tf_op jit(solution)/shard_map/pallas_call | solution.py:263
  (33 shorter events, 0.4 us)
Async XLA Ops:
  2.5 8.9 %collective-permute-start = (f32[7,3456]{1,0:T(8,128)}, f32[7,3456]{1,0:T(8,128)S(1)}, u32[]{:S(2)}, u32[]{:S(2)}) collective-permute-start(f32[7,3456]{1,0:T(8,128)} %get-tuple-element.7), channel_id=1, source_target_pairs={{0,8},{1,9},{2,10},{3,11},{4,12},{5,13},{6,14},{7,15},{8,16},{9,17... | collective-permute-start | bytes 290312 | tf_op jit(solution)/shard_map/ppermute | solution.py:201
  2.5 8.9 %copy-start.10 = (f32[7,2176]{1,0:T(8,128)S(1)}, f32[7,2176]{1,0:T(8,128)}, u32[]{:S(2)}) copy-start(f32[7,2176]{1,0:T(8,128)} %get-tuple-element.6) | copy-start | bytes 182788
  2.5 8.9 %collective-permute-start.1 = (f32[7,3456]{1,0:T(8,128)}, f32[7,3456]{1,0:T(8,128)S(1)}, u32[]{:S(2)}, u32[]{:S(2)}) collective-permute-start(f32[7,3456]{1,0:T(8,128)} %get-tuple-element.8), channel_id=1, source_target_pairs={{0,120},{1,121},{2,122},{3,123},{4,124},{5,125},{6,126},{7,127},{8... | collective-permute-start | bytes 290312 | tf_op jit(solution)/shard_map/ppermute | solution.py:201
  11.3 0.6 %copy-start.1 = (f32[7,3456]{1,0:T(8,128)}, f32[7,3456]{1,0:T(8,128)S(1)}, u32[]{:S(2)}) copy-start(f32[7,3456]{1,0:T(8,128)S(1)} %collective-permute-done.x_ref) | copy-start | bytes 290308
  11.4 0.7 %copy-start.2 = (f32[7,3456]{1,0:T(8,128)}, f32[7,3456]{1,0:T(8,128)S(1)}, u32[]{:S(2)}) copy-start(f32[7,3456]{1,0:T(8,128)S(1)} %collective-permute-done.1.y_ref) | copy-start | bytes 290308
  11.4 1.4 %copy-start.9 = (f32[7,2176]{1,0:T(8,128)S(1)}, f32[7,2176]{1,0:T(8,128)}, u32[]{:S(2)}) copy-start(f32[7,2176]{1,0:T(8,128)} %get-tuple-element.9) | copy-start | bytes 182788
  12.1 14.1 %collective-permute-start.2 = (f32[7,3456]{1,0:T(8,128)S(1)}, f32[7,3456]{1,0:T(8,128)S(1)}, u32[]{:S(2)}, u32[]{:S(2)}) collective-permute-start(f32[7,3456]{1,0:T(8,128)S(1)} %pad_maximum_fusion.2), channel_id=1, source_target_pairs={{0,1},{1,2},{2,3},{3,4},{4,5},{5,6},{6,7},{7,0},{8,9},{9,10},{10,1... | collective-permute-start | bytes 290312 | tf_op jit(solution)/shard_map/ppermute | solution.py:201
  12.9 13.3 %collective-permute-start.3 = (f32[7,3456]{1,0:T(8,128)S(1)}, f32[7,3456]{1,0:T(8,128)S(1)}, u32[]{:S(2)}, u32[]{:S(2)}) collective-permute-start(f32[7,3456]{1,0:T(8,128)S(1)} %pad_maximum_fusion.3), channel_id=1, source_target_pairs={{0,7},{1,0},{2,1},{3,2},{4,3},{5,4},{6,5},{7,6},{8,15},{9,8},{10,9... | collective-permute-start | bytes 290312 | tf_op jit(solution)/shard_map/ppermute | solution.py:201
  26.2 0.6 %copy-start.7 = (f32[7,3456]{1,0:T(8,128)}, f32[7,3456]{1,0:T(8,128)S(1)}, u32[]{:S(2)}) copy-start(f32[7,3456]{1,0:T(8,128)S(1)} %collective-permute-done.2.x) | copy-start | bytes 290308
  26.8 0.7 %copy-start.8 = (f32[7,3456]{1,0:T(8,128)}, f32[7,3456]{1,0:T(8,128)S(1)}, u32[]{:S(2)}) copy-start(f32[7,3456]{1,0:T(8,128)S(1)} %collective-permute-done.3.y) | copy-start | bytes 290308
  33.5 7.1 %copy-start = (f32[4,2,16,128]{3,2,1,0:T(8,128)}, f32[4,2,16,128]{3,2,1,0:T(8,128)S(1)}, u32[]{:S(2)}) copy-start(f32[4,2,16,128]{3,2,1,0:T(8,128)S(1)} %pad_maximum_fusion.4) | copy-start | bytes 196612
  33.5 7.0 %collective-permute-start.5 = (f32[8,8,128]{2,1,0:T(8,128)S(1)}, f32[8,8,128]{2,1,0:T(8,128)S(1)}, u32[]{:S(2)}, u32[]{:S(2)}) collective-permute-start(f32[8,8,128]{2,1,0:T(8,128)S(1)} %get-tuple-element.18), channel_id=1, source_target_pairs={{0,8},{1,9},{2,10},{3,11},{4,12},{5,13},{6,14},{7,15},{8,16},{9,17... | collective-permute-start | bytes 98312 | tf_op jit(solution)/shard_map/ppermute | solution.py:201
  33.6 6.9 %collective-permute-start.4 = (f32[8,8,128]{2,1,0:T(8,128)S(1)}, f32[8,8,128]{2,1,0:T(8,128)S(1)}, u32[]{:S(2)}, u32[]{:S(2)}) collective-permute-start(f32[8,8,128]{2,1,0:T(8,128)S(1)} %get-tuple-element.19), channel_id=1, source_target_pairs={{0,120},{1,121},{2,122},{3,123},{4,124},{5,125},{6,126},{7,127},{8... | collective-permute-start | bytes 98312 | tf_op jit(solution)/shard_map/ppermute | solution.py:201
  40.5 0.6 %copy-start.5 = (f32[8,8,128]{2,1,0:T(8,128)}, f32[8,8,128]{2,1,0:T(8,128)S(1)}, u32[]{:S(2)}) copy-start(f32[8,8,128]{2,1,0:T(8,128)S(1)} %collective-permute-done.5.lx_ref) | copy-start | bytes 98308
  40.6 0.6 %copy-start.6 = (f32[8,8,128]{2,1,0:T(8,128)}, f32[8,8,128]{2,1,0:T(8,128)S(1)}, u32[]{:S(2)}) copy-start(f32[8,8,128]{2,1,0:T(8,128)S(1)} %collective-permute-done.4.ux_ref) | copy-start | bytes 98308
  41.3 7.1 %collective-permute-start.7 = (f32[8,32,8]{2,1,0:T(8,128)S(1)}, f32[8,32,8]{2,1,0:T(8,128)S(1)}, u32[]{:S(2)}, u32[]{:S(2)}) collective-permute-start(f32[8,32,8]{2,1,0:T(8,128)S(1)} %get-tuple-element.12), channel_id=1, source_target_pairs={{0,1},{1,2},{2,3},{3,4},{4,5},{5,6},{6,7},{7,0},{8,9},{9,10},{10,1... | collective-permute-start | bytes 24584 | tf_op jit(solution)/shard_map/ppermute | solution.py:201
  41.3 7.1 %collective-permute-start.6 = (f32[8,32,8]{2,1,0:T(8,128)S(1)}, f32[8,32,8]{2,1,0:T(8,128)S(1)}, u32[]{:S(2)}, u32[]{:S(2)}) collective-permute-start(f32[8,32,8]{2,1,0:T(8,128)S(1)} %get-tuple-element.13), channel_id=1, source_target_pairs={{0,7},{1,0},{2,1},{3,2},{4,3},{5,4},{6,5},{7,6},{8,15},{9,8},{10,9... | collective-permute-start | bytes 24584 | tf_op jit(solution)/shard_map/ppermute | solution.py:201
  48.4 0.7 %copy-start.3 = (f32[8,32,8]{2,1,0:T(8,128)}, f32[8,32,8]{2,1,0:T(8,128)S(1)}, u32[]{:S(2)}) copy-start(f32[8,32,8]{2,1,0:T(8,128)S(1)} %collective-permute-done.7.ly_ref) | copy-start | bytes 24580
  49.1 0.6 %copy-start.4 = (f32[8,32,8]{2,1,0:T(8,128)}, f32[8,32,8]{2,1,0:T(8,128)S(1)}, u32[]{:S(2)}) copy-start(f32[8,32,8]{2,1,0:T(8,128)S(1)} %collective-permute-done.6.uy_ref) | copy-start | bytes 24580

commit v8 on v7

--- a/solution.py
+++ b/solution.py
@@ -12,6 +12,7 @@
 CAP_F = 2048
 CAP_D = 512
 MX = 2
+MY = 16
 
 
 SCREENING = 0.5
@@ -54,6 +55,51 @@
     acc_ref[...] += lax.dot_general(
         left, right, (((1,), (1,)), ((), ())), preferred_element_type=jnp.float32
     )
+
+
+def crossing_kernel(x_ref, y_ref, a_ref, o_ref):
+    o_ref[...] = a_ref[...]
+    for source, low in ((x_ref, 0), (y_ref, CY - MY)):
+        x = source[...]
+        p = x[0:4]
+        c = x[4:7].astype(jnp.int32)
+        width = p.shape[1]
+        masses = p[0:1]
+        vals = jnp.concatenate([masses, masses * p[1:4]], axis=0)
+        row = lax.shift_right_logical(c[0:1], 1) * CX + c[1:2]
+        near_j = c[2:3] - low
+        col = lax.bitwise_and(c[0:1], 1) * MY + near_j
+        col = jnp.where((near_j >= 0) & (near_j < MY), col, -1)
+        hi = vals.astype(jnp.bfloat16)
+        lo = (vals - hi.astype(jnp.float32)).astype(jnp.bfloat16)
+        parts = [q.astype(jnp.float32)[e : e + 1] for q in (hi, lo) for e in range(4)]
+        col_hot = (lax.broadcasted_iota(jnp.int32, (2 * MY, width), 0) == col).astype(jnp.float32)
+        weighted = jnp.concatenate([col_hot * part for part in parts], axis=0)
+        row_hot = (lax.broadcasted_iota(jnp.int32, (ROWS, width), 0) == row).astype(jnp.float32)
+        part = lax.dot_general(
+            row_hot, weighted, (((1,), (1,)), ((), ())), preferred_element_type=jnp.float32
+        )
+        for piece in range(4 * SPLITS):
+            for parity in range(2):
+                origin = (piece * 2 + parity) * MY
+                lane = parity * CY + low
+                o_ref[piece * ROWS : (piece + 1) * ROWS, lane : lane + MY] += part[:, origin : origin + MY]
+
+
+def deposit_crossing(first, second, acc):
+    block = first.shape[1]
+    return pl.pallas_call(
+        crossing_kernel,
+        grid=(1,),
+        in_specs=[
+            pl.BlockSpec((7, block), lambda b: (0, 0)),
+            pl.BlockSpec((7, block), lambda b: (0, 0)),
+            pl.BlockSpec(ACC_SHAPE, lambda b: (0, 0)),
+        ],
+        out_specs=pl.BlockSpec(ACC_SHAPE, lambda b: (0, 0)),
+        out_shape=jax.ShapeDtypeStruct(ACC_SHAPE, jnp.float32),
+        input_output_aliases={2: 0},
+    )(first, second, acc)
 
 
 def faces_kernel(x_ref, y_ref, a_ref, o_ref):
@@ -113,13 +159,6 @@
         accumulate(first, BLOCK, step, p_ref[...], c_ref[...], o_ref)
 
 
-def arrived_kernel(block, x_ref, y_ref, a_ref, o_ref):
-    o_ref[...] = a_ref[...]
-    for source in (x_ref, y_ref):
-        x = source[...]
-        accumulate(0, block, 0, x[0:4], x[4:7].astype(jnp.int32), o_ref)
-
-
 ACC_SHAPE = (4 * SPLITS * ROWS, COLS)
 
 
@@ -136,21 +175,6 @@
         out_shape=jax.ShapeDtypeStruct(ACC_SHAPE, jnp.float32),
         compiler_params=pltpu.CompilerParams(dimension_semantics=("arbitrary",)),
     )(counts, payload, cells)
-
-
-def deposit_arrived(first, second, acc, block):
-    return pl.pallas_call(
-        lambda x, y, a, o: arrived_kernel(block, x, y, a, o),
-        grid=(1,),
-        in_specs=[
-            pl.BlockSpec((7, block), lambda b: (0, 0)),
-            pl.BlockSpec((7, block), lambda b: (0, 0)),
-            pl.BlockSpec(ACC_SHAPE, lambda b: (0, 0)),
-        ],
-        out_specs=pl.BlockSpec(ACC_SHAPE, lambda b: (0, 0)),
-        out_shape=jax.ShapeDtypeStruct(ACC_SHAPE, jnp.float32),
-        input_output_aliases={2: 0},
-    )(first, second, acc)
 
 
 def pack_kernel(count_ref, p_ref, c_ref, plus_x, minus_x, plus_y, minus_y):
@@ -283,7 +307,7 @@
     from_minus_y = towards(plus_y, 0, 1)
     from_plus_y = towards(minus_y, 0, -1)
     total = deposit_faces(from_minus_x, from_plus_x, total)
-    total = deposit_arrived(from_minus_y, from_plus_y, total, face + 2 * corner)
+    total = deposit_crossing(from_minus_y, from_plus_y, total)
     total = total.reshape(SPLITS, 4, NZ // 2, CX, 2 * CY)
     summed = total[0, 0] + total[1, 0]
     density = jnp.stack([summed[..., :CY], summed[..., CY:]], axis=1).reshape(NZ, CX, CY)

time: 53.9 us -> 53.4 us (level)
    pallas_call x1, Pallas kernels: 4.05 us -> 3.49 us  [deposit_crossing(): pl.pallas_call(crossing_kernel, grid=(1,), in_specs=[pl.BlockSpec((7, blo...]
where the time goes in v8:
time: 53.4 us; the launch traced here: 52.8 us
  starting transfers between devices  20.1 us (38%)
  Pallas kernels  18.9 us (35%)
  waiting for transfers between devices  6.45 us (12%)
  local copies, waits for them, and re-layouts  4.6 us (9%)
  other arithmetic  1.99 us (4%)
  between operations  0.76 us (1%)
    ppermute x8, starting transfers between devices, towards(): return lax.ppermute(block, ('gx', 'gy'), route)  20.1 us
    pallas_call x1, Pallas kernels, deposit_local(): pl.pallas_call(local_kernel, grid_spec=pltpu.PrefetchScalarGridSpec(num_s...  7.12 us
    ppermute x8, waiting for transfers between devices, towards(): return lax.ppermute(block, ('gx', 'gy'), route)  6.45 us
    unnamed x22, local copies, waits for them, and re-layouts  3.78 us
    pallas_call x1, Pallas kernels, relax(): pl.pallas_call(relax_kernel, out_shape=jax.ShapeDtypeStruct((NZ, CX, CY),...  3.65 us
    pallas_call x1, Pallas kernels, deposit_crossing(): pl.pallas_call(crossing_kernel, grid=(1,), in_specs=[pl.BlockSpec((7, blo...  3.49 us
    pallas_call x1, Pallas kernels, deposit_faces(): pl.pallas_call(faces_kernel, grid=(1,), in_specs=[pl.BlockSpec((7, block)...  2.76 us
    pallas_call x1, Pallas kernels, pack(): pl.pallas_call(pack_kernel, in_specs=[pl.BlockSpec(memory_space=pltpu.SME...  1.85 us
  transfers between devices with their start and end apart: 8, of which 4 were waited for; matrix products, arithmetic and copies ran while one was open for 1% of the time, Pallas kernels for 19%

profile of v8, /device:TPU:0, one launch (start us, length us, event | category | flops | bytes accessed | tf_op | source)
XLA Modules:
  0.0 52.8 jit_solution(10040724687751972768)
XLA Ops:
  0.6 1.9 %shard_map.50 = (f32[7,3456]{1,0:T(8,128)}, f32[7,3456]{1,0:T(8,128)}, f32[7,2176]{1,0:T(8,128)}, f32[7,2176]{1,0:T(8,128)}) custom-call(s32[1,9]{1,0:T(1,128)} %count_ref.3, f32[4,16384]{1,0:T(4,128)} %p_ref.3, s32[3,16384]{1,0:T(4,128)} %c_ref.3), custom_call_target="tpu_custom_call" | custom-call | tf_op jit(solution)/shard_map/pallas_call | solution.py:207
  2.5 6.3 %collective-permute-start.1 = (f32[7,3456]{1,0:T(8,128)}, f32[7,3456]{1,0:T(8,128)S(1)}, u32[]{:S(2)}, u32[]{:S(2)}) collective-permute-start(f32[7,3456]{1,0:T(8,128)} %get-tuple-element.8), channel_id=1, source_target_pairs={{0,120},{1,121},{2,122},{3,123},{4,124},{5,125},{6,126},{7,127},{8... | collective-permute-start | bytes 290312 | tf_op jit(solution)/shard_map/ppermute | solution.py:225
  8.8 2.6 %collective-permute-done.x_ref = f32[7,3456]{1,0:T(8,128)S(1)} collective-permute-done((f32[7,3456]{1,0:T(8,128)}, f32[7,3456]{1,0:T(8,128)S(1)}, u32[]{:S(2)}, u32[]{:S(2)}) %collective-permute-start) | collective-permute-done | bytes 96800 | tf_op jit(solution)/shard_map/ppermute | solution.py:225
  11.5 0.5 copy-done.1
  12.0 0.1 copy-done.2
  12.1 0.8 %collective-permute-start.2 = (f32[7,3456]{1,0:T(8,128)S(1)}, f32[7,3456]{1,0:T(8,128)S(1)}, u32[]{:S(2)}, u32[]{:S(2)}) collective-permute-start(f32[7,3456]{1,0:T(8,128)S(1)} %pad_maximum_fusion.2), channel_id=1, source_target_pairs={{0,1},{1,2},{2,3},{3,4},{4,5},{5,6},{6,7},{7,0},{8,9},{9,10},{10,1... | collective-permute-start | bytes 290312 | tf_op jit(solution)/shard_map/ppermute | solution.py:225
  12.9 3.4 %collective-permute-start.3 = (f32[7,3456]{1,0:T(8,128)S(1)}, f32[7,3456]{1,0:T(8,128)S(1)}, u32[]{:S(2)}, u32[]{:S(2)}) collective-permute-start(f32[7,3456]{1,0:T(8,128)S(1)} %pad_maximum_fusion.3), channel_id=1, source_target_pairs={{0,7},{1,0},{2,1},{3,2},{4,3},{5,4},{6,5},{7,6},{8,15},{9,8},{10,9... | collective-permute-start | bytes 290312 | tf_op jit(solution)/shard_map/ppermute | solution.py:225
  16.3 7.1 %shard_map.51.a_ref = f32[512,256]{1,0:T(8,128)} custom-call(s32[1,9]{1,0:T(1,128)} %count_ref.3, f32[4,16384]{1,0:T(4,128)} %p_ref.3, s32[3,16384]{1,0:T(4,128)} %c_ref.3), custom_call_target="tpu_custom_call" | custom-call | tf_op jit(solution)/shard_map/pallas_call | solution.py:167
  23.4 2.8 %shard_map.52.a_ref = f32[512,256]{1,0:T(8,128)} custom-call(f32[7,3456]{1,0:T(8,128)} %copy-done.1, f32[7,3456]{1,0:T(8,128)} %copy-done.2, f32[512,256]{1,0:T(8,128)} %shard_map.51.a_ref), custom_call_target="tpu_custom_call", output_to_operand_aliasing={{}: (2, {})} | custom-call | tf_op jit(solution)/shard_map/pallas_call | solution.py:135
  26.2 0.6 %copy-done.7 = f32[7,3456]{1,0:T(8,128)} copy-done((f32[7,3456]{1,0:T(8,128)}, f32[7,3456]{1,0:T(8,128)S(1)}, u32[]{:S(2)}) %copy-start.7) | copy-done | bytes 96792
  26.8 0.6 %copy-done.8 = f32[7,3456]{1,0:T(8,128)} copy-done((f32[7,3456]{1,0:T(8,128)}, f32[7,3456]{1,0:T(8,128)S(1)}, u32[]{:S(2)}) %copy-start.8) | copy-done | bytes 96792
  27.5 3.5 %shard_map.53 = f32[512,256]{1,0:T(8,128)} custom-call(f32[7,3456]{1,0:T(8,128)} %copy-done.7, f32[7,3456]{1,0:T(8,128)} %copy-done.8, f32[512,256]{1,0:T(8,128)} %shard_map.52.a_ref), custom_call_target="tpu_custom_call", output_to_operand_aliasing={{}: (2, {})} | custom-call | tf_op jit(solution)/shard_map/pallas_call | solution.py:91
  31.0 0.9 %fusion.1 = f32[4,16,256]{2,1,0:T(8,128)S(1)} fusion(f32[2,4,4,16,256]{4,3,2,1,0:T(8,128)} %bitcast.17), kind=kLoop, calls=%fused_computation.9 | loop fusion | flops 16384 | bytes 196608 | tf_op jit(solution)/shard_map/add | solution.py:312
  31.9 1.1 %fusion = f32[3,4,16,256]{3,2,1,0:T(8,128)S(1)} fusion(f32[2,4,4,16,256]{4,3,2,1,0:T(8,128)} %bitcast.18), kind=kLoop, calls=%fused_computation.1 | loop fusion | flops 49152 | bytes 589824 | tf_op jit(solution)/shard_map/add | solution.py:315
  33.0 5.3 %collective-permute-start.4 = (f32[8,8,128]{2,1,0:T(8,128)S(1)}, f32[8,8,128]{2,1,0:T(8,128)S(1)}, u32[]{:S(2)}, u32[]{:S(2)}) collective-permute-start(f32[8,8,128]{2,1,0:T(8,128)S(1)} %get-tuple-element.19), channel_id=1, source_target_pairs={{0,120},{1,121},{2,122},{3,123},{4,124},{5,125},{6,126},{7,127},{8... | collective-permute-start | bytes 98312 | tf_op jit(solution)/shard_map/ppermute | solution.py:225
  38.4 1.6 %collective-permute-done.5.lx_ref = f32[8,8,128]{2,1,0:T(8,128)S(1)} collective-permute-done((f32[8,8,128]{2,1,0:T(8,128)S(1)}, f32[8,8,128]{2,1,0:T(8,128)S(1)}, u32[]{:S(2)}, u32[]{:S(2)}) %collective-permute-start.5) | collective-permute-done | bytes 32800 | tf_op jit(solution)/shard_map/ppermute | solution.py:225
  40.0 0.6 %copy-done.5 = f32[8,8,128]{2,1,0:T(8,128)} copy-done((f32[8,8,128]{2,1,0:T(8,128)}, f32[8,8,128]{2,1,0:T(8,128)S(1)}, u32[]{:S(2)}) %copy-start.5) | copy-done | bytes 32792
  40.6 0.1 fusion.2
  40.8 4.1 %collective-permute-start.6 = (f32[8,32,8]{2,1,0:T(8,128)S(1)}, f32[8,32,8]{2,1,0:T(8,128)S(1)}, u32[]{:S(2)}, u32[]{:S(2)}) collective-permute-start(f32[8,32,8]{2,1,0:T(8,128)S(1)} %get-tuple-element.13), channel_id=1, source_target_pairs={{0,7},{1,0},{2,1},{3,2},{4,3},{5,4},{6,5},{7,6},{8,15},{9,8},{10,9... | collective-permute-start | bytes 24584 | tf_op jit(solution)/shard_map/ppermute | solution.py:225
  44.9 0.7 %copy.8 = f32[3,4,2,16,128]{4,3,2,1,0:T(8,128)} copy(f32[3,4,2,16,128]{4,3,1,0,2:T(8,128)S(1)} %pad_maximum_fusion) | data formatting | bytes 393216 | tf_op jit(solution)/shard_map/stack | solution.py:316
  45.6 2.2 %collective-permute-done.7.ly_ref = f32[8,32,8]{2,1,0:T(8,128)S(1)} collective-permute-done((f32[8,32,8]{2,1,0:T(8,128)S(1)}, f32[8,32,8]{2,1,0:T(8,128)S(1)}, u32[]{:S(2)}, u32[]{:S(2)}) %collective-permute-start.7) | collective-permute-done | bytes 8224 | tf_op jit(solution)/shard_map/ppermute | solution.py:225
  47.9 0.6 %copy-done.3 = f32[8,32,8]{2,1,0:T(8,128)} copy-done((f32[8,32,8]{2,1,0:T(8,128)}, f32[8,32,8]{2,1,0:T(8,128)S(1)}, u32[]{:S(2)}) %copy-start.3) | copy-done | bytes 8216
  48.5 0.6 %copy-done.4 = f32[8,32,8]{2,1,0:T(8,128)} copy-done((f32[8,32,8]{2,1,0:T(8,128)}, f32[8,32,8]{2,1,0:T(8,128)S(1)}, u32[]{:S(2)}) %copy-start.4) | copy-done | bytes 8216
  49.1 3.6 %shard_map.54 = f32[8,16,128]{2,1,0:T(8,128)} custom-call(f32[8,16,128]{2,1,0:T(8,128)} %bitcast.21, f32[8,8,128]{2,1,0:T(8,128)} %copy-done.6, f32[8,8,128]{2,1,0:T(8,128)} %copy-done.5, f32[8,32,8]{2,1,0:T(8,128)} %copy-done.4, f32[8,32,8]{2,1,0:T(8,128)} %copy-done.3), custom_call_target="tpu_custom_call" | custom-call | tf_op jit(solution)/shard_map/pallas_call | solution.py:287
  (33 shorter events, 0.4 us)
Async XLA Ops:
  2.5 8.9 %collective-permute-start = (f32[7,3456]{1,0:T(8,128)}, f32[7,3456]{1,0:T(8,128)S(1)}, u32[]{:S(2)}, u32[]{:S(2)}) collective-permute-start(f32[7,3456]{1,0:T(8,128)} %get-tuple-element.7), channel_id=1, source_target_pairs={{0,8},{1,9},{2,10},{3,11},{4,12},{5,13},{6,14},{7,15},{8,16},{9,17... | collective-permute-start | bytes 290312 | tf_op jit(solution)/shard_map/ppermute | solution.py:225
  2.5 8.9 %copy-start.10 = (f32[7,2176]{1,0:T(8,128)S(1)}, f32[7,2176]{1,0:T(8,128)}, u32[]{:S(2)}) copy-start(f32[7,2176]{1,0:T(8,128)} %get-tuple-element.6) | copy-start | bytes 182788
  2.5 8.9 %collective-permute-start.1 = (f32[7,3456]{1,0:T(8,128)}, f32[7,3456]{1,0:T(8,128)S(1)}, u32[]{:S(2)}, u32[]{:S(2)}) collective-permute-start(f32[7,3456]{1,0:T(8,128)} %get-tuple-element.8), channel_id=1, source_target_pairs={{0,120},{1,121},{2,122},{3,123},{4,124},{5,125},{6,126},{7,127},{8... | collective-permute-start | bytes 290312 | tf_op jit(solution)/shard_map/ppermute | solution.py:225
  11.3 0.6 %copy-start.1 = (f32[7,3456]{1,0:T(8,128)}, f32[7,3456]{1,0:T(8,128)S(1)}, u32[]{:S(2)}) copy-start(f32[7,3456]{1,0:T(8,128)S(1)} %collective-permute-done.x_ref) | copy-start | bytes 290308
  11.4 0.7 %copy-start.2 = (f32[7,3456]{1,0:T(8,128)}, f32[7,3456]{1,0:T(8,128)S(1)}, u32[]{:S(2)}) copy-start(f32[7,3456]{1,0:T(8,128)S(1)} %collective-permute-done.1.y_ref) | copy-start | bytes 290308
  11.4 1.4 %copy-start.9 = (f32[7,2176]{1,0:T(8,128)S(1)}, f32[7,2176]{1,0:T(8,128)}, u32[]{:S(2)}) copy-start(f32[7,2176]{1,0:T(8,128)} %get-tuple-element.9) | copy-start | bytes 182788
  12.1 14.1 %collective-permute-start.2 = (f32[7,3456]{1,0:T(8,128)S(1)}, f32[7,3456]{1,0:T(8,128)S(1)}, u32[]{:S(2)}, u32[]{:S(2)}) collective-permute-start(f32[7,3456]{1,0:T(8,128)S(1)} %pad_maximum_fusion.2), channel_id=1, source_target_pairs={{0,1},{1,2},{2,3},{3,4},{4,5},{5,6},{6,7},{7,0},{8,9},{9,10},{10,1... | collective-permute-start | bytes 290312 | tf_op jit(solution)/shard_map/ppermute | solution.py:225
  12.9 13.3 %collective-permute-start.3 = (f32[7,3456]{1,0:T(8,128)S(1)}, f32[7,3456]{1,0:T(8,128)S(1)}, u32[]{:S(2)}, u32[]{:S(2)}) collective-permute-start(f32[7,3456]{1,0:T(8,128)S(1)} %pad_maximum_fusion.3), channel_id=1, source_target_pairs={{0,7},{1,0},{2,1},{3,2},{4,3},{5,4},{6,5},{7,6},{8,15},{9,8},{10,9... | collective-permute-start | bytes 290312 | tf_op jit(solution)/shard_map/ppermute | solution.py:225
  26.2 0.6 %copy-start.7 = (f32[7,3456]{1,0:T(8,128)}, f32[7,3456]{1,0:T(8,128)S(1)}, u32[]{:S(2)}) copy-start(f32[7,3456]{1,0:T(8,128)S(1)} %collective-permute-done.2.x_ref) | copy-start | bytes 290308
  26.8 0.7 %copy-start.8 = (f32[7,3456]{1,0:T(8,128)}, f32[7,3456]{1,0:T(8,128)S(1)}, u32[]{:S(2)}) copy-start(f32[7,3456]{1,0:T(8,128)S(1)} %collective-permute-done.3.y_ref) | copy-start | bytes 290308
  32.9 7.1 %copy-start = (f32[4,2,16,128]{3,2,1,0:T(8,128)}, f32[4,2,16,128]{3,2,1,0:T(8,128)S(1)}, u32[]{:S(2)}) copy-start(f32[4,2,16,128]{3,2,1,0:T(8,128)S(1)} %pad_maximum_fusion.4) | copy-start | bytes 196612
  33.0 7.0 %collective-permute-start.5 = (f32[8,8,128]{2,1,0:T(8,128)S(1)}, f32[8,8,128]{2,1,0:T(8,128)S(1)}, u32[]{:S(2)}, u32[]{:S(2)}) collective-permute-start(f32[8,8,128]{2,1,0:T(8,128)S(1)} %get-tuple-element.18), channel_id=1, source_target_pairs={{0,8},{1,9},{2,10},{3,11},{4,12},{5,13},{6,14},{7,15},{8,16},{9,17... | collective-permute-start | bytes 98312 | tf_op jit(solution)/shard_map/ppermute | solution.py:225
  33.0 6.9 %collective-permute-start.4 = (f32[8,8,128]{2,1,0:T(8,128)S(1)}, f32[8,8,128]{2,1,0:T(8,128)S(1)}, u32[]{:S(2)}, u32[]{:S(2)}) collective-permute-start(f32[8,8,128]{2,1,0:T(8,128)S(1)} %get-tuple-element.19), channel_id=1, source_target_pairs={{0,120},{1,121},{2,122},{3,123},{4,124},{5,125},{6,126},{7,127},{8... | collective-permute-start | bytes 98312 | tf_op jit(solution)/shard_map/ppermute | solution.py:225
  40.0 0.6 %copy-start.5 = (f32[8,8,128]{2,1,0:T(8,128)}, f32[8,8,128]{2,1,0:T(8,128)S(1)}, u32[]{:S(2)}) copy-start(f32[8,8,128]{2,1,0:T(8,128)S(1)} %collective-permute-done.5.lx_ref) | copy-start | bytes 98308
  40.0 0.6 %copy-start.6 = (f32[8,8,128]{2,1,0:T(8,128)}, f32[8,8,128]{2,1,0:T(8,128)S(1)}, u32[]{:S(2)}) copy-start(f32[8,8,128]{2,1,0:T(8,128)S(1)} %collective-permute-done.4.ux_ref) | copy-start | bytes 98308
  40.7 7.1 %collective-permute-start.7 = (f32[8,32,8]{2,1,0:T(8,128)S(1)}, f32[8,32,8]{2,1,0:T(8,128)S(1)}, u32[]{:S(2)}, u32[]{:S(2)}) collective-permute-start(f32[8,32,8]{2,1,0:T(8,128)S(1)} %get-tuple-element.12), channel_id=1, source_target_pairs={{0,1},{1,2},{2,3},{3,4},{4,5},{5,6},{6,7},{7,0},{8,9},{9,10},{10,1... | collective-permute-start | bytes 24584 | tf_op jit(solution)/shard_map/ppermute | solution.py:225
  40.8 7.1 %collective-permute-start.6 = (f32[8,32,8]{2,1,0:T(8,128)S(1)}, f32[8,32,8]{2,1,0:T(8,128)S(1)}, u32[]{:S(2)}, u32[]{:S(2)}) collective-permute-start(f32[8,32,8]{2,1,0:T(8,128)S(1)} %get-tuple-element.13), channel_id=1, source_target_pairs={{0,7},{1,0},{2,1},{3,2},{4,3},{5,4},{6,5},{7,6},{8,15},{9,8},{10,9... | collective-permute-start | bytes 24584 | tf_op jit(solution)/shard_map/ppermute | solution.py:225
  47.8 0.7 %copy-start.3 = (f32[8,32,8]{2,1,0:T(8,128)}, f32[8,32,8]{2,1,0:T(8,128)S(1)}, u32[]{:S(2)}) copy-start(f32[8,32,8]{2,1,0:T(8,128)S(1)} %collective-permute-done.7.ly_ref) | copy-start | bytes 24580
  48.5 0.6 %copy-start.4 = (f32[8,32,8]{2,1,0:T(8,128)}, f32[8,32,8]{2,1,0:T(8,128)S(1)}, u32[]{:S(2)}) copy-start(f32[8,32,8]{2,1,0:T(8,128)S(1)} %collective-permute-done.6.uy_ref) | copy-start | bytes 24580
